TPU v7x, 32 devices: a whole 2x2x4 slice. The times are simulated.
32 devices in a mesh: groups: 2 (over y), seq: 8 (over z, x), head: 2 (over core).
Axes of the slice: x: 2, y: 2, z: 4, core: 2. Of those that a mesh axis runs over, the one named last changes fastest.
Arguments:
- query_vectors: bfloat16 [2, 16384, 512], P(None, ('groups', 'seq'), 'head'), parts along dimension 1, may hold values from -8 to 8
- key_vectors: bfloat16 [2, 16384, 512], P(None, ('groups', 'seq'), 'head'), parts along dimension 1, may hold values from -8 to 8
- value_vectors: bfloat16 [2, 16384, 512], P(None, ('groups', 'seq'), 'head'), parts along dimension 1, may hold values from -12 to 12
Outputs:
- attended: bfloat16 [2, 16384, 512], P(None, ('groups', 'seq'), 'head'), parts along dimension 1
There are 2 independent parts, one for each index of `groups`. A program takes and returns all parts, laid end to end along the dimension named above; each array names one. Nothing has to cross between parts.
All inputs are finite; a program needn't handle non-finite values.
Results may differ from a plain program's by a relative error of at most 0.0039.
Values may be sent and summed in bfloat16 or wider, within the bound.
No kernel may reach another device: no remote copies, remote signals or barrier semaphores. Data moves between devices by JAX's collectives and lax.ppermute only.
A program may use at most 64 MiB of HBM per device.

v0:
```python
import math

import jax
import jax.numpy as jnp
from jax import lax
from jax.sharding import PartitionSpec as P

DH = 128
STRIDE = 1024


def shifted(block, axis, distance):
    devices = range(lax.axis_size(axis))
    route = [(i - distance, i) for i in devices if i - distance in devices]
    return lax.ppermute(block, axis, route)


def attend_columns(query_cols, key_cols, value_cols):
    score_scale = 1.0 / math.sqrt(DH)
    scores = (
        jnp.einsum("rchd,schd->chrs", query_cols, key_cols, preferred_element_type=jnp.float32)
        * score_scale
    )
    count = query_cols.shape[0]
    row_pos = jnp.arange(count, dtype=jnp.int32)[:, None]
    other_pos = jnp.arange(count, dtype=jnp.int32)[None, :]
    allowed = other_pos <= row_pos
    scores = jnp.where(allowed[None, None], scores, -jnp.inf)
    maxima = jnp.max(scores, axis=-1, keepdims=True)
    expo = jnp.exp(scores - maxima)
    weights = (expo / jnp.sum(expo, axis=-1, keepdims=True)).astype(jnp.bfloat16)
    return jnp.einsum(
        "chrs,schd->rchd", weights, value_cols, preferred_element_type=jnp.float32
    ).astype(jnp.bfloat16)


def local(query_vectors, key_vectors, value_vectors):
    local_tokens = query_vectors.shape[1]
    feature_width = query_vectors.shape[2]
    heads_here = feature_width // DH
    rows_here = local_tokens // STRIDE
    score_scale = 1.0 / math.sqrt(DH)
    prev_keys, prev_values = shifted(
        (key_vectors[0, local_tokens - STRIDE :], value_vectors[0, local_tokens - STRIDE :]),
        "seq",
        1,
    )
    ext_keys = jnp.concatenate([prev_keys, key_vectors[0]], axis=0).reshape(
        local_tokens + STRIDE, heads_here, DH
    )
    ext_values = jnp.concatenate([prev_values, value_vectors[0]], axis=0).reshape(
        local_tokens + STRIDE, heads_here, DH
    )
    queries = query_vectors[0].reshape(local_tokens, heads_here, DH)
    block_size = min(512, local_tokens)
    first_token = lax.axis_index("seq") * local_tokens

    def one_block(offset):
        query_block = lax.dynamic_slice_in_dim(queries, offset, block_size, 0)
        key_block = lax.dynamic_slice_in_dim(ext_keys, offset, STRIDE + block_size, 0)
        value_block = lax.dynamic_slice_in_dim(ext_values, offset, STRIDE + block_size, 0)
        scores = (
            jnp.einsum("qhd,khd->hqk", query_block, key_block, preferred_element_type=jnp.float32)
            * score_scale
        )
        query_pos = jnp.arange(block_size, dtype=jnp.int32)[:, None]
        key_pos = jnp.arange(STRIDE + block_size, dtype=jnp.int32)[None, :]
        allowed = (
            (key_pos > query_pos)
            & (key_pos <= STRIDE + query_pos)
            & (first_token + offset + key_pos >= STRIDE)
        )
        scores = jnp.where(allowed[None], scores, -jnp.inf)
        maxima = jnp.max(scores, axis=-1, keepdims=True)
        expo = jnp.exp(scores - maxima)
        weights = (expo / jnp.sum(expo, axis=-1, keepdims=True)).astype(jnp.bfloat16)
        return jnp.einsum(
            "hqk,khd->qhd", weights, value_block, preferred_element_type=jnp.float32
        ).astype(jnp.bfloat16)

    starts = jnp.arange(local_tokens // block_size, dtype=jnp.int32) * block_size
    row_out = lax.map(one_block, starts).reshape(local_tokens, feature_width)
    query_grid = query_vectors[1].reshape(rows_here, STRIDE, heads_here, DH)
    key_grid = key_vectors[1].reshape(rows_here, STRIDE, heads_here, DH)
    value_grid = value_vectors[1].reshape(rows_here, STRIDE, heads_here, DH)
    result = attend_columns(
        lax.all_to_all(query_grid, "seq", split_axis=1, concat_axis=0, tiled=True),
        lax.all_to_all(key_grid, "seq", split_axis=1, concat_axis=0, tiled=True),
        lax.all_to_all(value_grid, "seq", split_axis=1, concat_axis=0, tiled=True),
    )
    context = lax.all_to_all(result, "seq", split_axis=0, concat_axis=1, tiled=True)
    column_out = context.reshape(local_tokens, feature_width)
    return jnp.stack([row_out, column_out])


def solution(mesh):
    return jax.shard_map(
        local,
        mesh=mesh,
        in_specs=(
            P(None, ("groups", "seq"), "head"),
            P(None, ("groups", "seq"), "head"),
            P(None, ("groups", "seq"), "head"),
        ),
        out_specs=P(None, ("groups", "seq"), "head"),
        check_vma=False,
    )
```

profile of v0, /device:TPU:0, one launch (start us, length us, event | category | flops | bytes accessed | tf_op | source)
XLA Modules:
  0.0 122.1 jit_solution(14857121246988676300)
XLA Ops:
  0.0 1.3 %fusion.63 = (bf16[1,1024,256]{2,1,0:T(8,128)(2,1)S(1)}, bf16[1,1024,256]{2,1,0:T(8,128)(2,1)S(1)}) fusion(bf16[2,1024,256]{2,1,0:T(8,128)(2,1)} %param.5), kind=kLoop, calls=%fused_computation.57 | loop fusion | bytes 2097152 | tf_op jit(solution)/shard_map/slice | solution.py:54
  2.6 7.3 %all-to-all-start = ((bf16[1,1024,2,128]{3,2,0,1:T(2,128)(2,1)}), bf16[1,1024,2,128]{3,2,0,1:T(2,128)(2,1)S(1)}, u32[]{:S(2)}, u32[]{:S(2)}) async-start(bf16[1,1024,2,128]{3,2,0,1:T(2,128)(2,1)} %copy.71), calls=%async_computation | async-start | bytes 1048576 | tf_op jit(solution)/shard_map/all_to_all | solution.py:87
  10.9 1.1 copy.74
  12.0 12.3 %all-to-all-done = bf16[1,1024,2,128]{3,2,0,1:T(2,128)(2,1)S(1)} async-done(((bf16[1,1024,2,128]{3,2,0,1:T(2,128)(2,1)}), bf16[1,1024,2,128]{3,2,0,1:T(2,128)(2,1)S(1)}, u32[]{:S(2)}, u32[]{:S(2)}) %all-to-all-start) | async-done | bytes 524320 | tf_op jit(solution)/shard_map/all_to_all | solution.py:87
  24.3 3.6 %all-to-all-start.1 = ((bf16[1,1024,2,128]{3,2,0,1:T(2,128)(2,1)}), bf16[1,1024,2,128]{3,2,0,1:T(2,128)(2,1)S(1)}, u32[]{:S(2)}, u32[]{:S(2)}) async-start(bf16[1,1024,2,128]{3,2,0,1:T(2,128)(2,1)} %copy.74), calls=%async_computation.1 | async-start | bytes 1048576 | tf_op jit(solution)/shard_map/all_to_all | solution.py:88
  28.0 2.1 %slice_bitcast_fusion = (bf16[1024,256]{1,0:T(8,128)(2,1)}, bf16[1,1024,256]{2,1,0:T(8,128)(2,1)S(1)}, bf16[1,1024,256]{2,1,0:T(8,128)(2,1)S(1)}) fusion(bf16[2,1024,256]{2,1,0:T(8,128)(2,1)} %param.7), kind=kLoop, calls=%fused_computation.54 | loop fusion | bytes 2621440 | tf_op jit(solution)/shard_map/squeeze | solution.py:44
  30.1 4.7 %collective-permute-start = (bf16[1024,256]{1,0:T(8,128)(2,1)}, bf16[1024,256]{1,0:T(8,128)(2,1)}, u32[]{:S(2)}, u32[]{:S(2)}) collective-permute-start(bf16[1024,256]{1,0:T(8,128)(2,1)} %get-tuple-element.89), channel_id=1, source_target_pairs={{0,2},{2,4},{4,6},{6,8},{8,10},{10,12},{12,14},{1,3},{3,5},{5,7},{... | collective-permute-start | bytes 1572872 | tf_op jit(solution)/shard_map/ppermute | solution.py:15
  34.8 1.2 %copy.97 = bf16[1,1024,256]{1,2,0:T(8,128)(2,1)S(1)} copy(bf16[1,1024,256]{2,1,0:T(8,128)(2,1)} %get-tuple-element.85) | data formatting | bytes 1048576
  36.0 3.4 %collective-permute-start.1 = (bf16[1024,256]{0,1:T(8,128)(2,1)S(1)}, bf16[1024,256]{0,1:T(8,128)(2,1)}, u32[]{:S(2)}, u32[]{:S(2)}) collective-permute-start(bf16[1024,256]{0,1:T(8,128)(2,1)S(1)} %bitcast.36), channel_id=1, source_target_pairs={{0,2},{2,4},{4,6},{6,8},{8,10},{10,12},{12,14},{1,3},{3,5},{5,7},{... | collective-permute-start | bytes 1572872 | tf_op jit(solution)/shard_map/ppermute | solution.py:15
  42.0 5.5 %collective-permute-done = bf16[1024,256]{1,0:T(8,128)(2,1)} collective-permute-done((bf16[1024,256]{1,0:T(8,128)(2,1)}, bf16[1024,256]{1,0:T(8,128)(2,1)}, u32[]{:S(2)}, u32[]{:S(2)}) %collective-permute-start) | collective-permute-done | bytes 524320 | tf_op jit(solution)/shard_map/ppermute | solution.py:15
  47.5 1.2 %copy.63 = bf16[1024,256]{0,1:T(8,128)(2,1)S(1)} copy(bf16[1024,256]{1,0:T(8,128)(2,1)} %collective-permute-done) | data formatting | bytes 1048576 | tf_op jit(solution)/shard_map/ppermute | solution.py:15
  48.7 9.1 %collective-permute-done.1 = bf16[1024,256]{0,1:T(8,128)(2,1)} collective-permute-done((bf16[1024,256]{0,1:T(8,128)(2,1)S(1)}, bf16[1024,256]{0,1:T(8,128)(2,1)}, u32[]{:S(2)}, u32[]{:S(2)}) %collective-permute-start.1) | collective-permute-done | bytes 524320 | tf_op jit(solution)/shard_map/ppermute | solution.py:15
  57.8 2.1 %pad_maximum_fusion.1 = bf16[2048,2,128]{0,2,1:T(8,128)(2,1)} fusion(bf16[1024,2,128]{0,2,1:T(8,128)(2,1)S(1)} %bitcast.37, bf16[1024,2,128]{0,2,1:T(8,128)(2,1)} %bitcast.8), kind=kLoop, calls=%fused_computation.38 | loop fusion | flops 2097152 | bytes 2097152 | tf_op jit(solution)/shard_map/concatenate | solution.py:48
  59.9 10.2 %all-to-all-start.2 = ((bf16[1,1024,2,128]{3,2,0,1:T(2,128)(2,1)}), bf16[1,1024,2,128]{3,2,0,1:T(2,128)(2,1)S(1)}, u32[]{:S(2)}, u32[]{:S(2)}) async-start(bf16[1,1024,2,128]{3,2,0,1:T(2,128)(2,1)} %copy.80), calls=%async_computation.2 | async-start | bytes 1048576 | tf_op jit(solution)/shard_map/all_to_all | solution.py:89
  73.6 11.2 %all-to-all-done.2 = bf16[1,1024,2,128]{3,2,0,1:T(2,128)(2,1)S(1)} async-done(((bf16[1,1024,2,128]{3,2,0,1:T(2,128)(2,1)}), bf16[1,1024,2,128]{3,2,0,1:T(2,128)(2,1)S(1)}, u32[]{:S(2)}, u32[]{:S(2)}) %all-to-all-start.2) | async-done | bytes 524320 | tf_op jit(solution)/shard_map/all_to_all | solution.py:89
  85.3 1.2 copy.84
  86.4 3.7 %all-to-all-start.3 = ((bf16[8,128,2,128]{3,2,1,0:T(2,128)(2,1)}), bf16[8,128,2,128]{3,2,1,0:T(2,128)(2,1)S(1)}, u32[]{:S(2)}, u32[]{:S(2)}) async-start(bf16[8,128,2,128]{3,2,1,0:T(2,128)(2,1)} %copy.84), calls=%async_computation.3 | async-start | bytes 1048576 | tf_op jit(solution)/shard_map/all_to_all | solution.py:91
  90.1 28.0 %while.10 = (s32[]{:T(128)}, bf16[2,512,2,128]{1,3,2,0:T(8,128)(2,1)}, s32[2]{0:T(128)S(1)}, bf16[2048,2,128]{0,2,1:T(8,128)(2,1)S(1)}, s32[]{:T(128)}, /*index=...) while((s32[]{:T(128)}, ...), condition=%wide.region_3.4_spmd, body=%wide.region_0.3_spmd.sunk | while | flops 1225399808 | bytes 5522644 | solution.py:82
  95.3 3.6 %fusion.80 = f32[2,512]{1,0:T(2,128)S(1)} fusion(pred[512,1536]{1,0:T(8,128)(4,1)S(1)} %fusion.79, bf16[2048,2,128]{0,2,1:T(8,128)(2,1)S(1)} %get-tuple-element.165, s32[]{:T(128)S(6)} %select_n.38, bf16[1024,2,128]{0,2,1:T(8,128)(2,1)} %get-tuple-element.164, s32[]{:T(128)S(6)} %select_n.39), kind=kOutput, calls=%fused_computation.55.clone.1 | convolution fusion | flops 408946176 | bytes 1839112 | tf_op jit(solution)/shard_map/while/body/eval_jaxpr/sub | solution.py:75
  98.9 5.3 %fusion.81 = bf16[2,512,2,128]{1,3,2,0:T(8,128)(2,1)} fusion(bf16[2,512,2,128]{1,3,2,0:T(8,128)(2,1)} %get-tuple-element.149, s32[]{:T(128)S(6)} %copy.110, f32[2,512]{1,0:T(2,128)S(1)} %fusion.80, bf16[2048,2,128]{0,2,1:T(8,128)(2,1)S(1)} %get-tuple-element.162, s32[]{:T(128)S(6)} %select_n.38, pred[512,1536]{1,0:T(8,128)(4,1)S(1)} %fusion.79, ...), kind=kOutput, calls=%fused_computation.15.clone.1 | convolution fusion | flops 813304320 | bytes 2889728 | tf_op jit(solution)/shard_map/while/body/eval_jaxpr/hqk,khd->qhd/dot_general | solution.py:77
  109.3 3.6 %fusion.80 = f32[2,512]{1,0:T(2,128)S(1)} fusion(pred[512,1536]{1,0:T(8,128)(4,1)S(1)} %fusion.79, bf16[2048,2,128]{0,2,1:T(8,128)(2,1)S(1)} %get-tuple-element.165, s32[]{:T(128)S(6)} %select_n.38, bf16[1024,2,128]{0,2,1:T(8,128)(2,1)} %get-tuple-element.164, s32[]{:T(128)S(6)} %select_n.39), kind=kOutput, calls=%fused_computation.55.clone.1 | convolution fusion | flops 408946176 | bytes 1839112 | tf_op jit(solution)/shard_map/while/body/eval_jaxpr/sub | solution.py:75
  112.9 5.3 %fusion.81 = bf16[2,512,2,128]{1,3,2,0:T(8,128)(2,1)} fusion(bf16[2,512,2,128]{1,3,2,0:T(8,128)(2,1)} %get-tuple-element.149, s32[]{:T(128)S(6)} %copy.110, f32[2,512]{1,0:T(2,128)S(1)} %fusion.80, bf16[2048,2,128]{0,2,1:T(8,128)(2,1)S(1)} %get-tuple-element.162, s32[]{:T(128)S(6)} %select_n.38, pred[512,1536]{1,0:T(8,128)(4,1)S(1)} %fusion.79, ...), kind=kOutput, calls=%fused_computation.15.clone.1 | convolution fusion | flops 813304320 | bytes 2889728 | tf_op jit(solution)/shard_map/while/body/eval_jaxpr/hqk,khd->qhd/dot_general | solution.py:77
  118.2 1.6 %copy.69 = bf16[2,512,2,128]{1,0,3,2:T(2,128)(2,1)S(1)} copy(bf16[2,512,2,128]{1,3,2,0:T(8,128)(2,1)} %get-tuple-element.42) | data formatting | bytes 1048576 | tf_op jit(solution)/shard_map/while | solution.py:82
  120.8 1.3 %copy.86 = bf16[2,1024,256]{2,1,0:T(8,128)(2,1)} copy(bf16[2,1024,256]{1,2,0:T(8,128)(2,1)S(1)} %pad_maximum_fusion.2) | data formatting | bytes 2097152 | tf_op jit(solution)/shard_map/stack | solution.py:93
  (38 shorter events, 12.3 us)
Async XLA Ops:
  1.5 8.4 %copy-start = (bf16[2,1024,256]{2,1,0:T(8,128)(2,1)S(1)}, bf16[2,1024,256]{2,1,0:T(8,128)(2,1)}, u32[]{:S(2)}) copy-start(bf16[2,1024,256]{2,1,0:T(8,128)(2,1)} %param.6) | copy-start | bytes 3145732
  2.6 21.7 %all-to-all-start = ((bf16[1,1024,2,128]{3,2,0,1:T(2,128)(2,1)}), bf16[1,1024,2,128]{3,2,0,1:T(2,128)(2,1)S(1)}, u32[]{:S(2)}, u32[]{:S(2)}) async-start(bf16[1,1024,2,128]{3,2,0,1:T(2,128)(2,1)} %copy.71), calls=%async_computation | async-start | bytes 1048576 | tf_op jit(solution)/shard_map/all_to_all | solution.py:87
  24.3 35.5 %all-to-all-start.1 = ((bf16[1,1024,2,128]{3,2,0,1:T(2,128)(2,1)}), bf16[1,1024,2,128]{3,2,0,1:T(2,128)(2,1)S(1)}, u32[]{:S(2)}, u32[]{:S(2)}) async-start(bf16[1,1024,2,128]{3,2,0,1:T(2,128)(2,1)} %copy.74), calls=%async_computation.1 | async-start | bytes 1048576 | tf_op jit(solution)/shard_map/all_to_all | solution.py:88
  30.1 17.4 %collective-permute-start = (bf16[1024,256]{1,0:T(8,128)(2,1)}, bf16[1024,256]{1,0:T(8,128)(2,1)}, u32[]{:S(2)}, u32[]{:S(2)}) collective-permute-start(bf16[1024,256]{1,0:T(8,128)(2,1)} %get-tuple-element.89), channel_id=1, source_target_pairs={{0,2},{2,4},{4,6},{6,8},{8,10},{10,12},{12,14},{1,3},{3,5},{5,7},{... | collective-permute-start | bytes 1572872 | tf_op jit(solution)/shard_map/ppermute | solution.py:15
  36.0 21.7 %collective-permute-start.1 = (bf16[1024,256]{0,1:T(8,128)(2,1)S(1)}, bf16[1024,256]{0,1:T(8,128)(2,1)}, u32[]{:S(2)}, u32[]{:S(2)}) collective-permute-start(bf16[1024,256]{0,1:T(8,128)(2,1)S(1)} %bitcast.36), channel_id=1, source_target_pairs={{0,2},{2,4},{4,6},{6,8},{8,10},{10,12},{12,14},{1,3},{3,5},{5,7},{... | collective-permute-start | bytes 1572872 | tf_op jit(solution)/shard_map/ppermute | solution.py:15
  59.9 24.9 %all-to-all-start.2 = ((bf16[1,1024,2,128]{3,2,0,1:T(2,128)(2,1)}), bf16[1,1024,2,128]{3,2,0,1:T(2,128)(2,1)S(1)}, u32[]{:S(2)}, u32[]{:S(2)}) async-start(bf16[1,1024,2,128]{3,2,0,1:T(2,128)(2,1)} %copy.80), calls=%async_computation.2 | async-start | bytes 1048576 | tf_op jit(solution)/shard_map/all_to_all | solution.py:89
  85.2 4.9 %copy-start.1 = (bf16[2048,2,128]{0,2,1:T(8,128)(2,1)S(1)}, bf16[2048,2,128]{0,2,1:T(8,128)(2,1)}, u32[]{:S(2)}) copy-start(bf16[2048,2,128]{0,2,1:T(8,128)(2,1)} %pad_maximum_fusion.1) | copy-start | bytes 3145732
  85.2 4.9 %copy-start.2 = (bf16[2048,2,128]{0,2,1:T(8,128)(2,1)S(1)}, bf16[2048,2,128]{0,2,1:T(8,128)(2,1)}, u32[]{:S(2)}) copy-start(bf16[2048,2,128]{0,2,1:T(8,128)(2,1)} %pad_maximum_fusion) | copy-start | bytes 3145732
  86.4 33.7 %all-to-all-start.3 = ((bf16[8,128,2,128]{3,2,1,0:T(2,128)(2,1)}), bf16[8,128,2,128]{3,2,1,0:T(2,128)(2,1)S(1)}, u32[]{:S(2)}, u32[]{:S(2)}) async-start(bf16[8,128,2,128]{3,2,1,0:T(2,128)(2,1)} %copy.84), calls=%async_computation.3 | async-start | bytes 1048576 | tf_op jit(solution)/shard_map/all_to_all | solution.py:91
where the time goes:
time: 123 us; the launch traced here: 122 us
  waiting for transfers between devices  38 us (31%)
  starting transfers between devices  32.9 us (27%)
  local copies, waits for them, and re-layouts  18.9 us (15%)
  matrix products  18.9 us (15%)
  loops' own time  7.82 us (6%)
  other arithmetic  5.39 us (4%)
    ppermute x2, waiting for transfers between devices, shifted(): return lax.ppermute(block, axis, route)  14.5 us
    all_to_all x1, waiting for transfers between devices, local(): lax.all_to_all(query_grid, 'seq', split_axis=1, concat_axis=0, tiled=True)  12.3 us
    all_to_all x1, waiting for transfers between devices, local(): lax.all_to_all(value_grid, 'seq', split_axis=1, concat_axis=0, tiled=True)  11.2 us
    dot_general x2, matrix products, one_block(): jnp.einsum('hqk,khd->qhd', weights, value_block, preferred_element_type=j...  10.6 us
    all_to_all x1, starting transfers between devices, local(): lax.all_to_all(value_grid, 'seq', split_axis=1, concat_axis=0, tiled=True)  10.2 us
    ppermute x2, starting transfers between devices, shifted(): return lax.ppermute(block, axis, route)  8.12 us
    another operation x1, loops' own time, local(): row_out = lax.map(one_block, starts).reshape(local_tokens, feature_width)  7.82 us
    all_to_all x1, starting transfers between devices, local(): lax.all_to_all(query_grid, 'seq', split_axis=1, concat_axis=0, tiled=True)  7.25 us
  transfers between devices with their start and end apart: 6, of which 4 were waited for; matrix products, arithmetic and copies ran while one was open for 30% of the time, Pallas kernels for 0%

commit v1 on v0

v1 whole, which is shorter than its diff:
```python
import functools
import math

import jax
import jax.numpy as jnp
from jax import lax
from jax.experimental import pallas as pl
from jax.experimental.pallas import tpu as pltpu
from jax.sharding import PartitionSpec as P

DH = 128
STRIDE = 1024
QUERY_TILE = 256


def shifted(block, axis, distance):
    devices = range(lax.axis_size(axis))
    route = [(i - distance, i) for i in devices if i - distance in devices]
    return lax.ppermute(block, axis, route)


def attend_columns(query_cols, key_cols, value_cols):
    score_scale = 1.0 / math.sqrt(DH)
    scores = (
        jnp.einsum("rchd,schd->chrs", query_cols, key_cols, preferred_element_type=jnp.float32)
        * score_scale
    )
    count = query_cols.shape[0]
    row_pos = jnp.arange(count, dtype=jnp.int32)[:, None]
    other_pos = jnp.arange(count, dtype=jnp.int32)[None, :]
    allowed = other_pos <= row_pos
    scores = jnp.where(allowed[None, None], scores, -jnp.inf)
    maxima = jnp.max(scores, axis=-1, keepdims=True)
    expo = jnp.exp(scores - maxima)
    weights = (expo / jnp.sum(expo, axis=-1, keepdims=True)).astype(jnp.bfloat16)
    return jnp.einsum(
        "chrs,schd->rchd", weights, value_cols, preferred_element_type=jnp.float32
    ).astype(jnp.bfloat16)


def row_kernel(flag_ref, q_ref, kp_ref, kc_ref, vp_ref, vc_ref, o_ref):
    tile = pl.program_id(1)
    score_scale = 1.0 / math.sqrt(DH)
    dims = (((1,), (1,)), ((), ()))
    q = q_ref[...]
    prev_scores = lax.dot_general(q, kp_ref[...], dims, preferred_element_type=jnp.float32) * score_scale
    cur_scores = lax.dot_general(q, kc_ref[...], dims, preferred_element_type=jnp.float32) * score_scale
    tq = q.shape[0]
    query_pos = tile * tq + lax.broadcasted_iota(jnp.int32, (tq, STRIDE), 0)
    key_pos = lax.broadcasted_iota(jnp.int32, (tq, STRIDE), 1)
    has_prev = flag_ref[0] > 0
    prev_scores = jnp.where((key_pos > query_pos) & has_prev, prev_scores, -jnp.inf)
    cur_scores = jnp.where(key_pos <= query_pos, cur_scores, -jnp.inf)
    maxima = jnp.maximum(
        jnp.max(prev_scores, axis=1, keepdims=True), jnp.max(cur_scores, axis=1, keepdims=True)
    )
    prev_expo = jnp.exp(prev_scores - maxima)
    cur_expo = jnp.exp(cur_scores - maxima)
    total = jnp.sum(prev_expo, axis=1, keepdims=True) + jnp.sum(cur_expo, axis=1, keepdims=True)
    prev_w = (prev_expo / total).astype(jnp.bfloat16)
    cur_w = (cur_expo / total).astype(jnp.bfloat16)
    out = jnp.dot(prev_w, vp_ref[...], preferred_element_type=jnp.float32)
    out = out + jnp.dot(cur_w, vc_ref[...], preferred_element_type=jnp.float32)
    o_ref[...] = out.astype(o_ref.dtype)


def attend_rows(has_prev, queries, prev_keys, keys, prev_values, values):
    tokens, width = queries.shape
    heads = width // DH
    tiles = tokens // QUERY_TILE
    q_spec = pl.BlockSpec((QUERY_TILE, DH), lambda h, t, flag: (t, h))
    kv_spec = pl.BlockSpec((STRIDE, DH), lambda h, t, flag: (0, h))
    scores = heads * tokens * 2 * STRIDE
    return pl.pallas_call(
        row_kernel,
        out_shape=jax.ShapeDtypeStruct((tokens, width), jnp.bfloat16),
        grid_spec=pltpu.PrefetchScalarGridSpec(
            num_scalar_prefetch=1,
            grid=(heads, tiles),
            in_specs=[q_spec, kv_spec, kv_spec, kv_spec, kv_spec],
            out_specs=q_spec,
        ),
        cost_estimate=pl.CostEstimate(
            flops=4 * scores * DH, transcendentals=scores, bytes_accessed=6 * tokens * width * 2
        ),
    )(has_prev, queries, prev_keys, keys, prev_values, values)


def local(query_vectors, key_vectors, value_vectors):
    local_tokens = query_vectors.shape[1]
    feature_width = query_vectors.shape[2]
    heads_here = feature_width // DH
    rows_here = local_tokens // STRIDE
    assert rows_here == 1
    seq_index = lax.axis_index("seq")
    prev_keys, prev_values = shifted(
        (key_vectors[0, local_tokens - STRIDE :], value_vectors[0, local_tokens - STRIDE :]),
        "seq",
        1,
    )
    stacked = jnp.stack([query_vectors[1], key_vectors[1], value_vectors[1]]).reshape(
        3, rows_here, STRIDE, heads_here, DH
    )
    moved = lax.all_to_all(stacked, "seq", split_axis=2, concat_axis=1, tiled=True)
    result = attend_columns(moved[0], moved[1], moved[2])
    context = lax.all_to_all(result, "seq", split_axis=0, concat_axis=1, tiled=True)
    column_out = context.reshape(local_tokens, feature_width)
    has_prev = (seq_index > 0).astype(jnp.int32).reshape(1)
    row_out = attend_rows(
        has_prev, query_vectors[0], prev_keys, key_vectors[0], prev_values, value_vectors[0]
    )
    return jnp.stack([row_out, column_out])


def solution(mesh):
    return jax.shard_map(
        local,
        mesh=mesh,
        in_specs=(
            P(None, ("groups", "seq"), "head"),
            P(None, ("groups", "seq"), "head"),
            P(None, ("groups", "seq"), "head"),
        ),
        out_specs=P(None, ("groups", "seq"), "head"),
        check_vma=False,
    )
```

time: 123 us -> 113 us (0.919)
  the two profiles are of different devices: /device:TPU:0 before, /device:TPU:17 now
where the time goes in v1:
time: 113 us
  waiting for transfers between devices  63.2 us (56%)
  starting transfers between devices  19.4 us (17%)
  local copies, waits for them, and re-layouts  13 us (12%)
  Pallas kernels  12.6 us (11%)
  other arithmetic  3.12 us (3%)
  matrix products  1.18 us (1%)
    all_to_all x1, waiting for transfers between devices, local(): lax.all_to_all(stacked, 'seq', split_axis=2, concat_axis=1, tiled=True)  33.1 us
    ppermute x2, waiting for transfers between devices, shifted(): return lax.ppermute(block, axis, route)  30.1 us
    pallas_call x1, Pallas kernels, attend_rows(): pl.pallas_call(row_kernel, out_shape=jax.ShapeDtypeStruct((tokens, width)...  12.6 us
    all_to_all x1, starting transfers between devices, local(): lax.all_to_all(result, 'seq', split_axis=0, concat_axis=1, tiled=True)  7.68 us
    ppermute x2, starting transfers between devices, shifted(): return lax.ppermute(block, axis, route)  6.17 us
    all_to_all x1, starting transfers between devices, local(): lax.all_to_all(stacked, 'seq', split_axis=2, concat_axis=1, tiled=True)  5.58 us
    reshape x1, local copies, waits for them, and re-layouts, local(): jnp.stack([query_vectors[1], key_vectors[1], value_vectors[1]])  3 us
    unnamed x18, local copies, waits for them, and re-layouts  2.66 us
  transfers between devices with their start and end apart: 4, of which 3 were waited for; matrix products, arithmetic and copies ran while one was open for 0% of the time, Pallas kernels for 11%

profile of v1, /device:TPU:17, one launch (start us, length us, event | category | flops | bytes accessed | tf_op | source)
XLA Modules:
  0.0 112.7 jit_solution(15232062508838433394)
XLA Ops:
  0.0 2.1 %slice_bitcast_fusion.2 = (bf16[1024,256]{1,0:T(8,128)(2,1)}, bf16[1,1024,256]{2,1,0:T(8,128)(2,1)S(1)}) fusion(bf16[2,1024,256]{2,1,0:T(8,128)(2,1)} %param.3), kind=kLoop, calls=%fused_computation.13 | loop fusion | bytes 2097152 | tf_op jit(solution)/shard_map/squeeze | solution.py:110
  2.2 0.2 copy.47
  2.4 0.9 slice_bitcast_fusion.1
  3.4 1.0 copy-done.1
  4.5 0.9 slice_bitcast_fusion
  5.7 3.0 %copy.37 = bf16[3,1,1024,2,128]{4,3,0,1,2:T(2,128)(2,1)} copy(bf16[3,1,1024,2,128]{2,4,3,0,1:T(8,128)(2,1)S(1)} %bitcast.15) | data formatting | bytes 3145728 | tf_op jit(solution)/shard_map/reshape | solution.py:101
  8.7 5.6 %all-to-all-start = ((bf16[3,1,1024,2,128]{4,3,0,1,2:T(2,128)(2,1)}), bf16[3,1,1024,2,128]{4,3,0,1,2:T(2,128)(2,1)S(1)}, u32[]{:S(2)}, u32[]{:S(2)}) async-start(bf16[3,1,1024,2,128]{4,3,0,1,2:T(2,128)(2,1)} %copy.37), calls=%async_computation | async-start | bytes 3145728 | tf_op jit(solution)/shard_map/all_to_all | solution.py:104
  14.3 33.1 %all-to-all-done = bf16[3,1,1024,2,128]{4,3,0,1,2:T(2,128)(2,1)S(1)} async-done(((bf16[3,1,1024,2,128]{4,3,0,1,2:T(2,128)(2,1)}), bf16[3,1,1024,2,128]{4,3,0,1,2:T(2,128)(2,1)S(1)}, u32[]{:S(2)}, u32[]{:S(2)}) %all-to-all-start) | async-done | bytes 1572896 | tf_op jit(solution)/shard_map/all_to_all | solution.py:104
  47.4 1.1 fusion.14
  48.7 0.7 fusion.5
  49.4 0.4 copy.43
  49.8 0.8 fusion.15
  50.7 0.4 copy.45
  51.2 0.5 fusion.1
  51.7 1.2 %copy.46 = bf16[8,128,2,128]{3,2,1,0:T(2,128)(2,1)} copy(bf16[8,128,2,128]{3,0,2,1:T(8,128)(2,1)S(1)} %fusion.1) | data formatting | bytes 1048576 | tf_op jit(solution)/shard_map/convert_element_type | solution.py:38
  52.9 7.7 %all-to-all-start.1 = ((bf16[8,128,2,128]{3,2,1,0:T(2,128)(2,1)}), bf16[8,128,2,128]{3,2,1,0:T(2,128)(2,1)S(1)}, u32[]{:S(2)}, u32[]{:S(2)}) async-start(bf16[8,128,2,128]{3,2,1,0:T(2,128)(2,1)} %copy.46), calls=%async_computation.1 | async-start | bytes 1048576 | tf_op jit(solution)/shard_map/all_to_all | solution.py:106
  60.6 3.1 %collective-permute-start = (bf16[1024,256]{1,0:T(8,128)(2,1)S(1)}, bf16[1024,256]{1,0:T(8,128)(2,1)S(1)}, u32[]{:S(2)}, u32[]{:S(2)}) collective-permute-start(bf16[1024,256]{1,0:T(8,128)(2,1)S(1)} %copy-done.2), channel_id=1, source_target_pairs={{0,2},{2,4},{4,6},{6,8},{8,10},{10,12},{12,14},{1,3},{3,5},{5,7},{... | collective-permute-start | bytes 1572872 | tf_op jit(solution)/shard_map/ppermute | solution.py:19
  63.7 3.1 %collective-permute-start.1 = (bf16[1024,256]{1,0:T(8,128)(2,1)S(1)}, bf16[1024,256]{1,0:T(8,128)(2,1)S(1)}, u32[]{:S(2)}, u32[]{:S(2)}) collective-permute-start(bf16[1024,256]{1,0:T(8,128)(2,1)S(1)} %copy-done.3), channel_id=1, source_target_pairs={{0,2},{2,4},{4,6},{6,8},{8,10},{10,12},{12,14},{1,3},{3,5},{5,7},{... | collective-permute-start | bytes 1572872 | tf_op jit(solution)/shard_map/ppermute | solution.py:19
  66.8 18.8 %collective-permute-done.kp_ref = bf16[1024,256]{1,0:T(8,128)(2,1)S(1)} collective-permute-done((bf16[1024,256]{1,0:T(8,128)(2,1)S(1)}, bf16[1024,256]{1,0:T(8,128)(2,1)S(1)}, u32[]{:S(2)}, u32[]{:S(2)}) %collective-permute-start) | collective-permute-done | bytes 524320 | tf_op jit(solution)/shard_map/ppermute | solution.py:19
  85.6 11.2 %collective-permute-done.1.vp_ref = bf16[1024,256]{1,0:T(8,128)(2,1)S(1)} collective-permute-done((bf16[1024,256]{1,0:T(8,128)(2,1)S(1)}, bf16[1024,256]{1,0:T(8,128)(2,1)S(1)}, u32[]{:S(2)}, u32[]{:S(2)}) %collective-permute-start.1) | collective-permute-done | bytes 524320 | tf_op jit(solution)/shard_map/ppermute | solution.py:19
  96.8 0.8 copy-done.5
  97.6 12.6 %shard_map.37 = bf16[1024,256]{1,0:T(8,128)(2,1)} custom-call(s32[1]{0:T(128)} %bitcast.flag_ref, bf16[1024,256]{1,0:T(8,128)(2,1)} %get-tuple-element.12.q_ref, bf16[1024,256]{1,0:T(8,128)(2,1)} %copy-done.4, bf16[1024,256]{1,0:T(8,128)(2,1)} %get-tuple-element.10.kc_ref, bf16[1024,256]{1,0:T(8,128)(2,1)} %copy-done.5, ...), custom_call_target="tpu_custom_call" | custom-call | flops 2147483648 | bytes 3145728 | tf_op jit(solution)/shard_map/pallas_call | solution.py:74
  110.3 0.3 stack_reshape.3
  110.6 2.1 %pad_maximum_fusion.1 = bf16[2,1024,256]{2,1,0:T(8,128)(2,1)} fusion(bf16[1,1024,256]{2,1,0:T(8,128)(2,1)S(1)} %stack_reshape.3, bf16[1,1024,256]{2,1,0:T(8,128)(2,1)} %bitcast.19), kind=kLoop, calls=%fused_computation.6 | loop fusion | flops 524288 | bytes 2097152 | tf_op jit(solution)/shard_map/stack | solution.py:112
  (19 shorter events, 0.8 us)
Async XLA Ops:
  0.0 2.4 %copy-start = (bf16[2,1024,256]{2,1,0:T(8,128)(2,1)S(1)}, bf16[2,1024,256]{2,1,0:T(8,128)(2,1)}, u32[]{:S(2)}) copy-start(bf16[2,1024,256]{2,1,0:T(8,128)(2,1)} %param.4) | copy-start | bytes 3145732
  3.2 1.2 %copy-start.1 = (bf16[2,1024,256]{2,1,0:T(8,128)(2,1)S(1)}, bf16[2,1024,256]{2,1,0:T(8,128)(2,1)}, u32[]{:S(2)}) copy-start(bf16[2,1024,256]{2,1,0:T(8,128)(2,1)} %param.5) | copy-start | bytes 3145732
  8.7 38.7 %all-to-all-start = ((bf16[3,1,1024,2,128]{4,3,0,1,2:T(2,128)(2,1)}), bf16[3,1,1024,2,128]{4,3,0,1,2:T(2,128)(2,1)S(1)}, u32[]{:S(2)}, u32[]{:S(2)}) async-start(bf16[3,1,1024,2,128]{4,3,0,1,2:T(2,128)(2,1)} %copy.37), calls=%async_computation | async-start | bytes 3145728 | tf_op jit(solution)/shard_map/all_to_all | solution.py:104
  51.2 9.4 %copy-start.2 = (bf16[1024,256]{1,0:T(8,128)(2,1)S(1)}, bf16[1024,256]{1,0:T(8,128)(2,1)}, u32[]{:S(2)}) copy-start(bf16[1024,256]{1,0:T(8,128)(2,1)} %get-tuple-element.10.kc_ref) | copy-start | bytes 1572868
  51.2 12.5 %copy-start.3 = (bf16[1024,256]{1,0:T(8,128)(2,1)S(1)}, bf16[1024,256]{1,0:T(8,128)(2,1)}, u32[]{:S(2)}) copy-start(bf16[1024,256]{1,0:T(8,128)(2,1)} %get-tuple-element.8.vc_ref) | copy-start | bytes 1572868
  52.9 57.4 %all-to-all-start.1 = ((bf16[8,128,2,128]{3,2,1,0:T(2,128)(2,1)}), bf16[8,128,2,128]{3,2,1,0:T(2,128)(2,1)S(1)}, u32[]{:S(2)}, u32[]{:S(2)}) async-start(bf16[8,128,2,128]{3,2,1,0:T(2,128)(2,1)} %copy.46), calls=%async_computation.1 | async-start | bytes 1048576 | tf_op jit(solution)/shard_map/all_to_all | solution.py:106
  60.6 25.0 %collective-permute-start = (bf16[1024,256]{1,0:T(8,128)(2,1)S(1)}, bf16[1024,256]{1,0:T(8,128)(2,1)S(1)}, u32[]{:S(2)}, u32[]{:S(2)}) collective-permute-start(bf16[1024,256]{1,0:T(8,128)(2,1)S(1)} %copy-done.2), channel_id=1, source_target_pairs={{0,2},{2,4},{4,6},{6,8},{8,10},{10,12},{12,14},{1,3},{3,5},{5,7},{... | collective-permute-start | bytes 1572872 | tf_op jit(solution)/shard_map/ppermute | solution.py:19
  63.7 33.2 %collective-permute-start.1 = (bf16[1024,256]{1,0:T(8,128)(2,1)S(1)}, bf16[1024,256]{1,0:T(8,128)(2,1)S(1)}, u32[]{:S(2)}, u32[]{:S(2)}) collective-permute-start(bf16[1024,256]{1,0:T(8,128)(2,1)S(1)} %copy-done.3), channel_id=1, source_target_pairs={{0,2},{2,4},{4,6},{6,8},{8,10},{10,12},{12,14},{1,3},{3,5},{5,7},{... | collective-permute-start | bytes 1572872 | tf_op jit(solution)/shard_map/ppermute | solution.py:19
  85.6 11.2 %copy-start.4 = (bf16[1024,256]{1,0:T(8,128)(2,1)}, bf16[1024,256]{1,0:T(8,128)(2,1)S(1)}, u32[]{:S(2)}) copy-start(bf16[1024,256]{1,0:T(8,128)(2,1)S(1)} %collective-permute-done.kp_ref) | copy-start | bytes 1572868
  96.8 0.8 copy-start.5

commit v2 on v1

v2 whole, which is shorter than its diff:
```python
import functools
import math

import jax
import jax.numpy as jnp
from jax import lax
from jax.experimental import pallas as pl
from jax.experimental.pallas import tpu as pltpu
from jax.sharding import PartitionSpec as P

DH = 128
STRIDE = 1024
QUERY_TILE = 256


def shifted(block, axis, distance):
    devices = range(lax.axis_size(axis))
    route = [(i - distance, i) for i in devices if i - distance in devices]
    return lax.ppermute(block, axis, route)


def attend_columns(query_cols, key_cols, value_cols):
    score_scale = 1.0 / math.sqrt(DH)
    scores = (
        jnp.einsum("rchd,schd->chrs", query_cols, key_cols, preferred_element_type=jnp.float32)
        * score_scale
    )
    count = query_cols.shape[0]
    row_pos = jnp.arange(count, dtype=jnp.int32)[:, None]
    other_pos = jnp.arange(count, dtype=jnp.int32)[None, :]
    allowed = other_pos <= row_pos
    scores = jnp.where(allowed[None, None], scores, -jnp.inf)
    maxima = jnp.max(scores, axis=-1, keepdims=True)
    expo = jnp.exp(scores - maxima)
    weights = (expo / jnp.sum(expo, axis=-1, keepdims=True)).astype(jnp.bfloat16)
    return jnp.einsum(
        "chrs,schd->rchd", weights, value_cols, preferred_element_type=jnp.float32
    ).astype(jnp.bfloat16)


def row_kernel(flag_ref, q_ref, kp_ref, kc_ref, vp_ref, vc_ref, o_ref):
    score_scale = 1.0 / math.sqrt(DH)
    dims = (((1,), (1,)), ((), ()))
    has_prev = flag_ref[0] > 0
    tq = QUERY_TILE
    for tile in range(STRIDE // tq):
        low, high = tile * tq, (tile + 1) * tq
        q = q_ref[low:high, :]
        prev_scores = (
            lax.dot_general(q, kp_ref[low:, :], dims, preferred_element_type=jnp.float32)
            * score_scale
        )
        cur_scores = (
            lax.dot_general(q, kc_ref[:high, :], dims, preferred_element_type=jnp.float32)
            * score_scale
        )
        prev_shape = (tq, STRIDE - low)
        prev_ok = lax.broadcasted_iota(jnp.int32, prev_shape, 1) > lax.broadcasted_iota(
            jnp.int32, prev_shape, 0
        )
        cur_shape = (tq, high)
        cur_ok = lax.broadcasted_iota(jnp.int32, cur_shape, 1) <= lax.broadcasted_iota(
            jnp.int32, cur_shape, 0
        ) + low
        prev_scores = jnp.where(prev_ok & has_prev, prev_scores, -jnp.inf)
        cur_scores = jnp.where(cur_ok, cur_scores, -jnp.inf)
        maxima = jnp.maximum(
            jnp.max(prev_scores, axis=1, keepdims=True), jnp.max(cur_scores, axis=1, keepdims=True)
        )
        prev_expo = jnp.exp(prev_scores - maxima)
        cur_expo = jnp.exp(cur_scores - maxima)
        total = jnp.sum(prev_expo, axis=1, keepdims=True) + jnp.sum(cur_expo, axis=1, keepdims=True)
        inverse = 1.0 / total
        prev_w = (prev_expo * inverse).astype(jnp.bfloat16)
        cur_w = (cur_expo * inverse).astype(jnp.bfloat16)
        out = jnp.dot(prev_w, vp_ref[low:, :], preferred_element_type=jnp.float32)
        out = out + jnp.dot(cur_w, vc_ref[:high, :], preferred_element_type=jnp.float32)
        o_ref[low:high, :] = out.astype(o_ref.dtype)


def attend_rows(has_prev, queries, prev_keys, keys, prev_values, values):
    tokens, width = queries.shape
    heads = width // DH
    spec = pl.BlockSpec((STRIDE, DH), lambda h, flag: (0, h))
    scores = heads * tokens * (STRIDE + QUERY_TILE)
    return pl.pallas_call(
        row_kernel,
        out_shape=jax.ShapeDtypeStruct((tokens, width), jnp.bfloat16),
        grid_spec=pltpu.PrefetchScalarGridSpec(
            num_scalar_prefetch=1,
            grid=(heads,),
            in_specs=[spec] * 5,
            out_specs=spec,
        ),
        cost_estimate=pl.CostEstimate(
            flops=4 * scores * DH, transcendentals=scores, bytes_accessed=6 * tokens * width * 2
        ),
    )(has_prev, queries, prev_keys, keys, prev_values, values)


def local(query_vectors, key_vectors, value_vectors):
    local_tokens = query_vectors.shape[1]
    feature_width = query_vectors.shape[2]
    heads_here = feature_width // DH
    assert local_tokens == STRIDE
    blocks = lax.axis_size("seq")
    width = STRIDE // blocks
    seq_index = lax.axis_index("seq")
    prev_keys, prev_values = shifted((key_vectors[0], value_vectors[0]), "seq", 1)
    stacked = jnp.stack(
        [
            query_vectors[1].reshape(blocks, width, feature_width),
            key_vectors[1].reshape(blocks, width, feature_width),
            value_vectors[1].reshape(blocks, width, feature_width),
        ],
        axis=1,
    )
    moved = lax.all_to_all(stacked, "seq", split_axis=0, concat_axis=0, tiled=True)
    moved, prev_keys, prev_values = lax.optimization_barrier((moved, prev_keys, prev_values))
    grid = moved.reshape(blocks, 3, width, heads_here, DH)
    result = attend_columns(grid[:, 0], grid[:, 1], grid[:, 2])
    context = lax.all_to_all(
        result.reshape(blocks, width, feature_width), "seq", split_axis=0, concat_axis=0, tiled=True
    )
    column_out = context.reshape(local_tokens, feature_width)
    has_prev = (seq_index > 0).astype(jnp.int32).reshape(1)
    row_out = attend_rows(
        has_prev, query_vectors[0], prev_keys, key_vectors[0], prev_values, value_vectors[0]
    )
    return jnp.stack([row_out, column_out])


def solution(mesh):
    return jax.shard_map(
        local,
        mesh=mesh,
        in_specs=(
            P(None, ("groups", "seq"), "head"),
            P(None, ("groups", "seq"), "head"),
            P(None, ("groups", "seq"), "head"),
        ),
        out_specs=P(None, ("groups", "seq"), "head"),
        check_vma=False,
    )
```

time: 113 us -> 98.8 us (0.87)
  the two profiles are of different devices: /device:TPU:17 before, /device:TPU:0 now
where the time goes in v2:
time: 98.8 us; the launch traced here: 98.4 us
  starting transfers between devices  38.2 us (39%)
  waiting for transfers between devices  36.9 us (37%)
  local copies, waits for them, and re-layouts  10.9 us (11%)
  Pallas kernels  8.31 us (8%)
  other arithmetic  3.12 us (3%)
    ppermute x2, waiting for transfers between devices, shifted(): return lax.ppermute(block, axis, route)  30.6 us
    all_to_all x1, starting transfers between devices, local(): lax.all_to_all(result.reshape(blocks, width, feature_width), 'seq', split...  22.9 us
    pallas_call x1, Pallas kernels, attend_rows(): pl.pallas_call(row_kernel, out_shape=jax.ShapeDtypeStruct((tokens, width)...  8.31 us
    ppermute x2, starting transfers between devices, shifted(): return lax.ppermute(block, axis, route)  8.1 us
    all_to_all x1, starting transfers between devices, local(): lax.all_to_all(stacked, 'seq', split_axis=0, concat_axis=0, tiled=True)  7.25 us
    all_to_all x1, waiting for transfers between devices, local(): lax.all_to_all(result.reshape(blocks, width, feature_width), 'seq', split...  6.36 us
    unnamed x13, local copies, waits for them, and re-layouts  3.14 us
    squeeze x1, local copies, waits for them, and re-layouts, local(): query_vectors[0]  2.21 us
  transfers between devices with their start and end apart: 4, of which 3 were waited for; matrix products, arithmetic and copies ran while one was open for 0% of the time, Pallas kernels for 8%

profile of v2, /device:TPU:0, one launch (start us, length us, event | category | flops | bytes accessed | tf_op | source)
XLA Modules:
  0.0 98.4 jit_solution(17852957152188779452)
XLA Ops:
  0.0 2.2 %slice_bitcast_fusion.2 = (bf16[1024,256]{1,0:T(8,128)(2,1)}, bf16[1,1024,256]{2,1,0:T(8,128)(2,1)S(1)}) fusion(bf16[2,1024,256]{2,1,0:T(8,128)(2,1)} %param.3), kind=kLoop, calls=%fused_computation.13 | loop fusion | bytes 2097152 | tf_op jit(solution)/shard_map/squeeze | solution.py:128
  2.6 1.3 %copy.26 = bf16[8,3,128,256]{3,2,1,0:T(8,128)(2,1)} copy(bf16[8,3,128,256]{3,2,0,1:T(8,128)(2,1)S(1)} %pad_maximum_fusion) | data formatting | bytes 3145728 | tf_op jit(solution)/shard_map/stack | solution.py:110
  3.8 7.3 %all-to-all-start = ((bf16[8,3,128,256]{3,2,1,0:T(8,128)(2,1)}), bf16[8,3,128,256]{3,2,1,0:T(8,128)(2,1)S(1)}, u32[]{:S(2)}, u32[]{:S(2)}) async-start(bf16[8,3,128,256]{3,2,1,0:T(8,128)(2,1)} %copy.26), calls=%async_computation | async-start | bytes 3145728 | tf_op jit(solution)/shard_map/all_to_all | solution.py:118
  11.1 3.9 %collective-permute-start = (bf16[1024,256]{1,0:T(8,128)(2,1)S(1)}, bf16[1024,256]{1,0:T(8,128)(2,1)S(1)}, u32[]{:S(2)}, u32[]{:S(2)}) collective-permute-start(bf16[1024,256]{1,0:T(8,128)(2,1)S(1)} %get-tuple-element.18.kc_ref), channel_id=1, source_target_pairs={{0,2},{2,4},{4,6},{6,8},{8,10},{10,12},{12,14},{1,3},{3,5},{5,7},{... | collective-permute-start | bytes 1572872 | tf_op jit(solution)/shard_map/ppermute | solution.py:19
  15.1 4.2 %collective-permute-start.1 = (bf16[1024,256]{1,0:T(8,128)(2,1)S(1)}, bf16[1024,256]{1,0:T(8,128)(2,1)}, u32[]{:S(2)}, u32[]{:S(2)}) collective-permute-start(bf16[1024,256]{1,0:T(8,128)(2,1)S(1)} %get-tuple-element.16.vc_ref), channel_id=1, source_target_pairs={{0,2},{2,4},{4,6},{6,8},{8,10},{10,12},{12,14},{1,3},{3,5},{5,7},{... | collective-permute-start | bytes 1572872 | tf_op jit(solution)/shard_map/ppermute | solution.py:19
  19.2 18.3 %collective-permute-done.kp_ref = bf16[1024,256]{1,0:T(8,128)(2,1)S(1)} collective-permute-done((bf16[1024,256]{1,0:T(8,128)(2,1)S(1)}, bf16[1024,256]{1,0:T(8,128)(2,1)S(1)}, u32[]{:S(2)}, u32[]{:S(2)}) %collective-permute-start) | collective-permute-done | bytes 524320 | tf_op jit(solution)/shard_map/ppermute | solution.py:19
  37.5 0.8 copy-done.4
  38.3 12.2 %collective-permute-done.1.vp_ref = bf16[1024,256]{1,0:T(8,128)(2,1)} collective-permute-done((bf16[1024,256]{1,0:T(8,128)(2,1)S(1)}, bf16[1024,256]{1,0:T(8,128)(2,1)}, u32[]{:S(2)}, u32[]{:S(2)}) %collective-permute-start.1) | collective-permute-done | bytes 524320 | tf_op jit(solution)/shard_map/ppermute | solution.py:19
  50.6 0.9 copy.27
  51.5 0.9 fusion.14
  52.4 1.5 %copy.35 = bf16[8,1,128,2,128]{4,0,3,2,1:T(8,128)(2,1)S(1)} copy(bf16[8,1,128,2,128]{2,4,3,1,0:T(8,128)(2,1)} %get-tuple-element.11) | data formatting | bytes 1048576
  53.9 0.4 copy.36
  54.3 0.4 copy.37
  54.8 0.4 fusion.4
  55.2 0.4 copy.31
  55.6 0.8 fusion.15
  56.5 0.4 copy.32
  56.9 0.4 fusion.1
  57.3 1.2 %copy.33 = bf16[8,128,2,128]{1,3,2,0:T(8,128)(2,1)} copy(bf16[8,128,2,128]{3,0,2,1:T(8,128)(2,1)S(1)} %fusion.1) | data formatting | bytes 1048576 | tf_op jit(solution)/shard_map/convert_element_type | solution.py:38
  58.5 22.9 %all-to-all-start.1 = ((bf16[8,128,256]{1,2,0:T(8,128)(2,1)}), bf16[8,128,256]{1,2,0:T(8,128)(2,1)S(1)}, u32[]{:S(2)}, u32[]{:S(2)}) async-start(bf16[8,128,256]{1,2,0:T(8,128)(2,1)} %bitcast.13), calls=%async_computation.1 | async-start | bytes 1048576 | tf_op jit(solution)/shard_map/all_to_all | solution.py:122
  81.4 8.3 %shard_map.37 = bf16[1024,256]{1,0:T(8,128)(2,1)} custom-call(s32[1]{0:T(128)} %bitcast.flag_ref, bf16[1024,256]{1,0:T(8,128)(2,1)} %get-tuple-element.14.q_ref, bf16[1024,256]{1,0:T(8,128)(2,1)} %copy-done.4, bf16[1024,256]{1,0:T(8,128)(2,1)} %copy-done.2, bf16[1024,256]{1,0:T(8,128)(2,1)} %collective-permute-done.1.vp_ref, bf16[1024,256]{1,0:T(8,128)(2,1)} %copy-done.3), custom_call_target="tpu_custom_call" | custom-call | flops 1342177280 | bytes 3145728 | tf_op jit(solution)/shard_map/pallas_call | solution.py:86
  89.7 6.4 %all-to-all-done.1 = bf16[8,128,256]{1,2,0:T(8,128)(2,1)S(1)} async-done(((bf16[8,128,256]{1,2,0:T(8,128)(2,1)}), bf16[8,128,256]{1,2,0:T(8,128)(2,1)S(1)}, u32[]{:S(2)}, u32[]{:S(2)}) %all-to-all-start.1) | async-done | bytes 524320 | tf_op jit(solution)/shard_map/all_to_all | solution.py:122
  96.1 0.2 copy.34
  96.3 2.1 %pad_maximum_fusion.1 = bf16[2,1024,256]{2,1,0:T(8,128)(2,1)} fusion(bf16[1,1024,256]{2,1,0:T(8,128)(2,1)S(1)} %bitcast.27, bf16[1,1024,256]{2,1,0:T(8,128)(2,1)} %bitcast.31), kind=kLoop, calls=%fused_computation.6 | loop fusion | flops 524288 | bytes 2097152 | tf_op jit(solution)/shard_map/stack | solution.py:130
  (15 shorter events, 0.4 us)
Async XLA Ops:
  0.0 2.2 %copy-start = (bf16[2,1024,256]{2,1,0:T(8,128)(2,1)S(1)}, bf16[2,1024,256]{2,1,0:T(8,128)(2,1)}, u32[]{:S(2)}) copy-start(bf16[2,1024,256]{2,1,0:T(8,128)(2,1)} %param.4) | copy-start | bytes 3145732
  0.0 2.3 %copy-start.1 = (bf16[2,1024,256]{2,1,0:T(8,128)(2,1)S(1)}, bf16[2,1024,256]{2,1,0:T(8,128)(2,1)}, u32[]{:S(2)}) copy-start(bf16[2,1024,256]{2,1,0:T(8,128)(2,1)} %param.5) | copy-start | bytes 3145732
  2.3 8.8 %copy-start.2 = (bf16[1024,256]{1,0:T(8,128)(2,1)}, bf16[1024,256]{1,0:T(8,128)(2,1)S(1)}, u32[]{:S(2)}) copy-start(bf16[1024,256]{1,0:T(8,128)(2,1)S(1)} %get-tuple-element.18.kc_ref) | copy-start | bytes 1572868
  2.4 12.7 %copy-start.3 = (bf16[1024,256]{1,0:T(8,128)(2,1)}, bf16[1024,256]{1,0:T(8,128)(2,1)S(1)}, u32[]{:S(2)}) copy-start(bf16[1024,256]{1,0:T(8,128)(2,1)S(1)} %get-tuple-element.16.vc_ref) | copy-start | bytes 1572868
  3.8 46.7 %all-to-all-start = ((bf16[8,3,128,256]{3,2,1,0:T(8,128)(2,1)}), bf16[8,3,128,256]{3,2,1,0:T(8,128)(2,1)S(1)}, u32[]{:S(2)}, u32[]{:S(2)}) async-start(bf16[8,3,128,256]{3,2,1,0:T(8,128)(2,1)} %copy.26), calls=%async_computation | async-start | bytes 3145728 | tf_op jit(solution)/shard_map/all_to_all | solution.py:118
  11.1 26.4 %collective-permute-start = (bf16[1024,256]{1,0:T(8,128)(2,1)S(1)}, bf16[1024,256]{1,0:T(8,128)(2,1)S(1)}, u32[]{:S(2)}, u32[]{:S(2)}) collective-permute-start(bf16[1024,256]{1,0:T(8,128)(2,1)S(1)} %get-tuple-element.18.kc_ref), channel_id=1, source_target_pairs={{0,2},{2,4},{4,6},{6,8},{8,10},{10,12},{12,14},{1,3},{3,5},{5,7},{... | collective-permute-start | bytes 1572872 | tf_op jit(solution)/shard_map/ppermute | solution.py:19
  15.1 35.5 %collective-permute-start.1 = (bf16[1024,256]{1,0:T(8,128)(2,1)S(1)}, bf16[1024,256]{1,0:T(8,128)(2,1)}, u32[]{:S(2)}, u32[]{:S(2)}) collective-permute-start(bf16[1024,256]{1,0:T(8,128)(2,1)S(1)} %get-tuple-element.16.vc_ref), channel_id=1, source_target_pairs={{0,2},{2,4},{4,6},{6,8},{8,10},{10,12},{12,14},{1,3},{3,5},{5,7},{... | collective-permute-start | bytes 1572872 | tf_op jit(solution)/shard_map/ppermute | solution.py:19
  37.5 0.8 copy-start.4
  58.5 37.6 %all-to-all-start.1 = ((bf16[8,128,256]{1,2,0:T(8,128)(2,1)}), bf16[8,128,256]{1,2,0:T(8,128)(2,1)S(1)}, u32[]{:S(2)}, u32[]{:S(2)}) async-start(bf16[8,128,256]{1,2,0:T(8,128)(2,1)} %bitcast.13), calls=%async_computation.1 | async-start | bytes 1048576 | tf_op jit(solution)/shard_map/all_to_all | solution.py:122

commit v3 on v2

--- a/solution.py
+++ b/solution.py
@@ -78,24 +78,26 @@
         o_ref[low:high, :] = out.astype(o_ref.dtype)
 
 
-def attend_rows(has_prev, queries, prev_keys, keys, prev_values, values):
+def attend_rows(has_prev, queries, prev_pair, keys, values):
     tokens, width = queries.shape
     heads = width // DH
     spec = pl.BlockSpec((STRIDE, DH), lambda h, flag: (0, h))
+    prev_key_spec = pl.BlockSpec((None, STRIDE, DH), lambda h, flag: (0, 0, h))
+    prev_value_spec = pl.BlockSpec((None, STRIDE, DH), lambda h, flag: (1, 0, h))
     scores = heads * tokens * (STRIDE + QUERY_TILE)
     return pl.pallas_call(
         row_kernel,
-        out_shape=jax.ShapeDtypeStruct((tokens, width), jnp.bfloat16),
+        out_shape=jax.ShapeDtypeStruct((2, tokens, width), jnp.bfloat16),
         grid_spec=pltpu.PrefetchScalarGridSpec(
             num_scalar_prefetch=1,
             grid=(heads,),
-            in_specs=[spec] * 5,
-            out_specs=spec,
+            in_specs=[spec, prev_key_spec, spec, prev_value_spec, spec],
+            out_specs=prev_key_spec,
         ),
         cost_estimate=pl.CostEstimate(
             flops=4 * scores * DH, transcendentals=scores, bytes_accessed=6 * tokens * width * 2
         ),
-    )(has_prev, queries, prev_keys, keys, prev_values, values)
+    )(has_prev, queries, prev_pair, keys, prev_pair, values)
 
 
 def local(query_vectors, key_vectors, value_vectors):
@@ -106,7 +108,7 @@
     blocks = lax.axis_size("seq")
     width = STRIDE // blocks
     seq_index = lax.axis_index("seq")
-    prev_keys, prev_values = shifted((key_vectors[0], value_vectors[0]), "seq", 1)
+    prev_pair = shifted(jnp.stack([key_vectors[0], value_vectors[0]]), "seq", 1)
     stacked = jnp.stack(
         [
             query_vectors[1].reshape(blocks, width, feature_width),
@@ -116,7 +118,7 @@
         axis=1,
     )
     moved = lax.all_to_all(stacked, "seq", split_axis=0, concat_axis=0, tiled=True)
-    moved, prev_keys, prev_values = lax.optimization_barrier((moved, prev_keys, prev_values))
+    moved, prev_pair = lax.optimization_barrier((moved, prev_pair))
     grid = moved.reshape(blocks, 3, width, heads_here, DH)
     result = attend_columns(grid[:, 0], grid[:, 1], grid[:, 2])
     context = lax.all_to_all(
@@ -124,10 +126,8 @@
     )
     column_out = context.reshape(local_tokens, feature_width)
     has_prev = (seq_index > 0).astype(jnp.int32).reshape(1)
-    row_out = attend_rows(
-        has_prev, query_vectors[0], prev_keys, key_vectors[0], prev_values, value_vectors[0]
-    )
-    return jnp.stack([row_out, column_out])
+    both = attend_rows(has_prev, query_vectors[0], prev_pair, key_vectors[0], value_vectors[0])
+    return both.at[1].set(column_out)
 
 
 def solution(mesh):

time: 98.8 us -> 96.6 us (0.978)
  waiting for transfers between devices: 36.9 us -> 40.8 us
  starting transfers between devices: 38.2 us -> 35 us
  other arithmetic: 3.12 us -> 1.11 us
    ppermute x2 -> x1, waiting for transfers between devices: 30.6 us -> 34.5 us  [shifted(): return lax.ppermute(block, axis, route)]
    ppermute x2 -> x1, starting transfers between devices: 8.1 us -> 4.9 us  [shifted(): return lax.ppermute(block, axis, route)]
    squeeze x2 -> x0, local copies, waits for them, and re-layouts: 2.28 us -> none  [the longest x1 2.21 us: local(): query_vectors[0]]
    slice x0 -> x1, local copies, waits for them, and re-layouts: none -> 2.22 us  [local(): query_vectors[1].reshape(blocks, width, feature_width)]
    another operation x1, other arithmetic: 2.11 us -> 0.1 us  [local(): prev_pair = shifted(jnp.stack([key_vectors[0], value_vectors[0]]), 'seq', 1)]
    unnamed x13 -> x7, local copies, waits for them, and re-layouts: 3.14 us -> 1.3 us
    squeeze x1, local copies, waits for them, and re-layouts: 0.07 us -> 1.18 us  [local(): value_vectors[0]]
  transfers between devices with their start and end apart: 4 -> 3, of which waited for: 3 -> 2; matrix products, arithmetic and copies ran while one was open for 0% -> 0% of each run, Pallas kernels for 8% -> 9%
where the time goes in v3:
time: 96.6 us; the launch traced here: 96.3 us
  waiting for transfers between devices  40.8 us (42%)
  starting transfers between devices  35 us (36%)
  local copies, waits for them, and re-layouts  10.1 us (10%)
  Pallas kernels  8.3 us (9%)
  other arithmetic  1.11 us (1%)
    ppermute x1, waiting for transfers between devices, shifted(): return lax.ppermute(block, axis, route)  34.5 us
    all_to_all x1, starting transfers between devices, local(): lax.all_to_all(result.reshape(blocks, width, feature_width), 'seq', split...  22.9 us
    pallas_call x1, Pallas kernels, attend_rows(): pl.pallas_call(row_kernel, out_shape=jax.ShapeDtypeStruct((2, tokens, wid...  8.3 us
    all_to_all x1, starting transfers between devices, local(): lax.all_to_all(stacked, 'seq', split_axis=0, concat_axis=0, tiled=True)  7.25 us
    all_to_all x1, waiting for transfers between devices, local(): lax.all_to_all(result.reshape(blocks, width, feature_width), 'seq', split...  6.37 us
    ppermute x1, starting transfers between devices, shifted(): return lax.ppermute(block, axis, route)  4.9 us
    slice x1, local copies, waits for them, and re-layouts, local(): query_vectors[1].reshape(blocks, width, feature_width)  2.22 us
  transfers between devices with their start and end apart: 3, of which 2 were waited for; matrix products, arithmetic and copies ran while one was open for 0% of the time, Pallas kernels for 9%

profile of v3, /device:TPU:0, one launch (start us, length us, event | category | flops | bytes accessed | tf_op | source)
XLA Modules:
  0.0 96.3 jit_solution(16790101168655570194)
XLA Ops:
  0.0 2.2 %fusion.15 = (bf16[1,1024,256]{2,1,0:T(8,128)(2,1)S(1)}, bf16[1024,256]{1,0:T(8,128)(2,1)}) fusion(bf16[2,1024,256]{2,1,0:T(8,128)(2,1)} %param.5), kind=kLoop, calls=%fused_computation.25 | loop fusion | bytes 2097152 | tf_op jit(solution)/shard_map/slice | solution.py:114
  2.2 1.2 %slice_bitcast_fusion.1 = (bf16[1024,256]{1,0:T(8,128)(2,1)}, bf16[1,1024,256]{2,1,0:T(8,128)(2,1)S(1)}, bf16[1,1024,256]{2,1,0:T(8,128)(2,1)S(1)}, bf16[1,1024,...) fusion(bf16[2,1024,256]{2,1,0:T(8,128)(2,1)S(1)} %copy-done, ...), kind=kLoop, calls=%fused_computation.22 | loop fusion | bytes 5242880 | tf_op jit(solution)/shard_map/squeeze | solution.py:129
  3.4 0.2 pad_maximum_fusion
  3.6 1.3 %copy.26 = bf16[8,3,128,256]{3,2,1,0:T(8,128)(2,1)} copy(bf16[8,3,128,256]{3,2,0,1:T(8,128)(2,1)S(1)} %pad_maximum_fusion) | data formatting | bytes 3145728 | tf_op jit(solution)/shard_map/stack | solution.py:112
  4.8 7.3 %all-to-all-start = ((bf16[8,3,128,256]{3,2,1,0:T(8,128)(2,1)}), bf16[8,3,128,256]{3,2,1,0:T(8,128)(2,1)S(1)}, u32[]{:S(2)}, u32[]{:S(2)}) async-start(bf16[8,3,128,256]{3,2,1,0:T(8,128)(2,1)} %copy.26), calls=%async_computation | async-start | bytes 3145728 | tf_op jit(solution)/shard_map/all_to_all | solution.py:120
  12.1 0.1 pad_maximum_fusion.1
  12.2 4.9 %collective-permute-start = (bf16[2,1024,256]{2,1,0:T(8,128)(2,1)S(1)}, bf16[2,1024,256]{2,1,0:T(8,128)(2,1)}, u32[]{:S(2)}, u32[]{:S(2)}) collective-permute-start(bf16[2,1024,256]{2,1,0:T(8,128)(2,1)S(1)} %pad_maximum_fusion.1), channel_id=1, source_target_pairs={{0,2},{2,4},{4,6},{6,8},{8,10},{10,12},{12,14},{1,3},{3,5},{5,7},{... | collective-permute-start | bytes 3145736 | tf_op jit(solution)/shard_map/ppermute | solution.py:19
  17.1 34.5 %collective-permute-done.kp_ref.vp_ref = bf16[2,1024,256]{2,1,0:T(8,128)(2,1)} collective-permute-done((bf16[2,1024,256]{2,1,0:T(8,128)(2,1)S(1)}, bf16[2,1024,256]{2,1,0:T(8,128)(2,1)}, u32[]{:S(2)}, u32[]{:S(2)}) %collective-permute-start) | collective-permute-done | bytes 1048608 | tf_op jit(solution)/shard_map/ppermute | solution.py:19
  51.6 0.9 copy.27
  52.5 0.2 fusion.14
  52.7 0.4 copy.36
  53.1 0.4 copy.37
  53.5 0.4 fusion.4
  54.0 0.4 copy.31
  54.4 0.8 fusion.16
  55.2 0.4 copy.32
  55.7 0.4 copy.35
  56.1 0.4 fusion.1
  56.5 1.2 %copy.33 = bf16[8,128,2,128]{1,3,2,0:T(8,128)(2,1)} copy(bf16[8,128,2,128]{3,0,2,1:T(8,128)(2,1)S(1)} %fusion.1) | data formatting | bytes 1048576 | tf_op jit(solution)/shard_map/convert_element_type | solution.py:38
  57.8 22.9 %all-to-all-start.1 = ((bf16[8,128,256]{1,2,0:T(8,128)(2,1)}), bf16[8,128,256]{1,2,0:T(8,128)(2,1)S(1)}, u32[]{:S(2)}, u32[]{:S(2)}) async-start(bf16[8,128,256]{1,2,0:T(8,128)(2,1)} %bitcast.12), calls=%async_computation.1 | async-start | bytes 1048576 | tf_op jit(solution)/shard_map/all_to_all | solution.py:124
  80.6 8.3 %shard_map.37 = bf16[2,1024,256]{2,1,0:T(8,128)(2,1)} custom-call(s32[1]{0:T(128)} %bitcast.flag_ref, bf16[1024,256]{1,0:T(8,128)(2,1)} %get-tuple-element.31.q_ref, bf16[2,1024,256]{2,1,0:T(8,128)(2,1)} %collective-permute-done.kp_ref.vp_ref, bf16[1024,256]{1,0:T(8,128)(2,1)} %get-tuple-element.36.kc_ref, ...), custom_call_target="tpu_custom_call" | custom-call | flops 1342177280 | bytes 3145728 | tf_op jit(solution)/shard_map/pallas_call | solution.py:88
  88.9 6.4 %all-to-all-done.1 = bf16[8,128,256]{1,2,0:T(8,128)(2,1)S(1)} async-done(((bf16[8,128,256]{1,2,0:T(8,128)(2,1)}), bf16[8,128,256]{1,2,0:T(8,128)(2,1)S(1)}, u32[]{:S(2)}, u32[]{:S(2)}) %all-to-all-start.1) | async-done | bytes 524320 | tf_op jit(solution)/shard_map/all_to_all | solution.py:124
  95.3 0.2 copy.34
  95.5 0.8 bitcast_dynamic-update-slice_fusion
  (7 shorter events, 0.0 us)
Async XLA Ops:
  0.0 2.2 %copy-start.1 = (bf16[2,1024,256]{2,1,0:T(8,128)(2,1)S(1)}, bf16[2,1024,256]{2,1,0:T(8,128)(2,1)}, u32[]{:S(2)}) copy-start(bf16[2,1024,256]{2,1,0:T(8,128)(2,1)} %param.6) | copy-start | bytes 3145732
  0.0 2.2 %copy-start = (bf16[2,1024,256]{2,1,0:T(8,128)(2,1)S(1)}, bf16[2,1024,256]{2,1,0:T(8,128)(2,1)}, u32[]{:S(2)}) copy-start(bf16[2,1024,256]{2,1,0:T(8,128)(2,1)} %param.7) | copy-start | bytes 3145732
  4.8 46.7 %all-to-all-start = ((bf16[8,3,128,256]{3,2,1,0:T(8,128)(2,1)}), bf16[8,3,128,256]{3,2,1,0:T(8,128)(2,1)S(1)}, u32[]{:S(2)}, u32[]{:S(2)}) async-start(bf16[8,3,128,256]{3,2,1,0:T(8,128)(2,1)} %copy.26), calls=%async_computation | async-start | bytes 3145728 | tf_op jit(solution)/shard_map/all_to_all | solution.py:120
  12.2 39.4 %collective-permute-start = (bf16[2,1024,256]{2,1,0:T(8,128)(2,1)S(1)}, bf16[2,1024,256]{2,1,0:T(8,128)(2,1)}, u32[]{:S(2)}, u32[]{:S(2)}) collective-permute-start(bf16[2,1024,256]{2,1,0:T(8,128)(2,1)S(1)} %pad_maximum_fusion.1), channel_id=1, source_target_pairs={{0,2},{2,4},{4,6},{6,8},{8,10},{10,12},{12,14},{1,3},{3,5},{5,7},{... | collective-permute-start | bytes 3145736 | tf_op jit(solution)/shard_map/ppermute | solution.py:19
  57.8 37.5 %all-to-all-start.1 = ((bf16[8,128,256]{1,2,0:T(8,128)(2,1)}), bf16[8,128,256]{1,2,0:T(8,128)(2,1)S(1)}, u32[]{:S(2)}, u32[]{:S(2)}) async-start(bf16[8,128,256]{1,2,0:T(8,128)(2,1)} %bitcast.12), calls=%async_computation.1 | async-start | bytes 1048576 | tf_op jit(solution)/shard_map/all_to_all | solution.py:124

commit v4 on v3

--- a/solution.py
+++ b/solution.py
@@ -118,7 +118,7 @@
         axis=1,
     )
     moved = lax.all_to_all(stacked, "seq", split_axis=0, concat_axis=0, tiled=True)
-    moved, prev_pair = lax.optimization_barrier((moved, prev_pair))
+    _, prev_pair = lax.optimization_barrier((moved, prev_pair))
     grid = moved.reshape(blocks, 3, width, heads_here, DH)
     result = attend_columns(grid[:, 0], grid[:, 1], grid[:, 2])
     context = lax.all_to_all(

time: 96.6 us -> 84.7 us (0.88)
  the two profiles are of different devices: /device:TPU:0 before, /device:TPU:17 now
where the time goes in v4:
time: 84.7 us; the launch traced here: 84.4 us
  waiting for transfers between devices  46.5 us (55%)
  starting transfers between devices  16.4 us (19%)
  local copies, waits for them, and re-layouts  10.1 us (12%)
  Pallas kernels  8.31 us (10%)
  other arithmetic  2.08 us (2%)
    all_to_all x1, waiting for transfers between devices, local(): lax.all_to_all(stacked, 'seq', split_axis=0, concat_axis=0, tiled=True)  29 us
    ppermute x1, waiting for transfers between devices, shifted(): return lax.ppermute(block, axis, route)  17.5 us
    pallas_call x1, Pallas kernels, attend_rows(): pl.pallas_call(row_kernel, out_shape=jax.ShapeDtypeStruct((2, tokens, wid...  8.31 us
    all_to_all x1, starting transfers between devices, local(): lax.all_to_all(result.reshape(blocks, width, feature_width), 'seq', split...  7.72 us
    all_to_all x1, starting transfers between devices, local(): lax.all_to_all(stacked, 'seq', split_axis=0, concat_axis=0, tiled=True)  5.58 us
    ppermute x1, starting transfers between devices, shifted(): return lax.ppermute(block, axis, route)  3.08 us
    slice x1, local copies, waits for them, and re-layouts, local(): query_vectors[1].reshape(blocks, width, feature_width)  2.22 us
  transfers between devices with their start and end apart: 3, of which 2 were waited for; matrix products, arithmetic and copies ran while one was open for 8% of the time, Pallas kernels for 10%

profile of v4, /device:TPU:17, one launch (start us, length us, event | category | flops | bytes accessed | tf_op | source)
XLA Modules:
  0.0 84.4 jit_solution(11067991209354245473)
XLA Ops:
  0.0 2.2 %fusion.15 = (bf16[1,1024,256]{2,1,0:T(8,128)(2,1)S(1)}, bf16[1024,256]{1,0:T(8,128)(2,1)}) fusion(bf16[2,1024,256]{2,1,0:T(8,128)(2,1)} %param.5), kind=kLoop, calls=%fused_computation.25 | loop fusion | bytes 2097152 | tf_op jit(solution)/shard_map/slice | solution.py:114
  2.2 1.2 %slice_bitcast_fusion.1 = (bf16[1024,256]{1,0:T(8,128)(2,1)}, bf16[1,1024,256]{2,1,0:T(8,128)(2,1)S(1)}, bf16[1,1024,256]{2,1,0:T(8,128)(2,1)S(1)}, bf16[1,1024,...) fusion(bf16[2,1024,256]{2,1,0:T(8,128)(2,1)S(1)} %copy-done, ...), kind=kLoop, calls=%fused_computation.22 | loop fusion | bytes 5242880 | tf_op jit(solution)/shard_map/squeeze | solution.py:129
  3.4 0.2 pad_maximum_fusion
  3.6 1.3 %copy.26 = bf16[8,3,128,256]{3,2,1,0:T(8,128)(2,1)} copy(bf16[8,3,128,256]{3,2,0,1:T(8,128)(2,1)S(1)} %pad_maximum_fusion) | data formatting | bytes 3145728 | tf_op jit(solution)/shard_map/stack | solution.py:112
  4.8 5.6 %all-to-all-start = ((bf16[8,3,128,256]{3,2,1,0:T(8,128)(2,1)}), bf16[8,3,128,256]{3,2,1,0:T(8,128)(2,1)S(1)}, u32[]{:S(2)}, u32[]{:S(2)}) async-start(bf16[8,3,128,256]{3,2,1,0:T(8,128)(2,1)} %copy.26), calls=%async_computation | async-start | bytes 3145728 | tf_op jit(solution)/shard_map/all_to_all | solution.py:120
  10.4 1.1 %pad_maximum_fusion.1 = bf16[2,1024,256]{2,1,0:T(8,128)(2,1)} fusion(bf16[1,1024,256]{2,1,0:T(8,128)(2,1)S(1)} %get-tuple-element.23, bf16[1,1024,256]{2,1,0:T(8,128)(2,1)S(1)} %get-tuple-element.33), kind=kLoop, calls=%fused_computation.6 | loop fusion | flops 524288 | bytes 2097152 | tf_op jit(solution)/shard_map/stack | solution.py:111
  11.5 3.1 %collective-permute-start = (bf16[2,1024,256]{2,1,0:T(8,128)(2,1)}, bf16[2,1024,256]{2,1,0:T(8,128)(2,1)}, u32[]{:S(2)}, u32[]{:S(2)}) collective-permute-start(bf16[2,1024,256]{2,1,0:T(8,128)(2,1)} %pad_maximum_fusion.1), channel_id=1, source_target_pairs={{0,2},{2,4},{4,6},{6,8},{8,10},{10,12},{12,14},{1,3},{3,5},{5,7},{... | collective-permute-start | bytes 3145736 | tf_op jit(solution)/shard_map/ppermute | solution.py:19
  14.6 29.0 %all-to-all-done = bf16[8,3,128,256]{3,2,1,0:T(8,128)(2,1)S(1)} async-done(((bf16[8,3,128,256]{3,2,1,0:T(8,128)(2,1)}), bf16[8,3,128,256]{3,2,1,0:T(8,128)(2,1)S(1)}, u32[]{:S(2)}, u32[]{:S(2)}) %all-to-all-start) | async-done | bytes 1572896 | tf_op jit(solution)/shard_map/all_to_all | solution.py:120
  43.6 0.9 %copy.27 = bf16[8,3,128,256]{2,3,1,0:T(8,128)(2,1)S(1)} copy(bf16[8,3,128,256]{3,2,1,0:T(8,128)(2,1)S(1)} %all-to-all-done) | data formatting | bytes 3145728 | tf_op jit(solution)/shard_map/all_to_all | solution.py:120
  44.5 0.2 fusion.14
  44.6 0.4 copy.37
  45.1 0.4 copy.36
  45.5 0.4 fusion.4
  45.9 0.4 copy.31
  46.4 0.8 fusion.16
  47.2 0.4 copy.32
  47.6 0.4 copy.35
  48.1 0.4 fusion.1
  48.5 1.2 %copy.33 = bf16[8,128,2,128]{1,3,2,0:T(8,128)(2,1)} copy(bf16[8,128,2,128]{3,0,2,1:T(8,128)(2,1)S(1)} %fusion.1) | data formatting | bytes 1048576 | tf_op jit(solution)/shard_map/convert_element_type | solution.py:38
  49.7 7.7 %all-to-all-start.1 = ((bf16[8,128,256]{1,2,0:T(8,128)(2,1)}), bf16[8,128,256]{1,2,0:T(8,128)(2,1)S(1)}, u32[]{:S(2)}, u32[]{:S(2)}) async-start(bf16[8,128,256]{1,2,0:T(8,128)(2,1)} %bitcast.12), calls=%async_computation.1 | async-start | bytes 1048576 | tf_op jit(solution)/shard_map/all_to_all | solution.py:124
  57.5 17.5 %collective-permute-done.kp_ref.vp_ref = bf16[2,1024,256]{2,1,0:T(8,128)(2,1)} collective-permute-done((bf16[2,1024,256]{2,1,0:T(8,128)(2,1)}, bf16[2,1024,256]{2,1,0:T(8,128)(2,1)}, u32[]{:S(2)}, u32[]{:S(2)}) %collective-permute-start) | collective-permute-done | bytes 1048608 | tf_op jit(solution)/shard_map/ppermute | solution.py:19
  75.0 8.3 %shard_map.37 = bf16[2,1024,256]{2,1,0:T(8,128)(2,1)} custom-call(s32[1]{0:T(128)} %bitcast.flag_ref, bf16[1024,256]{1,0:T(8,128)(2,1)} %get-tuple-element.29.q_ref, bf16[2,1024,256]{2,1,0:T(8,128)(2,1)} %collective-permute-done.kp_ref.vp_ref, bf16[1024,256]{1,0:T(8,128)(2,1)} %get-tuple-element.34.kc_ref, ...), custom_call_target="tpu_custom_call" | custom-call | flops 1342177280 | bytes 3145728 | tf_op jit(solution)/shard_map/pallas_call | solution.py:88
  83.3 0.2 copy.34
  83.5 0.8 bitcast_dynamic-update-slice_fusion
  (7 shorter events, 0.0 us)
Async XLA Ops:
  0.0 2.2 %copy-start = (bf16[2,1024,256]{2,1,0:T(8,128)(2,1)S(1)}, bf16[2,1024,256]{2,1,0:T(8,128)(2,1)}, u32[]{:S(2)}) copy-start(bf16[2,1024,256]{2,1,0:T(8,128)(2,1)} %param.7) | copy-start | bytes 3145732
  0.0 2.2 %copy-start.1 = (bf16[2,1024,256]{2,1,0:T(8,128)(2,1)S(1)}, bf16[2,1024,256]{2,1,0:T(8,128)(2,1)}, u32[]{:S(2)}) copy-start(bf16[2,1024,256]{2,1,0:T(8,128)(2,1)} %param.6) | copy-start | bytes 3145732
  4.8 38.7 %all-to-all-start = ((bf16[8,3,128,256]{3,2,1,0:T(8,128)(2,1)}), bf16[8,3,128,256]{3,2,1,0:T(8,128)(2,1)S(1)}, u32[]{:S(2)}, u32[]{:S(2)}) async-start(bf16[8,3,128,256]{3,2,1,0:T(8,128)(2,1)} %copy.26), calls=%async_computation | async-start | bytes 3145728 | tf_op jit(solution)/shard_map/all_to_all | solution.py:120
  11.5 63.5 %collective-permute-start = (bf16[2,1024,256]{2,1,0:T(8,128)(2,1)}, bf16[2,1024,256]{2,1,0:T(8,128)(2,1)}, u32[]{:S(2)}, u32[]{:S(2)}) collective-permute-start(bf16[2,1024,256]{2,1,0:T(8,128)(2,1)} %pad_maximum_fusion.1), channel_id=1, source_target_pairs={{0,2},{2,4},{4,6},{6,8},{8,10},{10,12},{12,14},{1,3},{3,5},{5,7},{... | collective-permute-start | bytes 3145736 | tf_op jit(solution)/shard_map/ppermute | solution.py:19
  49.7 33.6 %all-to-all-start.1 = ((bf16[8,128,256]{1,2,0:T(8,128)(2,1)}), bf16[8,128,256]{1,2,0:T(8,128)(2,1)S(1)}, u32[]{:S(2)}, u32[]{:S(2)}) async-start(bf16[8,128,256]{1,2,0:T(8,128)(2,1)} %bitcast.12), calls=%async_computation.1 | async-start | bytes 1048576 | tf_op jit(solution)/shard_map/all_to_all | solution.py:124

commit v5 on v4

--- a/solution.py
+++ b/solution.py
@@ -38,44 +38,51 @@
     ).astype(jnp.bfloat16)
 
 
-def row_kernel(flag_ref, q_ref, kp_ref, kc_ref, vp_ref, vc_ref, o_ref):
+def row_tiles(with_prev, q_ref, kp_ref, kc_ref, vp_ref, vc_ref, o_ref):
     score_scale = 1.0 / math.sqrt(DH)
     dims = (((1,), (1,)), ((), ()))
-    has_prev = flag_ref[0] > 0
     tq = QUERY_TILE
+    upper = lax.broadcasted_iota(jnp.int32, (tq, tq), 1) > lax.broadcasted_iota(
+        jnp.int32, (tq, tq), 0
+    )
+
+    def scores(q, k_ref, low, high):
+        return lax.dot_general(q, k_ref[low:high, :], dims, preferred_element_type=jnp.float32) * score_scale
+
     for tile in range(STRIDE // tq):
         low, high = tile * tq, (tile + 1) * tq
         q = q_ref[low:high, :]
-        prev_scores = (
-            lax.dot_general(q, kp_ref[low:, :], dims, preferred_element_type=jnp.float32)
-            * score_scale
+        parts = []
+        if with_prev:
+            parts.append((jnp.where(upper, scores(q, kp_ref, low, high), -jnp.inf), vp_ref, low, high))
+            if high < STRIDE:
+                parts.append((scores(q, kp_ref, high, STRIDE), vp_ref, high, STRIDE))
+        if low > 0:
+            parts.append((scores(q, kc_ref, 0, low), vc_ref, 0, low))
+        parts.append((jnp.where(upper, -jnp.inf, scores(q, kc_ref, low, high)), vc_ref, low, high))
+        maxima = functools.reduce(
+            jnp.maximum, [jnp.max(p[0], axis=1, keepdims=True) for p in parts]
         )
-        cur_scores = (
-            lax.dot_general(q, kc_ref[:high, :], dims, preferred_element_type=jnp.float32)
-            * score_scale
-        )
-        prev_shape = (tq, STRIDE - low)
-        prev_ok = lax.broadcasted_iota(jnp.int32, prev_shape, 1) > lax.broadcasted_iota(
-            jnp.int32, prev_shape, 0
-        )
-        cur_shape = (tq, high)
-        cur_ok = lax.broadcasted_iota(jnp.int32, cur_shape, 1) <= lax.broadcasted_iota(
-            jnp.int32, cur_shape, 0
-        ) + low
-        prev_scores = jnp.where(prev_ok & has_prev, prev_scores, -jnp.inf)
-        cur_scores = jnp.where(cur_ok, cur_scores, -jnp.inf)
-        maxima = jnp.maximum(
-            jnp.max(prev_scores, axis=1, keepdims=True), jnp.max(cur_scores, axis=1, keepdims=True)
-        )
-        prev_expo = jnp.exp(prev_scores - maxima)
-        cur_expo = jnp.exp(cur_scores - maxima)
-        total = jnp.sum(prev_expo, axis=1, keepdims=True) + jnp.sum(cur_expo, axis=1, keepdims=True)
+        expos = [jnp.exp(p[0] - maxima) for p in parts]
+        total = functools.reduce(jnp.add, [jnp.sum(e, axis=1, keepdims=True) for e in expos])
         inverse = 1.0 / total
-        prev_w = (prev_expo * inverse).astype(jnp.bfloat16)
-        cur_w = (cur_expo * inverse).astype(jnp.bfloat16)
-        out = jnp.dot(prev_w, vp_ref[low:, :], preferred_element_type=jnp.float32)
-        out = out + jnp.dot(cur_w, vc_ref[:high, :], preferred_element_type=jnp.float32)
+        out = None
+        for e, (_, v_ref, a, b) in zip(expos, parts):
+            term = jnp.dot((e * inverse).astype(jnp.bfloat16), v_ref[a:b, :], preferred_element_type=jnp.float32)
+            out = term if out is None else out + term
         o_ref[low:high, :] = out.astype(o_ref.dtype)
+
+
+def row_kernel(flag_ref, *refs):
+    has_prev = flag_ref[0] > 0
+
+    @pl.when(has_prev)
+    def _():
+        row_tiles(True, *refs)
+
+    @pl.when(jnp.logical_not(has_prev))
+    def _():
+        row_tiles(False, *refs)
 
 
 def attend_rows(has_prev, queries, prev_pair, keys, values):

time: 84.7 us -> 84.8 us (level)
  no operation moved by 1% of the time
where the time goes in v5:
time: 84.8 us; the launch traced here: 84.5 us
  waiting for transfers between devices  46.5 us (55%)
  starting transfers between devices  16.4 us (19%)
  local copies, waits for them, and re-layouts  10.1 us (12%)
  Pallas kernels  8.42 us (10%)
  other arithmetic  2.08 us (2%)
    all_to_all x1, waiting for transfers between devices, local(): lax.all_to_all(stacked, 'seq', split_axis=0, concat_axis=0, tiled=True)  29 us
    ppermute x1, waiting for transfers between devices, shifted(): return lax.ppermute(block, axis, route)  17.5 us
    pallas_call x1, Pallas kernels, attend_rows(): pl.pallas_call(row_kernel, out_shape=jax.ShapeDtypeStruct((2, tokens, wid...  8.42 us
    all_to_all x1, starting transfers between devices, local(): lax.all_to_all(result.reshape(blocks, width, feature_width), 'seq', split...  7.72 us
    all_to_all x1, starting transfers between devices, local(): lax.all_to_all(stacked, 'seq', split_axis=0, concat_axis=0, tiled=True)  5.58 us
    ppermute x1, starting transfers between devices, shifted(): return lax.ppermute(block, axis, route)  3.08 us
    slice x1, local copies, waits for them, and re-layouts, local(): query_vectors[1].reshape(blocks, width, feature_width)  2.22 us
  transfers between devices with their start and end apart: 3, of which 2 were waited for; matrix products, arithmetic and copies ran while one was open for 8% of the time, Pallas kernels for 10%

profile of v5, /device:TPU:17, one launch (start us, length us, event | category | flops | bytes accessed | tf_op | source)
XLA Modules:
  0.0 84.5 jit_solution(13445729674963558889)
XLA Ops:
  0.0 2.2 %fusion.15 = (bf16[1,1024,256]{2,1,0:T(8,128)(2,1)S(1)}, bf16[1024,256]{1,0:T(8,128)(2,1)}) fusion(bf16[2,1024,256]{2,1,0:T(8,128)(2,1)} %param.5), kind=kLoop, calls=%fused_computation.25 | loop fusion | bytes 2097152 | tf_op jit(solution)/shard_map/slice | solution.py:121
  2.2 1.2 %slice_bitcast_fusion.1 = (bf16[1024,256]{1,0:T(8,128)(2,1)}, bf16[1,1024,256]{2,1,0:T(8,128)(2,1)S(1)}, bf16[1,1024,256]{2,1,0:T(8,128)(2,1)S(1)}, bf16[1,1024,...) fusion(bf16[2,1024,256]{2,1,0:T(8,128)(2,1)S(1)} %copy-done, ...), kind=kLoop, calls=%fused_computation.22 | loop fusion | bytes 5242880 | tf_op jit(solution)/shard_map/squeeze | solution.py:136
  3.4 0.2 pad_maximum_fusion
  3.6 1.3 %copy.26 = bf16[8,3,128,256]{3,2,1,0:T(8,128)(2,1)} copy(bf16[8,3,128,256]{3,2,0,1:T(8,128)(2,1)S(1)} %pad_maximum_fusion) | data formatting | bytes 3145728 | tf_op jit(solution)/shard_map/stack | solution.py:119
  4.8 5.6 %all-to-all-start = ((bf16[8,3,128,256]{3,2,1,0:T(8,128)(2,1)}), bf16[8,3,128,256]{3,2,1,0:T(8,128)(2,1)S(1)}, u32[]{:S(2)}, u32[]{:S(2)}) async-start(bf16[8,3,128,256]{3,2,1,0:T(8,128)(2,1)} %copy.26), calls=%async_computation | async-start | bytes 3145728 | tf_op jit(solution)/shard_map/all_to_all | solution.py:127
  10.4 1.1 %pad_maximum_fusion.1 = bf16[2,1024,256]{2,1,0:T(8,128)(2,1)} fusion(bf16[1,1024,256]{2,1,0:T(8,128)(2,1)S(1)} %get-tuple-element.23, bf16[1,1024,256]{2,1,0:T(8,128)(2,1)S(1)} %get-tuple-element.33), kind=kLoop, calls=%fused_computation.6 | loop fusion | flops 524288 | bytes 2097152 | tf_op jit(solution)/shard_map/stack | solution.py:118
  11.5 3.1 %collective-permute-start = (bf16[2,1024,256]{2,1,0:T(8,128)(2,1)}, bf16[2,1024,256]{2,1,0:T(8,128)(2,1)}, u32[]{:S(2)}, u32[]{:S(2)}) collective-permute-start(bf16[2,1024,256]{2,1,0:T(8,128)(2,1)} %pad_maximum_fusion.1), channel_id=1, source_target_pairs={{0,2},{2,4},{4,6},{6,8},{8,10},{10,12},{12,14},{1,3},{3,5},{5,7},{... | collective-permute-start | bytes 3145736 | tf_op jit(solution)/shard_map/ppermute | solution.py:19
  14.6 29.0 %all-to-all-done = bf16[8,3,128,256]{3,2,1,0:T(8,128)(2,1)S(1)} async-done(((bf16[8,3,128,256]{3,2,1,0:T(8,128)(2,1)}), bf16[8,3,128,256]{3,2,1,0:T(8,128)(2,1)S(1)}, u32[]{:S(2)}, u32[]{:S(2)}) %all-to-all-start) | async-done | bytes 1572896 | tf_op jit(solution)/shard_map/all_to_all | solution.py:127
  43.6 0.9 %copy.27 = bf16[8,3,128,256]{2,3,1,0:T(8,128)(2,1)S(1)} copy(bf16[8,3,128,256]{3,2,1,0:T(8,128)(2,1)S(1)} %all-to-all-done) | data formatting | bytes 3145728 | tf_op jit(solution)/shard_map/all_to_all | solution.py:127
  44.5 0.2 fusion.14
  44.6 0.4 copy.37
  45.1 0.4 copy.36
  45.5 0.4 fusion.4
  45.9 0.4 copy.31
  46.4 0.8 fusion.16
  47.2 0.4 copy.32
  47.6 0.4 copy.35
  48.1 0.4 fusion.1
  48.5 1.2 %copy.33 = bf16[8,128,2,128]{1,3,2,0:T(8,128)(2,1)} copy(bf16[8,128,2,128]{3,0,2,1:T(8,128)(2,1)S(1)} %fusion.1) | data formatting | bytes 1048576 | tf_op jit(solution)/shard_map/convert_element_type | solution.py:38
  49.7 7.7 %all-to-all-start.1 = ((bf16[8,128,256]{1,2,0:T(8,128)(2,1)}), bf16[8,128,256]{1,2,0:T(8,128)(2,1)S(1)}, u32[]{:S(2)}, u32[]{:S(2)}) async-start(bf16[8,128,256]{1,2,0:T(8,128)(2,1)} %bitcast.12), calls=%async_computation.1 | async-start | bytes 1048576 | tf_op jit(solution)/shard_map/all_to_all | solution.py:131
  57.5 17.5 %collective-permute-done.refs_1_.refs_3_ = bf16[2,1024,256]{2,1,0:T(8,128)(2,1)} collective-permute-done((bf16[2,1024,256]{2,1,0:T(8,128)(2,1)}, bf16[2,1024,256]{2,1,0:T(8,128)(2,1)}, u32[]{:S(2)}, u32[]{:S(2)}) %collective-permute-start) | collective-permute-done | bytes 1048608 | tf_op jit(solution)/shard_map/ppermute | solution.py:19
  75.0 8.4 %shard_map.37 = bf16[2,1024,256]{2,1,0:T(8,128)(2,1)} custom-call(s32[1]{0:T(128)} %bitcast.flag_ref, bf16[1024,256]{1,0:T(8,128)(2,1)} %get-tuple-element.29.refs_0_, bf16[2,1024,256]{2,1,0:T(8,128)(2,1)} %collective-permute-done.refs_1_.refs_3_, bf16[1024,256]{1,0:T(8,128)(2,1)} %get-tuple-element.34.refs_2_, ...), custom_call_target="tpu_custom_call" | custom-call | flops 1342177280 | bytes 3145728 | tf_op jit(solution)/shard_map/pallas_call | solution.py:95
  83.4 0.2 copy.34
  83.6 0.8 bitcast_dynamic-update-slice_fusion
  (7 shorter events, 0.0 us)
Async XLA Ops:
  0.0 2.2 %copy-start = (bf16[2,1024,256]{2,1,0:T(8,128)(2,1)S(1)}, bf16[2,1024,256]{2,1,0:T(8,128)(2,1)}, u32[]{:S(2)}) copy-start(bf16[2,1024,256]{2,1,0:T(8,128)(2,1)} %param.7) | copy-start | bytes 3145732
  0.0 2.2 %copy-start.1 = (bf16[2,1024,256]{2,1,0:T(8,128)(2,1)S(1)}, bf16[2,1024,256]{2,1,0:T(8,128)(2,1)}, u32[]{:S(2)}) copy-start(bf16[2,1024,256]{2,1,0:T(8,128)(2,1)} %param.6) | copy-start | bytes 3145732
  4.8 38.7 %all-to-all-start = ((bf16[8,3,128,256]{3,2,1,0:T(8,128)(2,1)}), bf16[8,3,128,256]{3,2,1,0:T(8,128)(2,1)S(1)}, u32[]{:S(2)}, u32[]{:S(2)}) async-start(bf16[8,3,128,256]{3,2,1,0:T(8,128)(2,1)} %copy.26), calls=%async_computation | async-start | bytes 3145728 | tf_op jit(solution)/shard_map/all_to_all | solution.py:127
  11.5 63.5 %collective-permute-start = (bf16[2,1024,256]{2,1,0:T(8,128)(2,1)}, bf16[2,1024,256]{2,1,0:T(8,128)(2,1)}, u32[]{:S(2)}, u32[]{:S(2)}) collective-permute-start(bf16[2,1024,256]{2,1,0:T(8,128)(2,1)} %pad_maximum_fusion.1), channel_id=1, source_target_pairs={{0,2},{2,4},{4,6},{6,8},{8,10},{10,12},{12,14},{1,3},{3,5},{5,7},{... | collective-permute-start | bytes 3145736 | tf_op jit(solution)/shard_map/ppermute | solution.py:19
  49.7 33.7 %all-to-all-start.1 = ((bf16[8,128,256]{1,2,0:T(8,128)(2,1)}), bf16[8,128,256]{1,2,0:T(8,128)(2,1)S(1)}, u32[]{:S(2)}, u32[]{:S(2)}) async-start(bf16[8,128,256]{1,2,0:T(8,128)(2,1)} %bitcast.12), calls=%async_computation.1 | async-start | bytes 1048576 | tf_op jit(solution)/shard_map/all_to_all | solution.py:131

commit v6 on v5

--- a/solution.py
+++ b/solution.py
@@ -107,6 +107,34 @@
     )(has_prev, queries, prev_pair, keys, prev_pair, values)
 
 
+def pack_kernel(q_ref, k_ref, v_ref, kp_ref, vp_ref, o_ref, pair_ref):
+    o_ref[0] = q_ref[...]
+    o_ref[1] = k_ref[...]
+    o_ref[2] = v_ref[...]
+    pair_ref[0] = kp_ref[...]
+    pair_ref[1] = vp_ref[...]
+
+
+def pack(query_vectors, key_vectors, value_vectors, blocks):
+    _, tokens, width = query_vectors.shape
+    size = tokens // blocks
+    column = pl.BlockSpec((None, size, width), lambda b: (1, b, 0))
+    row = pl.BlockSpec((None, size, width), lambda b: (0, b, 0))
+    return pl.pallas_call(
+        pack_kernel,
+        out_shape=(
+            jax.ShapeDtypeStruct((blocks, 3, size, width), query_vectors.dtype),
+            jax.ShapeDtypeStruct((2, tokens, width), query_vectors.dtype),
+        ),
+        grid=(blocks,),
+        in_specs=[column, column, column, row, row],
+        out_specs=(
+            pl.BlockSpec((None, 3, size, width), lambda b: (b, 0, 0, 0)),
+            pl.BlockSpec((2, size, width), lambda b: (0, b, 0)),
+        ),
+    )(query_vectors, key_vectors, value_vectors, key_vectors, value_vectors)
+
+
 def local(query_vectors, key_vectors, value_vectors):
     local_tokens = query_vectors.shape[1]
     feature_width = query_vectors.shape[2]
@@ -115,15 +143,19 @@
     blocks = lax.axis_size("seq")
     width = STRIDE // blocks
     seq_index = lax.axis_index("seq")
-    prev_pair = shifted(jnp.stack([key_vectors[0], value_vectors[0]]), "seq", 1)
-    stacked = jnp.stack(
-        [
-            query_vectors[1].reshape(blocks, width, feature_width),
-            key_vectors[1].reshape(blocks, width, feature_width),
-            value_vectors[1].reshape(blocks, width, feature_width),
-        ],
-        axis=1,
-    )
+    if width % 16 == 0:
+        stacked, pair = pack(query_vectors, key_vectors, value_vectors, blocks)
+    else:
+        pair = jnp.stack([key_vectors[0], value_vectors[0]])
+        stacked = jnp.stack(
+            [
+                query_vectors[1].reshape(blocks, width, feature_width),
+                key_vectors[1].reshape(blocks, width, feature_width),
+                value_vectors[1].reshape(blocks, width, feature_width),
+            ],
+            axis=1,
+        )
+    prev_pair = shifted(pair, "seq", 1)
     moved = lax.all_to_all(stacked, "seq", split_axis=0, concat_axis=0, tiled=True)
     _, prev_pair = lax.optimization_barrier((moved, prev_pair))
     grid = moved.reshape(blocks, 3, width, heads_here, DH)

time: 84.8 us -> 87.4 us (1.031)
  Pallas kernels: 8.42 us -> 14.3 us
  waiting for transfers between devices: 46.5 us -> 44.3 us
  local copies, waits for them, and re-layouts: 10.1 us -> 8.8 us
  other arithmetic: 2.08 us -> 0.84 us
  matrix products: 0.82 us -> 1.98 us
    pallas_call x0 -> x1, Pallas kernels: none -> 5.85 us  [pack(): pl.pallas_call(pack_kernel, out_shape=(jax.ShapeDtypeStruct((blocks, 3, s...]
    ppermute x1, waiting for transfers between devices: 17.5 us -> 14.3 us  [shifted(): return lax.ppermute(block, axis, route)]
    slice x1 -> x0, local copies, waits for them, and re-layouts: 2.22 us -> none  [local(): query_vectors[1].reshape(blocks, width, feature_width)]
    unnamed x7 -> x6, local copies, waits for them, and re-layouts: 1.3 us -> 0.01 us
    another operation x1 -> x0, local copies, waits for them, and re-layouts: 1.26 us -> none  [local(): jnp.stack([query_vectors[1].reshape(blocks, width, feature_width), key_ve...]
    another operation x2 -> x0, other arithmetic: 1.23 us -> none  [the longest x1 1.06 us: local(): prev_pair = shifted(jnp.stack([key_vectors[0], value_vectors[0]]), 'seq', 1)]
    convert_element_type x1, local copies, waits for them, and re-layouts: 1.22 us -> 2.38 us  [attend_columns(): return jnp.einsum('chrs,schd->rchd', weights, value_cols, preferred_eleme...]
    all_to_all x1, waiting for transfers between devices: 29 us -> 30 us  [local(): lax.all_to_all(stacked, 'seq', split_axis=0, concat_axis=0, tiled=True)]
  transfers between devices with their start and end apart: 3 -> 3, of which waited for: 2 -> 2; matrix products, arithmetic and copies ran while one was open for 8% -> 11% of each run, Pallas kernels for 10% -> 10%
where the time goes in v6:
time: 87.4 us; the launch traced here: 86.6 us
  waiting for transfers between devices  44.3 us (51%)
  starting transfers between devices  16.4 us (19%)
  Pallas kernels  14.3 us (16%)
  local copies, waits for them, and re-layouts  8.8 us (10%)
  matrix products  1.98 us (2%)
    all_to_all x1, waiting for transfers between devices, local(): lax.all_to_all(stacked, 'seq', split_axis=0, concat_axis=0, tiled=True)  30 us
    ppermute x1, waiting for transfers between devices, shifted(): return lax.ppermute(block, axis, route)  14.3 us
    pallas_call x1, Pallas kernels, attend_rows(): pl.pallas_call(row_kernel, out_shape=jax.ShapeDtypeStruct((2, tokens, wid...  8.42 us
    all_to_all x1, starting transfers between devices, local(): lax.all_to_all(result.reshape(blocks, width, feature_width), 'seq', split...  7.72 us
    pallas_call x1, Pallas kernels, pack(): pl.pallas_call(pack_kernel, out_shape=(jax.ShapeDtypeStruct((blocks, 3, s...  5.85 us
    all_to_all x1, starting transfers between devices, local(): lax.all_to_all(stacked, 'seq', split_axis=0, concat_axis=0, tiled=True)  5.58 us
    ppermute x1, starting transfers between devices, shifted(): return lax.ppermute(block, axis, route)  3.08 us
    convert_element_type x1, local copies, waits for them, and re-layouts, attend_columns(): return jnp.einsum('chrs,schd->rchd', weights, value_cols, preferred_eleme...  2.38 us
  transfers between devices with their start and end apart: 3, of which 2 were waited for; matrix products, arithmetic and copies ran while one was open for 11% of the time, Pallas kernels for 10%

profile of v6, /device:TPU:17, one launch (start us, length us, event | category | flops | bytes accessed | tf_op | source)
XLA Modules:
  0.0 86.6 jit_solution(5107121937155014896)
XLA Ops:
  0.0 5.8 %shard_map.37 = (bf16[8,3,128,256]{3,2,1,0:T(8,128)(2,1)}, bf16[2,1024,256]{2,1,0:T(8,128)(2,1)}) custom-call(bf16[2,1024,256]{2,1,0:T(8,128)(2,1)} %q_ref.1, bf16[2,1024,256]{2,1,0:T(8,128)(2,1)} %kp_ref.1, bf16[2,1024,256]{2,1,0:T(8,128)(2,1)} %vp_ref.1, bf16[2,1024,256]{2,1,0:T(8,128)(2,1)} %kp_ref.1, bf16[2,1024,256]{2,1,0:T(8,128)(2,1)} %vp_ref.1), custom_call_target="tpu_custom_call" | custom-call | tf_op jit(solution)/shard_map/pallas_call | solution.py:123
  5.8 5.6 %all-to-all-start = ((bf16[8,3,128,256]{3,2,1,0:T(8,128)(2,1)}), bf16[8,3,128,256]{3,2,1,0:T(8,128)(2,1)S(1)}, u32[]{:S(2)}, u32[]{:S(2)}) async-start(bf16[8,3,128,256]{3,2,1,0:T(8,128)(2,1)} %get-tuple-element.20), calls=%async_computation | async-start | bytes 3145728 | tf_op jit(solution)/shard_map/all_to_all | solution.py:159
  11.4 3.1 %collective-permute-start = (bf16[2,1024,256]{2,1,0:T(8,128)(2,1)}, bf16[2,1024,256]{2,1,0:T(8,128)(2,1)}, u32[]{:S(2)}, u32[]{:S(2)}) collective-permute-start(bf16[2,1024,256]{2,1,0:T(8,128)(2,1)} %get-tuple-element.21), channel_id=1, source_target_pairs={{0,2},{2,4},{4,6},{6,8},{8,10},{10,12},{12,14},{1,3},{3,5},{5,7},{... | collective-permute-start | bytes 3145736 | tf_op jit(solution)/shard_map/ppermute | solution.py:19
  14.5 30.0 %all-to-all-done = bf16[8,3,128,256]{3,2,1,0:T(8,128)(2,1)S(1)} async-done(((bf16[8,3,128,256]{3,2,1,0:T(8,128)(2,1)}), bf16[8,3,128,256]{3,2,1,0:T(8,128)(2,1)S(1)}, u32[]{:S(2)}, u32[]{:S(2)}) %all-to-all-start) | async-done | bytes 1572896 | tf_op jit(solution)/shard_map/all_to_all | solution.py:159
  44.6 0.4 reshape.60
  45.0 1.2 %fusion.11 = (bf16[8,1,128,2,128]{4,3,2,1,0:T(2,128)(2,1)S(1)}, bf16[8,1,128,2,128]{4,3,2,1,0:T(2,128)(2,1)S(1)}, bf16[8,1,128,2,128]{4,3,2,1,0:T(2,128)(2,1)S(1)}) fusion(bf16[8,3,128,2,128]{4,3,2,1,0:T(2,128)(2,1)S(1)} %reshape.60), kind=kLoop, calls=%fused_computation.22 | loop fusion | bytes 3145728 | tf_op jit(solution)/shard_map/slice | solution.py:162
  46.2 0.7 fusion.4
  46.9 0.4 copy.17
  47.3 0.8 fusion.12
  48.1 0.4 copy.18
  48.6 0.0 copy-start.2
  48.6 1.3 %fusion.1 = bf16[8,128,2,128]{3,0,2,1:T(8,128)(2,1)} fusion(bf16[128,2,8,8]{3,2,1,0:T(8,128)(2,1)S(1)} %copy.18, bf16[8,1,128,2,128]{4,3,2,1,0:T(2,128)(2,1)S(1)} %get-tuple-element.23), kind=kOutput, calls=%fused_computation.2 | convolution fusion | flops 4456448 | bytes 1081344 | tf_op jit(solution)/shard_map/chrs,schd->rchd/dot_general | solution.py:36
  49.9 2.4 %copy.19 = bf16[8,128,2,128]{1,3,2,0:T(8,128)(2,1)} copy(bf16[8,128,2,128]{3,0,2,1:T(8,128)(2,1)} %fusion.1) | data formatting | bytes 1048576 | tf_op jit(solution)/shard_map/convert_element_type | solution.py:38
  52.3 7.7 %all-to-all-start.1 = ((bf16[8,128,256]{1,2,0:T(8,128)(2,1)}), bf16[8,128,256]{1,2,0:T(8,128)(2,1)}, u32[]{:S(2)}, u32[]{:S(2)}) async-start(bf16[8,128,256]{1,2,0:T(8,128)(2,1)} %bitcast.25), calls=%async_computation.1 | async-start | bytes 1048576 | tf_op jit(solution)/shard_map/all_to_all | solution.py:163
  60.0 0.0 copy-done.2
  60.0 0.8 slice_bitcast_fusion.2.refs_0_
  60.8 0.0 copy-done
  60.8 0.0 copy-done.1
  60.8 1.1 %slice_bitcast_fusion = (bf16[1024,256]{1,0:T(8,128)(2,1)}, bf16[1024,256]{1,0:T(8,128)(2,1)}) fusion(bf16[2,1024,256]{2,1,0:T(8,128)(2,1)S(1)} %copy-done.1, bf16[2,1024,256]{2,1,0:T(8,128)(2,1)S(1)} %copy-done), kind=kLoop, calls=%fused_computation.10 | loop fusion | bytes 2097152 | tf_op jit(solution)/shard_map/squeeze | solution.py:168
  61.9 14.3 %collective-permute-done.refs_1_.refs_3_ = bf16[2,1024,256]{2,1,0:T(8,128)(2,1)} collective-permute-done((bf16[2,1024,256]{2,1,0:T(8,128)(2,1)}, bf16[2,1024,256]{2,1,0:T(8,128)(2,1)}, u32[]{:S(2)}, u32[]{:S(2)}) %collective-permute-start) | collective-permute-done | bytes 1048608 | tf_op jit(solution)/shard_map/ppermute | solution.py:19
  76.1 8.4 %shard_map.38 = bf16[2,1024,256]{2,1,0:T(8,128)(2,1)} custom-call(s32[1]{0:T(128)} %bitcast.flag_ref, bf16[1024,256]{1,0:T(8,128)(2,1)} %slice_bitcast_fusion.2.refs_0_, bf16[2,1024,256]{2,1,0:T(8,128)(2,1)} %collective-permute-done.refs_1_.refs_3_, bf16[1024,256]{1,0:T(8,128)(2,1)} %get-tuple-element.29.refs_2_, ...), custom_call_target="tpu_custom_call" | custom-call | flops 1342177280 | bytes 3145728 | tf_op jit(solution)/shard_map/pallas_call | solution.py:95
  84.6 0.0 all-to-all-done.1
  84.6 1.2 %copy.20 = bf16[8,128,256]{2,1,0:T(8,128)(2,1)S(1)} copy(bf16[8,128,256]{1,2,0:T(8,128)(2,1)} %all-to-all-done.1) | data formatting | bytes 1048576 | tf_op jit(solution)/shard_map/all_to_all | solution.py:163
  85.8 0.8 bitcast_dynamic-update-slice_fusion
  (4 shorter events, 0.0 us)
Async XLA Ops:
  5.8 38.7 %all-to-all-start = ((bf16[8,3,128,256]{3,2,1,0:T(8,128)(2,1)}), bf16[8,3,128,256]{3,2,1,0:T(8,128)(2,1)S(1)}, u32[]{:S(2)}, u32[]{:S(2)}) async-start(bf16[8,3,128,256]{3,2,1,0:T(8,128)(2,1)} %get-tuple-element.20), calls=%async_computation | async-start | bytes 3145728 | tf_op jit(solution)/shard_map/all_to_all | solution.py:159
  11.4 64.7 %collective-permute-start = (bf16[2,1024,256]{2,1,0:T(8,128)(2,1)}, bf16[2,1024,256]{2,1,0:T(8,128)(2,1)}, u32[]{:S(2)}, u32[]{:S(2)}) collective-permute-start(bf16[2,1024,256]{2,1,0:T(8,128)(2,1)} %get-tuple-element.21), channel_id=1, source_target_pairs={{0,2},{2,4},{4,6},{6,8},{8,10},{10,12},{12,14},{1,3},{3,5},{5,7},{... | collective-permute-start | bytes 3145736 | tf_op jit(solution)/shard_map/ppermute | solution.py:19
  48.6 11.4 %copy-start.2 = (bf16[2,1024,256]{2,1,0:T(8,128)(2,1)S(1)}, bf16[2,1024,256]{2,1,0:T(8,128)(2,1)}, u32[]{:S(2)}) copy-start(bf16[2,1024,256]{2,1,0:T(8,128)(2,1)} %q_ref.1) | copy-start | bytes 3145732
  49.9 10.9 %copy-start = (bf16[2,1024,256]{2,1,0:T(8,128)(2,1)S(1)}, bf16[2,1024,256]{2,1,0:T(8,128)(2,1)}, u32[]{:S(2)}) copy-start(bf16[2,1024,256]{2,1,0:T(8,128)(2,1)} %kp_ref.1) | copy-start | bytes 3145732
  49.9 10.9 %copy-start.1 = (bf16[2,1024,256]{2,1,0:T(8,128)(2,1)S(1)}, bf16[2,1024,256]{2,1,0:T(8,128)(2,1)}, u32[]{:S(2)}) copy-start(bf16[2,1024,256]{2,1,0:T(8,128)(2,1)} %vp_ref.1) | copy-start | bytes 3145732
  52.3 32.3 %all-to-all-start.1 = ((bf16[8,128,256]{1,2,0:T(8,128)(2,1)}), bf16[8,128,256]{1,2,0:T(8,128)(2,1)}, u32[]{:S(2)}, u32[]{:S(2)}) async-start(bf16[8,128,256]{1,2,0:T(8,128)(2,1)} %bitcast.25), calls=%async_computation.1 | async-start | bytes 1048576 | tf_op jit(solution)/shard_map/all_to_all | solution.py:163

commit v7 on v6

--- a/solution.py
+++ b/solution.py
@@ -108,29 +108,31 @@
 
 
 def pack_kernel(q_ref, k_ref, v_ref, kp_ref, vp_ref, o_ref, pair_ref):
-    o_ref[0] = q_ref[...]
-    o_ref[1] = k_ref[...]
-    o_ref[2] = v_ref[...]
+    shape = (o_ref.shape[0], o_ref.shape[2], o_ref.shape[3])
+    o_ref[:, 0] = q_ref[...].reshape(shape)
+    o_ref[:, 1] = k_ref[...].reshape(shape)
+    o_ref[:, 2] = v_ref[...].reshape(shape)
     pair_ref[0] = kp_ref[...]
     pair_ref[1] = vp_ref[...]
 
 
-def pack(query_vectors, key_vectors, value_vectors, blocks):
+def pack(query_vectors, key_vectors, value_vectors, blocks, steps=2):
     _, tokens, width = query_vectors.shape
     size = tokens // blocks
-    column = pl.BlockSpec((None, size, width), lambda b: (1, b, 0))
-    row = pl.BlockSpec((None, size, width), lambda b: (0, b, 0))
+    rows = tokens // steps
+    column = pl.BlockSpec((None, rows, width), lambda b: (1, b, 0))
+    row = pl.BlockSpec((None, rows, width), lambda b: (0, b, 0))
     return pl.pallas_call(
         pack_kernel,
         out_shape=(
             jax.ShapeDtypeStruct((blocks, 3, size, width), query_vectors.dtype),
             jax.ShapeDtypeStruct((2, tokens, width), query_vectors.dtype),
         ),
-        grid=(blocks,),
+        grid=(steps,),
         in_specs=[column, column, column, row, row],
         out_specs=(
-            pl.BlockSpec((None, 3, size, width), lambda b: (b, 0, 0, 0)),
-            pl.BlockSpec((2, size, width), lambda b: (0, b, 0)),
+            pl.BlockSpec((blocks // steps, 3, size, width), lambda b: (b, 0, 0, 0)),
+            pl.BlockSpec((2, rows, width), lambda b: (0, b, 0)),
         ),
     )(query_vectors, key_vectors, value_vectors, key_vectors, value_vectors)
 

time: 87.4 us -> 84 us (0.961)
  Pallas kernels: 14.3 us -> 11.3 us
    pallas_call x1, Pallas kernels: 5.85 us -> 2.85 us  [pack(): pl.pallas_call(pack_kernel, out_shape=(jax.ShapeDtypeStruct((blocks, 3, s...]
where the time goes in v7:
time: 84 us; the launch traced here: 83.6 us
  waiting for transfers between devices  44.3 us (53%)
  starting transfers between devices  16.4 us (20%)
  Pallas kernels  11.3 us (13%)
  local copies, waits for them, and re-layouts  8.8 us (10%)
  matrix products  1.98 us (2%)
  other arithmetic  0.84 us (1%)
    all_to_all x1, waiting for transfers between devices, local(): lax.all_to_all(stacked, 'seq', split_axis=0, concat_axis=0, tiled=True)  30 us
    ppermute x1, waiting for transfers between devices, shifted(): return lax.ppermute(block, axis, route)  14.3 us
    pallas_call x1, Pallas kernels, attend_rows(): pl.pallas_call(row_kernel, out_shape=jax.ShapeDtypeStruct((2, tokens, wid...  8.42 us
    all_to_all x1, starting transfers between devices, local(): lax.all_to_all(result.reshape(blocks, width, feature_width), 'seq', split...  7.72 us
    all_to_all x1, starting transfers between devices, local(): lax.all_to_all(stacked, 'seq', split_axis=0, concat_axis=0, tiled=True)  5.58 us
    ppermute x1, starting transfers between devices, shifted(): return lax.ppermute(block, axis, route)  3.08 us
    pallas_call x1, Pallas kernels, pack(): pl.pallas_call(pack_kernel, out_shape=(jax.ShapeDtypeStruct((blocks, 3, s...  2.85 us
    convert_element_type x1, local copies, waits for them, and re-layouts, attend_columns(): return jnp.einsum('chrs,schd->rchd', weights, value_cols, preferred_eleme...  2.38 us
  transfers between devices with their start and end apart: 3, of which 2 were waited for; matrix products, arithmetic and copies ran while one was open for 11% of the time, Pallas kernels for 10%

profile of v7, /device:TPU:17, one launch (start us, length us, event | category | flops | bytes accessed | tf_op | source)
XLA Modules:
  0.0 83.6 jit_solution(12497630194478633105)
XLA Ops:
  0.0 2.8 %shard_map.37 = (bf16[8,3,128,256]{3,2,1,0:T(8,128)(2,1)}, bf16[2,1024,256]{2,1,0:T(8,128)(2,1)}) custom-call(bf16[2,1024,256]{2,1,0:T(8,128)(2,1)} %q_ref.1, bf16[2,1024,256]{2,1,0:T(8,128)(2,1)} %kp_ref.1, bf16[2,1024,256]{2,1,0:T(8,128)(2,1)} %vp_ref.1, bf16[2,1024,256]{2,1,0:T(8,128)(2,1)} %kp_ref.1, bf16[2,1024,256]{2,1,0:T(8,128)(2,1)} %vp_ref.1), custom_call_target="tpu_custom_call" | custom-call | tf_op jit(solution)/shard_map/pallas_call | solution.py:125
  2.8 5.6 %all-to-all-start = ((bf16[8,3,128,256]{3,2,1,0:T(8,128)(2,1)}), bf16[8,3,128,256]{3,2,1,0:T(8,128)(2,1)S(1)}, u32[]{:S(2)}, u32[]{:S(2)}) async-start(bf16[8,3,128,256]{3,2,1,0:T(8,128)(2,1)} %get-tuple-element.20), calls=%async_computation | async-start | bytes 3145728 | tf_op jit(solution)/shard_map/all_to_all | solution.py:161
  8.4 3.1 %collective-permute-start = (bf16[2,1024,256]{2,1,0:T(8,128)(2,1)}, bf16[2,1024,256]{2,1,0:T(8,128)(2,1)}, u32[]{:S(2)}, u32[]{:S(2)}) collective-permute-start(bf16[2,1024,256]{2,1,0:T(8,128)(2,1)} %get-tuple-element.21), channel_id=1, source_target_pairs={{0,2},{2,4},{4,6},{6,8},{8,10},{10,12},{12,14},{1,3},{3,5},{5,7},{... | collective-permute-start | bytes 3145736 | tf_op jit(solution)/shard_map/ppermute | solution.py:19
  11.5 30.0 %all-to-all-done = bf16[8,3,128,256]{3,2,1,0:T(8,128)(2,1)S(1)} async-done(((bf16[8,3,128,256]{3,2,1,0:T(8,128)(2,1)}), bf16[8,3,128,256]{3,2,1,0:T(8,128)(2,1)S(1)}, u32[]{:S(2)}, u32[]{:S(2)}) %all-to-all-start) | async-done | bytes 1572896 | tf_op jit(solution)/shard_map/all_to_all | solution.py:161
  41.6 0.4 reshape.60
  42.0 1.2 %fusion.11 = (bf16[8,1,128,2,128]{4,3,2,1,0:T(2,128)(2,1)S(1)}, bf16[8,1,128,2,128]{4,3,2,1,0:T(2,128)(2,1)S(1)}, bf16[8,1,128,2,128]{4,3,2,1,0:T(2,128)(2,1)S(1)}) fusion(bf16[8,3,128,2,128]{4,3,2,1,0:T(2,128)(2,1)S(1)} %reshape.60), kind=kLoop, calls=%fused_computation.22 | loop fusion | bytes 3145728 | tf_op jit(solution)/shard_map/slice | solution.py:164
  43.2 0.7 fusion.4
  43.9 0.4 copy.17
  44.3 0.8 fusion.12
  45.1 0.4 copy.18
  45.6 0.0 copy-start.2
  45.6 1.3 %fusion.1 = bf16[8,128,2,128]{3,0,2,1:T(8,128)(2,1)} fusion(bf16[128,2,8,8]{3,2,1,0:T(8,128)(2,1)S(1)} %copy.18, bf16[8,1,128,2,128]{4,3,2,1,0:T(2,128)(2,1)S(1)} %get-tuple-element.23), kind=kOutput, calls=%fused_computation.2 | convolution fusion | flops 4456448 | bytes 1081344 | tf_op jit(solution)/shard_map/chrs,schd->rchd/dot_general | solution.py:36
  46.9 2.4 %copy.19 = bf16[8,128,2,128]{1,3,2,0:T(8,128)(2,1)} copy(bf16[8,128,2,128]{3,0,2,1:T(8,128)(2,1)} %fusion.1) | data formatting | bytes 1048576 | tf_op jit(solution)/shard_map/convert_element_type | solution.py:38
  49.3 7.7 %all-to-all-start.1 = ((bf16[8,128,256]{1,2,0:T(8,128)(2,1)}), bf16[8,128,256]{1,2,0:T(8,128)(2,1)}, u32[]{:S(2)}, u32[]{:S(2)}) async-start(bf16[8,128,256]{1,2,0:T(8,128)(2,1)} %bitcast.25), calls=%async_computation.1 | async-start | bytes 1048576 | tf_op jit(solution)/shard_map/all_to_all | solution.py:165
  57.0 0.0 copy-done.2
  57.0 0.8 slice_bitcast_fusion.2.refs_0_
  57.8 0.0 copy-done
  57.8 0.0 copy-done.1
  57.8 1.1 %slice_bitcast_fusion = (bf16[1024,256]{1,0:T(8,128)(2,1)}, bf16[1024,256]{1,0:T(8,128)(2,1)}) fusion(bf16[2,1024,256]{2,1,0:T(8,128)(2,1)S(1)} %copy-done.1, bf16[2,1024,256]{2,1,0:T(8,128)(2,1)S(1)} %copy-done), kind=kLoop, calls=%fused_computation.10 | loop fusion | bytes 2097152 | tf_op jit(solution)/shard_map/squeeze | solution.py:170
  58.9 14.3 %collective-permute-done.refs_1_.refs_3_ = bf16[2,1024,256]{2,1,0:T(8,128)(2,1)} collective-permute-done((bf16[2,1024,256]{2,1,0:T(8,128)(2,1)}, bf16[2,1024,256]{2,1,0:T(8,128)(2,1)}, u32[]{:S(2)}, u32[]{:S(2)}) %collective-permute-start) | collective-permute-done | bytes 1048608 | tf_op jit(solution)/shard_map/ppermute | solution.py:19
  73.1 8.4 %shard_map.38 = bf16[2,1024,256]{2,1,0:T(8,128)(2,1)} custom-call(s32[1]{0:T(128)} %bitcast.flag_ref, bf16[1024,256]{1,0:T(8,128)(2,1)} %slice_bitcast_fusion.2.refs_0_, bf16[2,1024,256]{2,1,0:T(8,128)(2,1)} %collective-permute-done.refs_1_.refs_3_, bf16[1024,256]{1,0:T(8,128)(2,1)} %get-tuple-element.29.refs_2_, ...), custom_call_target="tpu_custom_call" | custom-call | flops 1342177280 | bytes 3145728 | tf_op jit(solution)/shard_map/pallas_call | solution.py:95
  81.6 0.0 all-to-all-done.1
  81.6 1.2 %copy.20 = bf16[8,128,256]{2,1,0:T(8,128)(2,1)S(1)} copy(bf16[8,128,256]{1,2,0:T(8,128)(2,1)} %all-to-all-done.1) | data formatting | bytes 1048576 | tf_op jit(solution)/shard_map/all_to_all | solution.py:165
  82.8 0.8 bitcast_dynamic-update-slice_fusion
  (4 shorter events, 0.0 us)
Async XLA Ops:
  2.8 38.7 %all-to-all-start = ((bf16[8,3,128,256]{3,2,1,0:T(8,128)(2,1)}), bf16[8,3,128,256]{3,2,1,0:T(8,128)(2,1)S(1)}, u32[]{:S(2)}, u32[]{:S(2)}) async-start(bf16[8,3,128,256]{3,2,1,0:T(8,128)(2,1)} %get-tuple-element.20), calls=%async_computation | async-start | bytes 3145728 | tf_op jit(solution)/shard_map/all_to_all | solution.py:161
  8.4 64.7 %collective-permute-start = (bf16[2,1024,256]{2,1,0:T(8,128)(2,1)}, bf16[2,1024,256]{2,1,0:T(8,128)(2,1)}, u32[]{:S(2)}, u32[]{:S(2)}) collective-permute-start(bf16[2,1024,256]{2,1,0:T(8,128)(2,1)} %get-tuple-element.21), channel_id=1, source_target_pairs={{0,2},{2,4},{4,6},{6,8},{8,10},{10,12},{12,14},{1,3},{3,5},{5,7},{... | collective-permute-start | bytes 3145736 | tf_op jit(solution)/shard_map/ppermute | solution.py:19
  45.6 11.4 %copy-start.2 = (bf16[2,1024,256]{2,1,0:T(8,128)(2,1)S(1)}, bf16[2,1024,256]{2,1,0:T(8,128)(2,1)}, u32[]{:S(2)}) copy-start(bf16[2,1024,256]{2,1,0:T(8,128)(2,1)} %q_ref.1) | copy-start | bytes 3145732
  46.9 10.9 %copy-start = (bf16[2,1024,256]{2,1,0:T(8,128)(2,1)S(1)}, bf16[2,1024,256]{2,1,0:T(8,128)(2,1)}, u32[]{:S(2)}) copy-start(bf16[2,1024,256]{2,1,0:T(8,128)(2,1)} %kp_ref.1) | copy-start | bytes 3145732
  46.9 10.9 %copy-start.1 = (bf16[2,1024,256]{2,1,0:T(8,128)(2,1)S(1)}, bf16[2,1024,256]{2,1,0:T(8,128)(2,1)}, u32[]{:S(2)}) copy-start(bf16[2,1024,256]{2,1,0:T(8,128)(2,1)} %vp_ref.1) | copy-start | bytes 3145732
  49.3 32.3 %all-to-all-start.1 = ((bf16[8,128,256]{1,2,0:T(8,128)(2,1)}), bf16[8,128,256]{1,2,0:T(8,128)(2,1)}, u32[]{:S(2)}, u32[]{:S(2)}) async-start(bf16[8,128,256]{1,2,0:T(8,128)(2,1)} %bitcast.25), calls=%async_computation.1 | async-start | bytes 1048576 | tf_op jit(solution)/shard_map/all_to_all | solution.py:165

commit v8 on v7

--- a/solution.py
+++ b/solution.py
@@ -47,7 +47,7 @@
     )
 
     def scores(q, k_ref, low, high):
-        return lax.dot_general(q, k_ref[low:high, :], dims, preferred_element_type=jnp.float32) * score_scale
+        return lax.dot_general(q, k_ref[low:high, :], dims, preferred_element_type=jnp.float32)
 
     for tile in range(STRIDE // tq):
         low, high = tile * tq, (tile + 1) * tq
@@ -63,7 +63,7 @@
         maxima = functools.reduce(
             jnp.maximum, [jnp.max(p[0], axis=1, keepdims=True) for p in parts]
         )
-        expos = [jnp.exp(p[0] - maxima) for p in parts]
+        expos = [jnp.exp2((p[0] - maxima) * (score_scale * math.log2(math.e))) for p in parts]
         total = functools.reduce(jnp.add, [jnp.sum(e, axis=1, keepdims=True) for e in expos])
         inverse = 1.0 / total
         out = None

time: 84 us -> 83.6 us (level)
  no operation moved by 1% of the time
where the time goes in v8:
time: 83.6 us; the launch traced here: 83.2 us
  waiting for transfers between devices  44.3 us (53%)
  starting transfers between devices  16.4 us (20%)
  Pallas kernels  10.9 us (13%)
  local copies, waits for them, and re-layouts  8.8 us (11%)
  matrix products  1.98 us (2%)
  other arithmetic  0.84 us (1%)
    all_to_all x1, waiting for transfers between devices, local(): lax.all_to_all(stacked, 'seq', split_axis=0, concat_axis=0, tiled=True)  30 us
    ppermute x1, waiting for transfers between devices, shifted(): return lax.ppermute(block, axis, route)  14.3 us
    pallas_call x1, Pallas kernels, attend_rows(): pl.pallas_call(row_kernel, out_shape=jax.ShapeDtypeStruct((2, tokens, wid...  8.03 us
    all_to_all x1, starting transfers between devices, local(): lax.all_to_all(result.reshape(blocks, width, feature_width), 'seq', split...  7.72 us
    all_to_all x1, starting transfers between devices, local(): lax.all_to_all(stacked, 'seq', split_axis=0, concat_axis=0, tiled=True)  5.58 us
    ppermute x1, starting transfers between devices, shifted(): return lax.ppermute(block, axis, route)  3.08 us
    pallas_call x1, Pallas kernels, pack(): pl.pallas_call(pack_kernel, out_shape=(jax.ShapeDtypeStruct((blocks, 3, s...  2.85 us
    convert_element_type x1, local copies, waits for them, and re-layouts, attend_columns(): return jnp.einsum('chrs,schd->rchd', weights, value_cols, preferred_eleme...  2.38 us
  transfers between devices with their start and end apart: 3, of which 2 were waited for; matrix products, arithmetic and copies ran while one was open for 11% of the time, Pallas kernels for 10%

profile of v8, /device:TPU:17, one launch (start us, length us, event | category | flops | bytes accessed | tf_op | source)
XLA Modules:
  0.0 83.2 jit_solution(6691639807695411269)
XLA Ops:
  0.0 2.8 %shard_map.37 = (bf16[8,3,128,256]{3,2,1,0:T(8,128)(2,1)}, bf16[2,1024,256]{2,1,0:T(8,128)(2,1)}) custom-call(bf16[2,1024,256]{2,1,0:T(8,128)(2,1)} %q_ref.1, bf16[2,1024,256]{2,1,0:T(8,128)(2,1)} %kp_ref.1, bf16[2,1024,256]{2,1,0:T(8,128)(2,1)} %vp_ref.1, bf16[2,1024,256]{2,1,0:T(8,128)(2,1)} %kp_ref.1, bf16[2,1024,256]{2,1,0:T(8,128)(2,1)} %vp_ref.1), custom_call_target="tpu_custom_call" | custom-call | tf_op jit(solution)/shard_map/pallas_call | solution.py:125
  2.8 5.6 %all-to-all-start = ((bf16[8,3,128,256]{3,2,1,0:T(8,128)(2,1)}), bf16[8,3,128,256]{3,2,1,0:T(8,128)(2,1)S(1)}, u32[]{:S(2)}, u32[]{:S(2)}) async-start(bf16[8,3,128,256]{3,2,1,0:T(8,128)(2,1)} %get-tuple-element.20), calls=%async_computation | async-start | bytes 3145728 | tf_op jit(solution)/shard_map/all_to_all | solution.py:161
  8.4 3.1 %collective-permute-start = (bf16[2,1024,256]{2,1,0:T(8,128)(2,1)}, bf16[2,1024,256]{2,1,0:T(8,128)(2,1)}, u32[]{:S(2)}, u32[]{:S(2)}) collective-permute-start(bf16[2,1024,256]{2,1,0:T(8,128)(2,1)} %get-tuple-element.21), channel_id=1, source_target_pairs={{0,2},{2,4},{4,6},{6,8},{8,10},{10,12},{12,14},{1,3},{3,5},{5,7},{... | collective-permute-start | bytes 3145736 | tf_op jit(solution)/shard_map/ppermute | solution.py:19
  11.5 30.0 %all-to-all-done = bf16[8,3,128,256]{3,2,1,0:T(8,128)(2,1)S(1)} async-done(((bf16[8,3,128,256]{3,2,1,0:T(8,128)(2,1)}), bf16[8,3,128,256]{3,2,1,0:T(8,128)(2,1)S(1)}, u32[]{:S(2)}, u32[]{:S(2)}) %all-to-all-start) | async-done | bytes 1572896 | tf_op jit(solution)/shard_map/all_to_all | solution.py:161
  41.6 0.4 reshape.60
  42.0 1.2 %fusion.11 = (bf16[8,1,128,2,128]{4,3,2,1,0:T(2,128)(2,1)S(1)}, bf16[8,1,128,2,128]{4,3,2,1,0:T(2,128)(2,1)S(1)}, bf16[8,1,128,2,128]{4,3,2,1,0:T(2,128)(2,1)S(1)}) fusion(bf16[8,3,128,2,128]{4,3,2,1,0:T(2,128)(2,1)S(1)} %reshape.60), kind=kLoop, calls=%fused_computation.22 | loop fusion | bytes 3145728 | tf_op jit(solution)/shard_map/slice | solution.py:164
  43.2 0.7 fusion.4
  43.9 0.4 copy.17
  44.3 0.8 fusion.12
  45.1 0.4 copy.18
  45.6 0.0 copy-start.2
  45.6 1.3 %fusion.1 = bf16[8,128,2,128]{3,0,2,1:T(8,128)(2,1)} fusion(bf16[128,2,8,8]{3,2,1,0:T(8,128)(2,1)S(1)} %copy.18, bf16[8,1,128,2,128]{4,3,2,1,0:T(2,128)(2,1)S(1)} %get-tuple-element.23), kind=kOutput, calls=%fused_computation.2 | convolution fusion | flops 4456448 | bytes 1081344 | tf_op jit(solution)/shard_map/chrs,schd->rchd/dot_general | solution.py:36
  46.9 2.4 %copy.19 = bf16[8,128,2,128]{1,3,2,0:T(8,128)(2,1)} copy(bf16[8,128,2,128]{3,0,2,1:T(8,128)(2,1)} %fusion.1) | data formatting | bytes 1048576 | tf_op jit(solution)/shard_map/convert_element_type | solution.py:38
  49.3 7.7 %all-to-all-start.1 = ((bf16[8,128,256]{1,2,0:T(8,128)(2,1)}), bf16[8,128,256]{1,2,0:T(8,128)(2,1)}, u32[]{:S(2)}, u32[]{:S(2)}) async-start(bf16[8,128,256]{1,2,0:T(8,128)(2,1)} %bitcast.25), calls=%async_computation.1 | async-start | bytes 1048576 | tf_op jit(solution)/shard_map/all_to_all | solution.py:165
  57.0 0.0 copy-done.2
  57.0 0.8 %slice_bitcast_fusion.2.refs_0_ = bf16[1024,256]{1,0:T(8,128)(2,1)} fusion(bf16[2,1024,256]{2,1,0:T(8,128)(2,1)S(1)} %copy-done.2), kind=kLoop, calls=%fused_computation.12 | loop fusion | bytes 1048576 | tf_op jit(solution)/shard_map/squeeze | solution.py:170
  57.8 0.0 copy-done
  57.8 0.0 copy-done.1
  57.8 1.1 %slice_bitcast_fusion = (bf16[1024,256]{1,0:T(8,128)(2,1)}, bf16[1024,256]{1,0:T(8,128)(2,1)}) fusion(bf16[2,1024,256]{2,1,0:T(8,128)(2,1)S(1)} %copy-done.1, bf16[2,1024,256]{2,1,0:T(8,128)(2,1)S(1)} %copy-done), kind=kLoop, calls=%fused_computation.10 | loop fusion | bytes 2097152 | tf_op jit(solution)/shard_map/squeeze | solution.py:170
  58.9 14.3 %collective-permute-done.refs_1_.refs_3_ = bf16[2,1024,256]{2,1,0:T(8,128)(2,1)} collective-permute-done((bf16[2,1024,256]{2,1,0:T(8,128)(2,1)}, bf16[2,1024,256]{2,1,0:T(8,128)(2,1)}, u32[]{:S(2)}, u32[]{:S(2)}) %collective-permute-start) | collective-permute-done | bytes 1048608 | tf_op jit(solution)/shard_map/ppermute | solution.py:19
  73.1 8.0 %shard_map.38 = bf16[2,1024,256]{2,1,0:T(8,128)(2,1)} custom-call(s32[1]{0:T(128)} %bitcast.flag_ref, bf16[1024,256]{1,0:T(8,128)(2,1)} %slice_bitcast_fusion.2.refs_0_, bf16[2,1024,256]{2,1,0:T(8,128)(2,1)} %collective-permute-done.refs_1_.refs_3_, bf16[1024,256]{1,0:T(8,128)(2,1)} %get-tuple-element.29.refs_2_, ...), custom_call_target="tpu_custom_call" | custom-call | flops 1342177280 | bytes 3145728 | tf_op jit(solution)/shard_map/pallas_call | solution.py:95
  81.2 0.0 all-to-all-done.1
  81.2 1.2 %copy.20 = bf16[8,128,256]{2,1,0:T(8,128)(2,1)S(1)} copy(bf16[8,128,256]{1,2,0:T(8,128)(2,1)} %all-to-all-done.1) | data formatting | bytes 1048576 | tf_op jit(solution)/shard_map/all_to_all | solution.py:165
  82.4 0.8 bitcast_dynamic-update-slice_fusion
  (4 shorter events, 0.0 us)
Async XLA Ops:
  2.8 38.7 %all-to-all-start = ((bf16[8,3,128,256]{3,2,1,0:T(8,128)(2,1)}), bf16[8,3,128,256]{3,2,1,0:T(8,128)(2,1)S(1)}, u32[]{:S(2)}, u32[]{:S(2)}) async-start(bf16[8,3,128,256]{3,2,1,0:T(8,128)(2,1)} %get-tuple-element.20), calls=%async_computation | async-start | bytes 3145728 | tf_op jit(solution)/shard_map/all_to_all | solution.py:161
  8.4 64.7 %collective-permute-start = (bf16[2,1024,256]{2,1,0:T(8,128)(2,1)}, bf16[2,1024,256]{2,1,0:T(8,128)(2,1)}, u32[]{:S(2)}, u32[]{:S(2)}) collective-permute-start(bf16[2,1024,256]{2,1,0:T(8,128)(2,1)} %get-tuple-element.21), channel_id=1, source_target_pairs={{0,2},{2,4},{4,6},{6,8},{8,10},{10,12},{12,14},{1,3},{3,5},{5,7},{... | collective-permute-start | bytes 3145736 | tf_op jit(solution)/shard_map/ppermute | solution.py:19
  45.6 11.4 %copy-start.2 = (bf16[2,1024,256]{2,1,0:T(8,128)(2,1)S(1)}, bf16[2,1024,256]{2,1,0:T(8,128)(2,1)}, u32[]{:S(2)}) copy-start(bf16[2,1024,256]{2,1,0:T(8,128)(2,1)} %q_ref.1) | copy-start | bytes 3145732
  46.9 10.9 %copy-start = (bf16[2,1024,256]{2,1,0:T(8,128)(2,1)S(1)}, bf16[2,1024,256]{2,1,0:T(8,128)(2,1)}, u32[]{:S(2)}) copy-start(bf16[2,1024,256]{2,1,0:T(8,128)(2,1)} %kp_ref.1) | copy-start | bytes 3145732
  46.9 10.9 %copy-start.1 = (bf16[2,1024,256]{2,1,0:T(8,128)(2,1)S(1)}, bf16[2,1024,256]{2,1,0:T(8,128)(2,1)}, u32[]{:S(2)}) copy-start(bf16[2,1024,256]{2,1,0:T(8,128)(2,1)} %vp_ref.1) | copy-start | bytes 3145732
  49.3 31.9 %all-to-all-start.1 = ((bf16[8,128,256]{1,2,0:T(8,128)(2,1)}), bf16[8,128,256]{1,2,0:T(8,128)(2,1)}, u32[]{:S(2)}, u32[]{:S(2)}) async-start(bf16[8,128,256]{1,2,0:T(8,128)(2,1)} %bitcast.25), calls=%async_computation.1 | async-start | bytes 1048576 | tf_op jit(solution)/shard_map/all_to_all | solution.py:165

commit v9 on v8

--- a/solution.py
+++ b/solution.py
@@ -126,13 +126,13 @@
         pack_kernel,
         out_shape=(
             jax.ShapeDtypeStruct((blocks, 3, size, width), query_vectors.dtype),
-            jax.ShapeDtypeStruct((2, tokens, width), query_vectors.dtype),
+            jax.ShapeDtypeStruct((steps, 2, rows, width), query_vectors.dtype),
         ),
         grid=(steps,),
         in_specs=[column, column, column, row, row],
         out_specs=(
             pl.BlockSpec((blocks // steps, 3, size, width), lambda b: (b, 0, 0, 0)),
-            pl.BlockSpec((2, rows, width), lambda b: (0, b, 0)),
+            pl.BlockSpec((None, 2, rows, width), lambda b: (b, 0, 0, 0)),
         ),
     )(query_vectors, key_vectors, value_vectors, key_vectors, value_vectors)
 
@@ -145,10 +145,12 @@
     blocks = lax.axis_size("seq")
     width = STRIDE // blocks
     seq_index = lax.axis_index("seq")
+    half_rows = STRIDE // 2
     if width % 16 == 0:
         stacked, pair = pack(query_vectors, key_vectors, value_vectors, blocks)
     else:
-        pair = jnp.stack([key_vectors[0], value_vectors[0]])
+        pair = jnp.stack([key_vectors[0], value_vectors[0]]).reshape(2, 2, half_rows, feature_width)
+        pair = jnp.moveaxis(pair, 1, 0)
         stacked = jnp.stack(
             [
                 query_vectors[1].reshape(blocks, width, feature_width),
@@ -157,9 +159,16 @@
             ],
             axis=1,
         )
-    prev_pair = shifted(pair, "seq", 1)
+    first_half = shifted(pair[0], "seq", 1)
+    second_direct = lax.ppermute(pair[1], "seq", [(i, i + 1) for i in range(0, blocks - 1, 2)])
+    second_out = lax.ppermute(pair[1], "seq", [(i, i + 2) for i in range(1, blocks - 2, 2)])
+    second_relay = lax.ppermute(second_out, "seq", [(i, i - 1) for i in range(3, blocks, 2)])
     moved = lax.all_to_all(stacked, "seq", split_axis=0, concat_axis=0, tiled=True)
-    _, prev_pair = lax.optimization_barrier((moved, prev_pair))
+    _, first_half, second_direct, second_relay = lax.optimization_barrier(
+        (moved, first_half, second_direct, second_relay)
+    )
+    second_half = jnp.where(seq_index % 2 == 1, second_direct, second_relay)
+    prev_pair = jnp.concatenate([first_half, second_half], axis=1)
     grid = moved.reshape(blocks, 3, width, heads_here, DH)
     result = attend_columns(grid[:, 0], grid[:, 1], grid[:, 2])
     context = lax.all_to_all(

time: 83.6 us -> 96.8 us (1.16)
  starting transfers between devices: 16.4 us -> 36.2 us
  waiting for transfers between devices: 44.3 us -> 33.3 us
  other arithmetic: 0.84 us -> 4.03 us
  local copies, waits for them, and re-layouts: 8.8 us -> 9.81 us
    ppermute x1, waiting for transfers between devices: 14.3 us -> 0.01 us  [shifted(): return lax.ppermute(block, axis, route)]
    all_to_all x1, starting transfers between devices: 7.72 us -> 20.3 us  [local(): lax.all_to_all(result.reshape(blocks, width, feature_width), 'seq', split...]
    ppermute x0 -> x3, waiting for transfers between devices: none -> 11.4 us  [the longest x1 11.4 us: local(): lax.ppermute(second_out, 'seq', [(i, i - 1) for i in range(3, blocks, 2)])]
    ppermute x0 -> x3, starting transfers between devices: none -> 8.27 us  [the longest x1 5.52 us: local(): lax.ppermute(pair[1], 'seq', [(i, i + 1) for i in range(0, blocks - 1, 2)])]
    all_to_all x1, waiting for transfers between devices: 30 us -> 21.9 us  [local(): lax.all_to_all(stacked, 'seq', split_axis=0, concat_axis=0, tiled=True)]
    concatenate x0 -> x1, other arithmetic: none -> 2.09 us  [local(): prev_pair = jnp.concatenate([first_half, second_half], axis=1)]
    ppermute x1, starting transfers between devices: 3.08 us -> 1.91 us  [shifted(): return lax.ppermute(block, axis, route)]
    select_n x0 -> x1, other arithmetic: none -> 1.1 us  [local(): second_half = jnp.where(seq_index % 2 == 1, second_direct, second_relay)]
  transfers between devices with their start and end apart: 3 -> 6, of which waited for: 2 -> 2; matrix products, arithmetic and copies ran while one was open for 11% -> 14% of each run, Pallas kernels for 10% -> 8%
where the time goes in v9:
time: 96.8 us; the launch traced here: 96.3 us
  starting transfers between devices  36.2 us (37%)
  waiting for transfers between devices  33.3 us (34%)
  Pallas kernels  10.9 us (11%)
  local copies, waits for them, and re-layouts  9.81 us (10%)
  other arithmetic  4.03 us (4%)
  matrix products  1.96 us (2%)
    all_to_all x1, waiting for transfers between devices, local(): lax.all_to_all(stacked, 'seq', split_axis=0, concat_axis=0, tiled=True)  21.9 us
    all_to_all x1, starting transfers between devices, local(): lax.all_to_all(result.reshape(blocks, width, feature_width), 'seq', split...  20.3 us
    ppermute x1, waiting for transfers between devices, local(): lax.ppermute(second_out, 'seq', [(i, i - 1) for i in range(3, blocks, 2)])  11.4 us
    pallas_call x1, Pallas kernels, attend_rows(): pl.pallas_call(row_kernel, out_shape=jax.ShapeDtypeStruct((2, tokens, wid...  8.03 us
    all_to_all x1, starting transfers between devices, local(): lax.all_to_all(stacked, 'seq', split_axis=0, concat_axis=0, tiled=True)  5.71 us
    ppermute x1, starting transfers between devices, local(): lax.ppermute(pair[1], 'seq', [(i, i + 1) for i in range(0, blocks - 1, 2)])  5.52 us
    pallas_call x1, Pallas kernels, pack(): pl.pallas_call(pack_kernel, out_shape=(jax.ShapeDtypeStruct((blocks, 3, s...  2.85 us
    convert_element_type x1, local copies, waits for them, and re-layouts, attend_columns(): return jnp.einsum('chrs,schd->rchd', weights, value_cols, preferred_eleme...  2.38 us
  transfers between devices with their start and end apart: 6, of which 2 were waited for; matrix products, arithmetic and copies ran while one was open for 14% of the time, Pallas kernels for 8%

profile of v9, /device:TPU:17, one launch (start us, length us, event | category | flops | bytes accessed | tf_op | source)
XLA Modules:
  0.0 96.3 jit_solution(1049683505082831916)
XLA Ops:
  0.0 2.8 %shard_map.37 = (bf16[8,3,128,256]{3,2,1,0:T(8,128)(2,1)}, bf16[2,2,512,256]{3,2,1,0:T(8,128)(2,1)}) custom-call(bf16[2,1024,256]{2,1,0:T(8,128)(2,1)} %q_ref.1, bf16[2,1024,256]{2,1,0:T(8,128)(2,1)} %kp_ref.1, bf16[2,1024,256]{2,1,0:T(8,128)(2,1)} %vp_ref.1, bf16[2,1024,256]{2,1,0:T(8,128)(2,1)} %kp_ref.1, bf16[2,1024,256]{2,1,0:T(8,128)(2,1)} %vp_ref.1), custom_call_target="tpu_custom_call" | custom-call | tf_op jit(solution)/shard_map/pallas_call | solution.py:125
  2.9 5.7 %all-to-all-start = ((bf16[8,3,128,256]{3,2,1,0:T(8,128)(2,1)}), bf16[8,3,128,256]{3,2,1,0:T(8,128)(2,1)S(1)}, u32[]{:S(2)}, u32[]{:S(2)}) async-start(bf16[8,3,128,256]{3,2,1,0:T(8,128)(2,1)} %get-tuple-element.22), calls=%async_computation | async-start | bytes 3145728 | tf_op jit(solution)/shard_map/all_to_all | solution.py:166
  8.6 1.0 %slice_bitcast_fusion.2 = (bf16[2,512,256]{2,1,0:T(8,128)(2,1)}, bf16[2,512,256]{2,1,0:T(8,128)(2,1)}) fusion(bf16[2,2,512,256]{3,2,1,0:T(8,128)(2,1)S(1)} %copy-done.3), kind=kLoop, calls=%fused_computation.13 | loop fusion | bytes 2097152 | tf_op jit(solution)/shard_map/squeeze | solution.py:163
  9.6 1.5 %collective-permute-start.2 = (bf16[2,512,256]{2,1,0:T(8,128)(2,1)}, bf16[2,512,256]{2,1,0:T(8,128)(2,1)}, u32[]{:S(2)}, u32[]{:S(2)}) collective-permute-start(bf16[2,512,256]{2,1,0:T(8,128)(2,1)} %get-tuple-element.30), channel_id=1, source_target_pairs={{2,6},{6,10},{10,14},{3,7},{7,11},{11,15},{18,22},{22,26},{26,30},... | collective-permute-start | bytes 1572872 | tf_op jit(solution)/shard_map/ppermute | solution.py:164
  11.1 5.5 %collective-permute-start.1 = (bf16[2,512,256]{2,1,0:T(8,128)(2,1)}, bf16[2,512,256]{2,1,0:T(8,128)(2,1)}, u32[]{:S(2)}, u32[]{:S(2)}) collective-permute-start(bf16[2,512,256]{2,1,0:T(8,128)(2,1)} %get-tuple-element.30), channel_id=1, source_target_pairs={{0,2},{4,6},{8,10},{12,14},{1,3},{5,7},{9,11},{13,15},{16,18},{20,... | collective-permute-start | bytes 1572872 | tf_op jit(solution)/shard_map/ppermute | solution.py:163
  16.6 1.9 %collective-permute-start = (bf16[2,512,256]{2,1,0:T(8,128)(2,1)}, bf16[2,512,256]{2,1,0:T(8,128)(2,1)}, u32[]{:S(2)}, u32[]{:S(2)}) collective-permute-start(bf16[2,512,256]{2,1,0:T(8,128)(2,1)} %get-tuple-element.31), channel_id=1, source_target_pairs={{0,2},{2,4},{4,6},{6,8},{8,10},{10,12},{12,14},{1,3},{3,5},{5,7},{... | collective-permute-start | bytes 1572872 | tf_op jit(solution)/shard_map/ppermute | solution.py:19
  18.5 1.3 %collective-permute-start.3 = (bf16[2,512,256]{2,1,0:T(8,128)(2,1)}, bf16[2,512,256]{2,1,0:T(8,128)(2,1)}, u32[]{:S(2)}, u32[]{:S(2)}) collective-permute-start(bf16[2,512,256]{2,1,0:T(8,128)(2,1)} %collective-permute-done.2), channel_id=1, source_target_pairs={{6,4},{10,8},{14,12},{7,5},{11,9},{15,13},{22,20},{26,24},{30,28},... | collective-permute-start | bytes 1572872 | tf_op jit(solution)/shard_map/ppermute | solution.py:165
  19.8 21.9 %all-to-all-done = bf16[8,3,128,256]{3,2,1,0:T(8,128)(2,1)S(1)} async-done(((bf16[8,3,128,256]{3,2,1,0:T(8,128)(2,1)}), bf16[8,3,128,256]{3,2,1,0:T(8,128)(2,1)S(1)}, u32[]{:S(2)}, u32[]{:S(2)}) %all-to-all-start) | async-done | bytes 1572896 | tf_op jit(solution)/shard_map/all_to_all | solution.py:166
  42.1 1.2 %fusion.11 = (bf16[8,1,128,2,128]{4,3,2,1,0:T(2,128)(2,1)S(1)}, bf16[8,1,128,2,128]{4,3,2,1,0:T(2,128)(2,1)S(1)}, bf16[8,1,128,2,128]{4,3,2,1,0:T(2,128)(2,1)S(1)}) fusion(bf16[8,3,128,2,128]{4,3,2,1,0:T(2,128)(2,1)S(1)} %reshape.60), kind=kLoop, calls=%fused_computation.26 | loop fusion | bytes 3145728 | tf_op jit(solution)/shard_map/slice | solution.py:173
  43.3 0.7 fusion.4
  44.0 0.4 copy.17
  44.4 0.8 fusion.12
  45.3 0.4 copy.18
  45.7 1.3 %fusion.1 = bf16[8,128,2,128]{3,0,2,1:T(8,128)(2,1)} fusion(bf16[128,2,8,8]{3,2,1,0:T(8,128)(2,1)S(1)} %copy.18, bf16[8,1,128,2,128]{4,3,2,1,0:T(2,128)(2,1)S(1)} %get-tuple-element.27), kind=kOutput, calls=%fused_computation.2 | convolution fusion | flops 4456448 | bytes 1081344 | tf_op jit(solution)/shard_map/chrs,schd->rchd/dot_general | solution.py:36
  47.0 2.4 %copy.19 = bf16[8,128,2,128]{1,3,2,0:T(8,128)(2,1)} copy(bf16[8,128,2,128]{3,0,2,1:T(8,128)(2,1)} %fusion.1) | data formatting | bytes 1048576 | tf_op jit(solution)/shard_map/convert_element_type | solution.py:38
  49.4 20.3 %all-to-all-start.1 = ((bf16[8,128,256]{1,2,0:T(8,128)(2,1)}), bf16[8,128,256]{1,2,0:T(8,128)(2,1)}, u32[]{:S(2)}, u32[]{:S(2)}) async-start(bf16[8,128,256]{1,2,0:T(8,128)(2,1)} %bitcast.29), calls=%async_computation.1 | async-start | bytes 1048576 | tf_op jit(solution)/shard_map/all_to_all | solution.py:174
  69.7 0.8 slice_bitcast_fusion.4.refs_0_
  70.5 1.0 %slice_bitcast_fusion = (bf16[1024,256]{1,0:T(8,128)(2,1)}, bf16[1024,256]{1,0:T(8,128)(2,1)}) fusion(bf16[2,1024,256]{2,1,0:T(8,128)(2,1)S(1)} %copy-done.1, bf16[2,1024,256]{2,1,0:T(8,128)(2,1)S(1)} %copy-done), kind=kLoop, calls=%fused_computation.11 | loop fusion | bytes 2097152 | tf_op jit(solution)/shard_map/squeeze | solution.py:179
  71.5 11.4 %collective-permute-done.3 = bf16[2,512,256]{2,1,0:T(8,128)(2,1)} collective-permute-done((bf16[2,512,256]{2,1,0:T(8,128)(2,1)}, bf16[2,512,256]{2,1,0:T(8,128)(2,1)}, u32[]{:S(2)}, u32[]{:S(2)}) %collective-permute-start.3) | collective-permute-done | bytes 524320 | tf_op jit(solution)/shard_map/ppermute | solution.py:165
  82.9 1.1 %broadcast_select_fusion = bf16[2,512,256]{2,1,0:T(8,128)(2,1)S(1)} fusion(bf16[2,512,256]{2,1,0:T(8,128)(2,1)} %collective-permute-done.1, bf16[2,512,256]{2,1,0:T(8,128)(2,1)} %collective-permute-done.3, pred[]{:T(512)S(6)} %eq.5), kind=kLoop, calls=%fused_computation.16 | loop fusion | flops 262144 | bytes 1572865 | tf_op jit(solution)/shard_map/jit(_where)/select_n | solution.py:170
  84.0 2.1 %pad_maximum_fusion.refs_1_.refs_3_ = bf16[2,1024,256]{2,1,0:T(8,128)(2,1)} fusion(bf16[2,512,256]{2,1,0:T(8,128)(2,1)S(1)} %broadcast_select_fusion, bf16[2,512,256]{2,1,0:T(8,128)(2,1)} %collective-permute-done), kind=kLoop, calls=%fused_computation.5 | loop fusion | flops 2097152 | bytes 2097152 | tf_op jit(solution)/shard_map/concatenate | solution.py:171
  86.1 8.0 %shard_map.38 = bf16[2,1024,256]{2,1,0:T(8,128)(2,1)} custom-call(s32[1]{0:T(128)} %bitcast.flag_ref, bf16[1024,256]{1,0:T(8,128)(2,1)} %slice_bitcast_fusion.4.refs_0_, bf16[2,1024,256]{2,1,0:T(8,128)(2,1)} %pad_maximum_fusion.refs_1_.refs_3_, bf16[1024,256]{1,0:T(8,128)(2,1)} %get-tuple-element.35.refs_2_, ...), custom_call_target="tpu_custom_call" | custom-call | flops 1342177280 | bytes 3145728 | tf_op jit(solution)/shard_map/pallas_call | solution.py:95
  94.2 1.2 %copy.20 = bf16[8,128,256]{2,1,0:T(8,128)(2,1)S(1)} copy(bf16[8,128,256]{1,2,0:T(8,128)(2,1)} %all-to-all-done.1) | data formatting | bytes 1048576 | tf_op jit(solution)/shard_map/all_to_all | solution.py:174
  95.4 0.8 bitcast_dynamic-update-slice_fusion
  (15 shorter events, 0.5 us)
Async XLA Ops:
  2.8 5.7 %copy-start.3 = (bf16[2,2,512,256]{3,2,1,0:T(8,128)(2,1)S(1)}, bf16[2,2,512,256]{3,2,1,0:T(8,128)(2,1)}, u32[]{:S(2)}) copy-start(bf16[2,2,512,256]{3,2,1,0:T(8,128)(2,1)} %get-tuple-element.23) | copy-start | bytes 3145732
  2.9 38.9 %all-to-all-start = ((bf16[8,3,128,256]{3,2,1,0:T(8,128)(2,1)}), bf16[8,3,128,256]{3,2,1,0:T(8,128)(2,1)S(1)}, u32[]{:S(2)}, u32[]{:S(2)}) async-start(bf16[8,3,128,256]{3,2,1,0:T(8,128)(2,1)} %get-tuple-element.22), calls=%async_computation | async-start | bytes 3145728 | tf_op jit(solution)/shard_map/all_to_all | solution.py:166
  9.6 8.9 %collective-permute-start.2 = (bf16[2,512,256]{2,1,0:T(8,128)(2,1)}, bf16[2,512,256]{2,1,0:T(8,128)(2,1)}, u32[]{:S(2)}, u32[]{:S(2)}) collective-permute-start(bf16[2,512,256]{2,1,0:T(8,128)(2,1)} %get-tuple-element.30), channel_id=1, source_target_pairs={{2,6},{6,10},{10,14},{3,7},{7,11},{11,15},{18,22},{22,26},{26,30},... | collective-permute-start | bytes 1572872 | tf_op jit(solution)/shard_map/ppermute | solution.py:164
  11.1 60.5 %collective-permute-start.1 = (bf16[2,512,256]{2,1,0:T(8,128)(2,1)}, bf16[2,512,256]{2,1,0:T(8,128)(2,1)}, u32[]{:S(2)}, u32[]{:S(2)}) collective-permute-start(bf16[2,512,256]{2,1,0:T(8,128)(2,1)} %get-tuple-element.30), channel_id=1, source_target_pairs={{0,2},{4,6},{8,10},{12,14},{1,3},{5,7},{9,11},{13,15},{16,18},{20,... | collective-permute-start | bytes 1572872 | tf_op jit(solution)/shard_map/ppermute | solution.py:163
  16.6 55.0 %collective-permute-start = (bf16[2,512,256]{2,1,0:T(8,128)(2,1)}, bf16[2,512,256]{2,1,0:T(8,128)(2,1)}, u32[]{:S(2)}, u32[]{:S(2)}) collective-permute-start(bf16[2,512,256]{2,1,0:T(8,128)(2,1)} %get-tuple-element.31), channel_id=1, source_target_pairs={{0,2},{2,4},{4,6},{6,8},{8,10},{10,12},{12,14},{1,3},{3,5},{5,7},{... | collective-permute-start | bytes 1572872 | tf_op jit(solution)/shard_map/ppermute | solution.py:19
  18.5 64.4 %collective-permute-start.3 = (bf16[2,512,256]{2,1,0:T(8,128)(2,1)}, bf16[2,512,256]{2,1,0:T(8,128)(2,1)}, u32[]{:S(2)}, u32[]{:S(2)}) collective-permute-start(bf16[2,512,256]{2,1,0:T(8,128)(2,1)} %collective-permute-done.2), channel_id=1, source_target_pairs={{6,4},{10,8},{14,12},{7,5},{11,9},{15,13},{22,20},{26,24},{30,28},... | collective-permute-start | bytes 1572872 | tf_op jit(solution)/shard_map/ppermute | solution.py:165
  45.7 23.9 %copy-start.2 = (bf16[2,1024,256]{2,1,0:T(8,128)(2,1)S(1)}, bf16[2,1024,256]{2,1,0:T(8,128)(2,1)}, u32[]{:S(2)}) copy-start(bf16[2,1024,256]{2,1,0:T(8,128)(2,1)} %q_ref.1) | copy-start | bytes 3145732
  47.0 23.5 %copy-start = (bf16[2,1024,256]{2,1,0:T(8,128)(2,1)S(1)}, bf16[2,1024,256]{2,1,0:T(8,128)(2,1)}, u32[]{:S(2)}) copy-start(bf16[2,1024,256]{2,1,0:T(8,128)(2,1)} %kp_ref.1) | copy-start | bytes 3145732
  47.0 23.5 %copy-start.1 = (bf16[2,1024,256]{2,1,0:T(8,128)(2,1)S(1)}, bf16[2,1024,256]{2,1,0:T(8,128)(2,1)}, u32[]{:S(2)}) copy-start(bf16[2,1024,256]{2,1,0:T(8,128)(2,1)} %vp_ref.1) | copy-start | bytes 3145732
  49.4 44.8 %all-to-all-start.1 = ((bf16[8,128,256]{1,2,0:T(8,128)(2,1)}), bf16[8,128,256]{1,2,0:T(8,128)(2,1)}, u32[]{:S(2)}, u32[]{:S(2)}) async-start(bf16[8,128,256]{1,2,0:T(8,128)(2,1)} %bitcast.29), calls=%async_computation.1 | async-start | bytes 1048576 | tf_op jit(solution)/shard_map/all_to_all | solution.py:174

commit v10 on v8

--- a/solution.py
+++ b/solution.py
@@ -10,7 +10,7 @@
 
 DH = 128
 STRIDE = 1024
-QUERY_TILE = 256
+QUERY_TILE = 128
 
 
 def shifted(block, axis, distance):

time: 83.6 us -> 86.6 us (1.036)
  Pallas kernels: 10.9 us -> 13.8 us
    pallas_call x1, Pallas kernels: 8.03 us -> 10.9 us  [attend_rows(): pl.pallas_call(row_kernel, out_shape=jax.ShapeDtypeStruct((2, tokens, wid...]
  transfers between devices with their start and end apart: 3 -> 3, of which waited for: 2 -> 2; matrix products, arithmetic and copies ran while one was open for 11% -> 11% of each run, Pallas kernels for 10% -> 13%
where the time goes in v10:
time: 86.6 us; the launch traced here: 86.2 us
  waiting for transfers between devices  44.3 us (51%)
  starting transfers between devices  16.4 us (19%)
  Pallas kernels  13.8 us (16%)
  local copies, waits for them, and re-layouts  8.8 us (10%)
  matrix products  1.98 us (2%)
    all_to_all x1, waiting for transfers between devices, local(): lax.all_to_all(stacked, 'seq', split_axis=0, concat_axis=0, tiled=True)  30 us
    ppermute x1, waiting for transfers between devices, shifted(): return lax.ppermute(block, axis, route)  14.3 us
    pallas_call x1, Pallas kernels, attend_rows(): pl.pallas_call(row_kernel, out_shape=jax.ShapeDtypeStruct((2, tokens, wid...  10.9 us
    all_to_all x1, starting transfers between devices, local(): lax.all_to_all(result.reshape(blocks, width, feature_width), 'seq', split...  7.72 us
    all_to_all x1, starting transfers between devices, local(): lax.all_to_all(stacked, 'seq', split_axis=0, concat_axis=0, tiled=True)  5.58 us
    ppermute x1, starting transfers between devices, shifted(): return lax.ppermute(block, axis, route)  3.08 us
    pallas_call x1, Pallas kernels, pack(): pl.pallas_call(pack_kernel, out_shape=(jax.ShapeDtypeStruct((blocks, 3, s...  2.85 us
    convert_element_type x1, local copies, waits for them, and re-layouts, attend_columns(): return jnp.einsum('chrs,schd->rchd', weights, value_cols, preferred_eleme...  2.38 us
  transfers between devices with their start and end apart: 3, of which 2 were waited for; matrix products, arithmetic and copies ran while one was open for 11% of the time, Pallas kernels for 13%

profile of v10, /device:TPU:17, one launch (start us, length us, event | category | flops | bytes accessed | tf_op | source)
XLA Modules:
  0.0 86.2 jit_solution(5153034273753427663)
XLA Ops:
  0.0 2.8 %shard_map.37 = (bf16[8,3,128,256]{3,2,1,0:T(8,128)(2,1)}, bf16[2,1024,256]{2,1,0:T(8,128)(2,1)}) custom-call(bf16[2,1024,256]{2,1,0:T(8,128)(2,1)} %q_ref.1, bf16[2,1024,256]{2,1,0:T(8,128)(2,1)} %kp_ref.1, bf16[2,1024,256]{2,1,0:T(8,128)(2,1)} %vp_ref.1, bf16[2,1024,256]{2,1,0:T(8,128)(2,1)} %kp_ref.1, bf16[2,1024,256]{2,1,0:T(8,128)(2,1)} %vp_ref.1), custom_call_target="tpu_custom_call" | custom-call | tf_op jit(solution)/shard_map/pallas_call | solution.py:125
  2.8 5.6 %all-to-all-start = ((bf16[8,3,128,256]{3,2,1,0:T(8,128)(2,1)}), bf16[8,3,128,256]{3,2,1,0:T(8,128)(2,1)S(1)}, u32[]{:S(2)}, u32[]{:S(2)}) async-start(bf16[8,3,128,256]{3,2,1,0:T(8,128)(2,1)} %get-tuple-element.20), calls=%async_computation | async-start | bytes 3145728 | tf_op jit(solution)/shard_map/all_to_all | solution.py:161
  8.4 3.1 %collective-permute-start = (bf16[2,1024,256]{2,1,0:T(8,128)(2,1)}, bf16[2,1024,256]{2,1,0:T(8,128)(2,1)}, u32[]{:S(2)}, u32[]{:S(2)}) collective-permute-start(bf16[2,1024,256]{2,1,0:T(8,128)(2,1)} %get-tuple-element.21), channel_id=1, source_target_pairs={{0,2},{2,4},{4,6},{6,8},{8,10},{10,12},{12,14},{1,3},{3,5},{5,7},{... | collective-permute-start | bytes 3145736 | tf_op jit(solution)/shard_map/ppermute | solution.py:19
  11.5 30.0 %all-to-all-done = bf16[8,3,128,256]{3,2,1,0:T(8,128)(2,1)S(1)} async-done(((bf16[8,3,128,256]{3,2,1,0:T(8,128)(2,1)}), bf16[8,3,128,256]{3,2,1,0:T(8,128)(2,1)S(1)}, u32[]{:S(2)}, u32[]{:S(2)}) %all-to-all-start) | async-done | bytes 1572896 | tf_op jit(solution)/shard_map/all_to_all | solution.py:161
  41.6 0.4 reshape.60
  42.0 1.2 %fusion.11 = (bf16[8,1,128,2,128]{4,3,2,1,0:T(2,128)(2,1)S(1)}, bf16[8,1,128,2,128]{4,3,2,1,0:T(2,128)(2,1)S(1)}, bf16[8,1,128,2,128]{4,3,2,1,0:T(2,128)(2,1)S(1)}) fusion(bf16[8,3,128,2,128]{4,3,2,1,0:T(2,128)(2,1)S(1)} %reshape.60), kind=kLoop, calls=%fused_computation.22 | loop fusion | bytes 3145728 | tf_op jit(solution)/shard_map/slice | solution.py:164
  43.2 0.7 fusion.4
  43.9 0.4 copy.17
  44.3 0.8 fusion.12
  45.1 0.4 copy.18
  45.6 0.0 copy-start.2
  45.6 1.3 %fusion.1 = bf16[8,128,2,128]{3,0,2,1:T(8,128)(2,1)} fusion(bf16[128,2,8,8]{3,2,1,0:T(8,128)(2,1)S(1)} %copy.18, bf16[8,1,128,2,128]{4,3,2,1,0:T(2,128)(2,1)S(1)} %get-tuple-element.23), kind=kOutput, calls=%fused_computation.2 | convolution fusion | flops 4456448 | bytes 1081344 | tf_op jit(solution)/shard_map/chrs,schd->rchd/dot_general | solution.py:36
  46.9 2.4 %copy.19 = bf16[8,128,2,128]{1,3,2,0:T(8,128)(2,1)} copy(bf16[8,128,2,128]{3,0,2,1:T(8,128)(2,1)} %fusion.1) | data formatting | bytes 1048576 | tf_op jit(solution)/shard_map/convert_element_type | solution.py:38
  49.3 7.7 %all-to-all-start.1 = ((bf16[8,128,256]{1,2,0:T(8,128)(2,1)}), bf16[8,128,256]{1,2,0:T(8,128)(2,1)}, u32[]{:S(2)}, u32[]{:S(2)}) async-start(bf16[8,128,256]{1,2,0:T(8,128)(2,1)} %bitcast.25), calls=%async_computation.1 | async-start | bytes 1048576 | tf_op jit(solution)/shard_map/all_to_all | solution.py:165
  57.0 0.0 copy-done.2
  57.0 0.8 slice_bitcast_fusion.2.refs_0_
  57.8 0.0 copy-done
  57.8 0.0 copy-done.1
  57.8 1.1 %slice_bitcast_fusion = (bf16[1024,256]{1,0:T(8,128)(2,1)}, bf16[1024,256]{1,0:T(8,128)(2,1)}) fusion(bf16[2,1024,256]{2,1,0:T(8,128)(2,1)S(1)} %copy-done.1, bf16[2,1024,256]{2,1,0:T(8,128)(2,1)S(1)} %copy-done), kind=kLoop, calls=%fused_computation.10 | loop fusion | bytes 2097152 | tf_op jit(solution)/shard_map/squeeze | solution.py:170
  58.9 14.3 %collective-permute-done.refs_1_.refs_3_ = bf16[2,1024,256]{2,1,0:T(8,128)(2,1)} collective-permute-done((bf16[2,1024,256]{2,1,0:T(8,128)(2,1)}, bf16[2,1024,256]{2,1,0:T(8,128)(2,1)}, u32[]{:S(2)}, u32[]{:S(2)}) %collective-permute-start) | collective-permute-done | bytes 1048608 | tf_op jit(solution)/shard_map/ppermute | solution.py:19
  73.1 10.9 %shard_map.38 = bf16[2,1024,256]{2,1,0:T(8,128)(2,1)} custom-call(s32[1]{0:T(128)} %bitcast.flag_ref, bf16[1024,256]{1,0:T(8,128)(2,1)} %slice_bitcast_fusion.2.refs_0_, bf16[2,1024,256]{2,1,0:T(8,128)(2,1)} %collective-permute-done.refs_1_.refs_3_, bf16[1024,256]{1,0:T(8,128)(2,1)} %get-tuple-element.29.refs_2_, ...), custom_call_target="tpu_custom_call" | custom-call | flops 1207959552 | bytes 3145728 | tf_op jit(solution)/shard_map/pallas_call | solution.py:95
  84.1 0.0 all-to-all-done.1
  84.1 1.2 %copy.20 = bf16[8,128,256]{2,1,0:T(8,128)(2,1)S(1)} copy(bf16[8,128,256]{1,2,0:T(8,128)(2,1)} %all-to-all-done.1) | data formatting | bytes 1048576 | tf_op jit(solution)/shard_map/all_to_all | solution.py:165
  85.3 0.8 bitcast_dynamic-update-slice_fusion
  (4 shorter events, 0.0 us)
Async XLA Ops:
  2.8 38.7 %all-to-all-start = ((bf16[8,3,128,256]{3,2,1,0:T(8,128)(2,1)}), bf16[8,3,128,256]{3,2,1,0:T(8,128)(2,1)S(1)}, u32[]{:S(2)}, u32[]{:S(2)}) async-start(bf16[8,3,128,256]{3,2,1,0:T(8,128)(2,1)} %get-tuple-element.20), calls=%async_computation | async-start | bytes 3145728 | tf_op jit(solution)/shard_map/all_to_all | solution.py:161
  8.4 64.7 %collective-permute-start = (bf16[2,1024,256]{2,1,0:T(8,128)(2,1)}, bf16[2,1024,256]{2,1,0:T(8,128)(2,1)}, u32[]{:S(2)}, u32[]{:S(2)}) collective-permute-start(bf16[2,1024,256]{2,1,0:T(8,128)(2,1)} %get-tuple-element.21), channel_id=1, source_target_pairs={{0,2},{2,4},{4,6},{6,8},{8,10},{10,12},{12,14},{1,3},{3,5},{5,7},{... | collective-permute-start | bytes 3145736 | tf_op jit(solution)/shard_map/ppermute | solution.py:19
  45.6 11.4 %copy-start.2 = (bf16[2,1024,256]{2,1,0:T(8,128)(2,1)S(1)}, bf16[2,1024,256]{2,1,0:T(8,128)(2,1)}, u32[]{:S(2)}) copy-start(bf16[2,1024,256]{2,1,0:T(8,128)(2,1)} %q_ref.1) | copy-start | bytes 3145732
  46.9 10.9 %copy-start = (bf16[2,1024,256]{2,1,0:T(8,128)(2,1)S(1)}, bf16[2,1024,256]{2,1,0:T(8,128)(2,1)}, u32[]{:S(2)}) copy-start(bf16[2,1024,256]{2,1,0:T(8,128)(2,1)} %kp_ref.1) | copy-start | bytes 3145732
  46.9 10.9 %copy-start.1 = (bf16[2,1024,256]{2,1,0:T(8,128)(2,1)S(1)}, bf16[2,1024,256]{2,1,0:T(8,128)(2,1)}, u32[]{:S(2)}) copy-start(bf16[2,1024,256]{2,1,0:T(8,128)(2,1)} %vp_ref.1) | copy-start | bytes 3145732
  49.3 34.8 %all-to-all-start.1 = ((bf16[8,128,256]{1,2,0:T(8,128)(2,1)}), bf16[8,128,256]{1,2,0:T(8,128)(2,1)}, u32[]{:S(2)}, u32[]{:S(2)}) async-start(bf16[8,128,256]{1,2,0:T(8,128)(2,1)} %bitcast.25), calls=%async_computation.1 | async-start | bytes 1048576 | tf_op jit(solution)/shard_map/all_to_all | solution.py:165

commit v11 on v10

--- a/solution.py
+++ b/solution.py
@@ -10,7 +10,7 @@
 
 DH = 128
 STRIDE = 1024
-QUERY_TILE = 128
+QUERY_TILE = 512
 
 
 def shifted(block, axis, distance):

time: 86.6 us -> 83.8 us (0.968)
  Pallas kernels: 13.8 us -> 11 us
    pallas_call x1, Pallas kernels: 10.9 us -> 8.14 us  [attend_rows(): pl.pallas_call(row_kernel, out_shape=jax.ShapeDtypeStruct((2, tokens, wid...]
  transfers between devices with their start and end apart: 3 -> 3, of which waited for: 2 -> 2; matrix products, arithmetic and copies ran while one was open for 11% -> 11% of each run, Pallas kernels for 13% -> 10%
where the time goes in v11:
time: 83.8 us; the launch traced here: 83.4 us
  waiting for transfers between devices  44.3 us (53%)
  starting transfers between devices  16.4 us (20%)
  Pallas kernels  11 us (13%)
  local copies, waits for them, and re-layouts  8.8 us (11%)
  matrix products  1.98 us (2%)
  other arithmetic  0.84 us (1%)
    all_to_all x1, waiting for transfers between devices, local(): lax.all_to_all(stacked, 'seq', split_axis=0, concat_axis=0, tiled=True)  30 us
    ppermute x1, waiting for transfers between devices, shifted(): return lax.ppermute(block, axis, route)  14.3 us
    pallas_call x1, Pallas kernels, attend_rows(): pl.pallas_call(row_kernel, out_shape=jax.ShapeDtypeStruct((2, tokens, wid...  8.14 us
    all_to_all x1, starting transfers between devices, local(): lax.all_to_all(result.reshape(blocks, width, feature_width), 'seq', split...  7.72 us
    all_to_all x1, starting transfers between devices, local(): lax.all_to_all(stacked, 'seq', split_axis=0, concat_axis=0, tiled=True)  5.58 us
    ppermute x1, starting transfers between devices, shifted(): return lax.ppermute(block, axis, route)  3.08 us
    pallas_call x1, Pallas kernels, pack(): pl.pallas_call(pack_kernel, out_shape=(jax.ShapeDtypeStruct((blocks, 3, s...  2.85 us
    convert_element_type x1, local copies, waits for them, and re-layouts, attend_columns(): return jnp.einsum('chrs,schd->rchd', weights, value_cols, preferred_eleme...  2.38 us
  transfers between devices with their start and end apart: 3, of which 2 were waited for; matrix products, arithmetic and copies ran while one was open for 11% of the time, Pallas kernels for 10%

profile of v11, /device:TPU:17, one launch (start us, length us, event | category | flops | bytes accessed | tf_op | source)
XLA Modules:
  0.0 83.4 jit_solution(5967061093360518920)
XLA Ops:
  0.0 2.8 %shard_map.37 = (bf16[8,3,128,256]{3,2,1,0:T(8,128)(2,1)}, bf16[2,1024,256]{2,1,0:T(8,128)(2,1)}) custom-call(bf16[2,1024,256]{2,1,0:T(8,128)(2,1)} %q_ref.1, bf16[2,1024,256]{2,1,0:T(8,128)(2,1)} %kp_ref.1, bf16[2,1024,256]{2,1,0:T(8,128)(2,1)} %vp_ref.1, bf16[2,1024,256]{2,1,0:T(8,128)(2,1)} %kp_ref.1, bf16[2,1024,256]{2,1,0:T(8,128)(2,1)} %vp_ref.1), custom_call_target="tpu_custom_call" | custom-call | tf_op jit(solution)/shard_map/pallas_call | solution.py:125
  2.8 5.6 %all-to-all-start = ((bf16[8,3,128,256]{3,2,1,0:T(8,128)(2,1)}), bf16[8,3,128,256]{3,2,1,0:T(8,128)(2,1)S(1)}, u32[]{:S(2)}, u32[]{:S(2)}) async-start(bf16[8,3,128,256]{3,2,1,0:T(8,128)(2,1)} %get-tuple-element.20), calls=%async_computation | async-start | bytes 3145728 | tf_op jit(solution)/shard_map/all_to_all | solution.py:161
  8.4 3.1 %collective-permute-start = (bf16[2,1024,256]{2,1,0:T(8,128)(2,1)}, bf16[2,1024,256]{2,1,0:T(8,128)(2,1)}, u32[]{:S(2)}, u32[]{:S(2)}) collective-permute-start(bf16[2,1024,256]{2,1,0:T(8,128)(2,1)} %get-tuple-element.21), channel_id=1, source_target_pairs={{0,2},{2,4},{4,6},{6,8},{8,10},{10,12},{12,14},{1,3},{3,5},{5,7},{... | collective-permute-start | bytes 3145736 | tf_op jit(solution)/shard_map/ppermute | solution.py:19
  11.5 30.0 %all-to-all-done = bf16[8,3,128,256]{3,2,1,0:T(8,128)(2,1)S(1)} async-done(((bf16[8,3,128,256]{3,2,1,0:T(8,128)(2,1)}), bf16[8,3,128,256]{3,2,1,0:T(8,128)(2,1)S(1)}, u32[]{:S(2)}, u32[]{:S(2)}) %all-to-all-start) | async-done | bytes 1572896 | tf_op jit(solution)/shard_map/all_to_all | solution.py:161
  41.6 0.4 reshape.60
  42.0 1.2 %fusion.11 = (bf16[8,1,128,2,128]{4,3,2,1,0:T(2,128)(2,1)S(1)}, bf16[8,1,128,2,128]{4,3,2,1,0:T(2,128)(2,1)S(1)}, bf16[8,1,128,2,128]{4,3,2,1,0:T(2,128)(2,1)S(1)}) fusion(bf16[8,3,128,2,128]{4,3,2,1,0:T(2,128)(2,1)S(1)} %reshape.60), kind=kLoop, calls=%fused_computation.22 | loop fusion | bytes 3145728 | tf_op jit(solution)/shard_map/slice | solution.py:164
  43.2 0.7 fusion.4
  43.9 0.4 copy.17
  44.3 0.8 fusion.12
  45.1 0.4 copy.18
  45.6 0.0 copy-start.2
  45.6 1.3 %fusion.1 = bf16[8,128,2,128]{3,0,2,1:T(8,128)(2,1)} fusion(bf16[128,2,8,8]{3,2,1,0:T(8,128)(2,1)S(1)} %copy.18, bf16[8,1,128,2,128]{4,3,2,1,0:T(2,128)(2,1)S(1)} %get-tuple-element.23), kind=kOutput, calls=%fused_computation.2 | convolution fusion | flops 4456448 | bytes 1081344 | tf_op jit(solution)/shard_map/chrs,schd->rchd/dot_general | solution.py:36
  46.9 2.4 %copy.19 = bf16[8,128,2,128]{1,3,2,0:T(8,128)(2,1)} copy(bf16[8,128,2,128]{3,0,2,1:T(8,128)(2,1)} %fusion.1) | data formatting | bytes 1048576 | tf_op jit(solution)/shard_map/convert_element_type | solution.py:38
  49.3 7.7 %all-to-all-start.1 = ((bf16[8,128,256]{1,2,0:T(8,128)(2,1)}), bf16[8,128,256]{1,2,0:T(8,128)(2,1)}, u32[]{:S(2)}, u32[]{:S(2)}) async-start(bf16[8,128,256]{1,2,0:T(8,128)(2,1)} %bitcast.25), calls=%async_computation.1 | async-start | bytes 1048576 | tf_op jit(solution)/shard_map/all_to_all | solution.py:165
  57.0 0.0 copy-done.2
  57.0 0.8 %slice_bitcast_fusion.2.refs_0_ = bf16[1024,256]{1,0:T(8,128)(2,1)} fusion(bf16[2,1024,256]{2,1,0:T(8,128)(2,1)S(1)} %copy-done.2), kind=kLoop, calls=%fused_computation.12 | loop fusion | bytes 1048576 | tf_op jit(solution)/shard_map/squeeze | solution.py:170
  57.8 0.0 copy-done
  57.8 0.0 copy-done.1
  57.8 1.1 %slice_bitcast_fusion = (bf16[1024,256]{1,0:T(8,128)(2,1)}, bf16[1024,256]{1,0:T(8,128)(2,1)}) fusion(bf16[2,1024,256]{2,1,0:T(8,128)(2,1)S(1)} %copy-done.1, bf16[2,1024,256]{2,1,0:T(8,128)(2,1)S(1)} %copy-done), kind=kLoop, calls=%fused_computation.10 | loop fusion | bytes 2097152 | tf_op jit(solution)/shard_map/squeeze | solution.py:170
  58.9 14.3 %collective-permute-done.refs_1_.refs_3_ = bf16[2,1024,256]{2,1,0:T(8,128)(2,1)} collective-permute-done((bf16[2,1024,256]{2,1,0:T(8,128)(2,1)}, bf16[2,1024,256]{2,1,0:T(8,128)(2,1)}, u32[]{:S(2)}, u32[]{:S(2)}) %collective-permute-start) | collective-permute-done | bytes 1048608 | tf_op jit(solution)/shard_map/ppermute | solution.py:19
  73.1 8.1 %shard_map.38 = bf16[2,1024,256]{2,1,0:T(8,128)(2,1)} custom-call(s32[1]{0:T(128)} %bitcast.flag_ref, bf16[1024,256]{1,0:T(8,128)(2,1)} %slice_bitcast_fusion.2.refs_0_, bf16[2,1024,256]{2,1,0:T(8,128)(2,1)} %collective-permute-done.refs_1_.refs_3_, bf16[1024,256]{1,0:T(8,128)(2,1)} %get-tuple-element.29.refs_2_, ...), custom_call_target="tpu_custom_call" | custom-call | flops 1610612736 | bytes 3145728 | tf_op jit(solution)/shard_map/pallas_call | solution.py:95
  81.3 0.0 all-to-all-done.1
  81.3 1.2 %copy.20 = bf16[8,128,256]{2,1,0:T(8,128)(2,1)S(1)} copy(bf16[8,128,256]{1,2,0:T(8,128)(2,1)} %all-to-all-done.1) | data formatting | bytes 1048576 | tf_op jit(solution)/shard_map/all_to_all | solution.py:165
  82.5 0.8 bitcast_dynamic-update-slice_fusion
  (4 shorter events, 0.0 us)
Async XLA Ops:
  2.8 38.7 %all-to-all-start = ((bf16[8,3,128,256]{3,2,1,0:T(8,128)(2,1)}), bf16[8,3,128,256]{3,2,1,0:T(8,128)(2,1)S(1)}, u32[]{:S(2)}, u32[]{:S(2)}) async-start(bf16[8,3,128,256]{3,2,1,0:T(8,128)(2,1)} %get-tuple-element.20), calls=%async_computation | async-start | bytes 3145728 | tf_op jit(solution)/shard_map/all_to_all | solution.py:161
  8.4 64.7 %collective-permute-start = (bf16[2,1024,256]{2,1,0:T(8,128)(2,1)}, bf16[2,1024,256]{2,1,0:T(8,128)(2,1)}, u32[]{:S(2)}, u32[]{:S(2)}) collective-permute-start(bf16[2,1024,256]{2,1,0:T(8,128)(2,1)} %get-tuple-element.21), channel_id=1, source_target_pairs={{0,2},{2,4},{4,6},{6,8},{8,10},{10,12},{12,14},{1,3},{3,5},{5,7},{... | collective-permute-start | bytes 3145736 | tf_op jit(solution)/shard_map/ppermute | solution.py:19
  45.6 11.4 %copy-start.2 = (bf16[2,1024,256]{2,1,0:T(8,128)(2,1)S(1)}, bf16[2,1024,256]{2,1,0:T(8,128)(2,1)}, u32[]{:S(2)}) copy-start(bf16[2,1024,256]{2,1,0:T(8,128)(2,1)} %q_ref.1) | copy-start | bytes 3145732
  46.9 10.9 %copy-start = (bf16[2,1024,256]{2,1,0:T(8,128)(2,1)S(1)}, bf16[2,1024,256]{2,1,0:T(8,128)(2,1)}, u32[]{:S(2)}) copy-start(bf16[2,1024,256]{2,1,0:T(8,128)(2,1)} %kp_ref.1) | copy-start | bytes 3145732
  46.9 10.9 %copy-start.1 = (bf16[2,1024,256]{2,1,0:T(8,128)(2,1)S(1)}, bf16[2,1024,256]{2,1,0:T(8,128)(2,1)}, u32[]{:S(2)}) copy-start(bf16[2,1024,256]{2,1,0:T(8,128)(2,1)} %vp_ref.1) | copy-start | bytes 3145732
  49.3 32.0 %all-to-all-start.1 = ((bf16[8,128,256]{1,2,0:T(8,128)(2,1)}), bf16[8,128,256]{1,2,0:T(8,128)(2,1)}, u32[]{:S(2)}, u32[]{:S(2)}) async-start(bf16[8,128,256]{1,2,0:T(8,128)(2,1)} %bitcast.25), calls=%async_computation.1 | async-start | bytes 1048576 | tf_op jit(solution)/shard_map/all_to_all | solution.py:165

commit v12 on v11

--- a/solution.py
+++ b/solution.py
@@ -159,9 +159,9 @@
         )
     prev_pair = shifted(pair, "seq", 1)
     moved = lax.all_to_all(stacked, "seq", split_axis=0, concat_axis=0, tiled=True)
-    _, prev_pair = lax.optimization_barrier((moved, prev_pair))
     grid = moved.reshape(blocks, 3, width, heads_here, DH)
     result = attend_columns(grid[:, 0], grid[:, 1], grid[:, 2])
+    result, prev_pair = lax.optimization_barrier((result, prev_pair))
     context = lax.all_to_all(
         result.reshape(blocks, width, feature_width), "seq", split_axis=0, concat_axis=0, tiled=True
     )

time: 83.8 us -> 92.3 us (1.10)
  the two profiles are of different devices: /device:TPU:17 before, /device:TPU:0 now
where the time goes in v12:
time: 92.3 us; the launch traced here: 91.9 us
  waiting for transfers between devices  39.4 us (43%)
  starting transfers between devices  32 us (35%)
  Pallas kernels  8.83 us (10%)
  local copies, waits for them, and re-layouts  8.8 us (10%)
  matrix products  1.98 us (2%)
    all_to_all x1, waiting for transfers between devices, local(): lax.all_to_all(stacked, 'seq', split_axis=0, concat_axis=0, tiled=True)  32.1 us
    all_to_all x1, starting transfers between devices, local(): lax.all_to_all(result.reshape(blocks, width, feature_width), 'seq', split...  19.9 us
    all_to_all x1, waiting for transfers between devices, local(): lax.all_to_all(result.reshape(blocks, width, feature_width), 'seq', split...  7.27 us
    all_to_all x1, starting transfers between devices, local(): lax.all_to_all(stacked, 'seq', split_axis=0, concat_axis=0, tiled=True)  7.26 us
    pallas_call x1, Pallas kernels, attend_rows(): pl.pallas_call(row_kernel, out_shape=jax.ShapeDtypeStruct((2, tokens, wid...  5.99 us
    ppermute x1, starting transfers between devices, shifted(): return lax.ppermute(block, axis, route)  4.9 us
    pallas_call x1, Pallas kernels, pack(): pl.pallas_call(pack_kernel, out_shape=(jax.ShapeDtypeStruct((blocks, 3, s...  2.84 us
    optimization_barrier x1, local copies, waits for them, and re-layouts, local(): result, prev_pair = lax.optimization_barrier((result, prev_pair))  2.38 us
  transfers between devices with their start and end apart: 3, of which 2 were waited for; matrix products, arithmetic and copies ran while one was open for 8% of the time, Pallas kernels for 7%

profile of v12, /device:TPU:0, one launch (start us, length us, event | category | flops | bytes accessed | tf_op | source)
XLA Modules:
  0.0 91.9 jit_solution(17713823789239617314)
XLA Ops:
  0.0 2.8 %shard_map.37 = (bf16[8,3,128,256]{3,2,1,0:T(8,128)(2,1)}, bf16[2,1024,256]{2,1,0:T(8,128)(2,1)}) custom-call(bf16[2,1024,256]{2,1,0:T(8,128)(2,1)} %q_ref.1, bf16[2,1024,256]{2,1,0:T(8,128)(2,1)} %kp_ref.1, bf16[2,1024,256]{2,1,0:T(8,128)(2,1)} %vp_ref.1, bf16[2,1024,256]{2,1,0:T(8,128)(2,1)} %kp_ref.1, bf16[2,1024,256]{2,1,0:T(8,128)(2,1)} %vp_ref.1), custom_call_target="tpu_custom_call" | custom-call | tf_op jit(solution)/shard_map/pallas_call | solution.py:125
  2.8 7.3 %all-to-all-start = ((bf16[8,3,128,256]{3,2,1,0:T(8,128)(2,1)}), bf16[8,3,128,256]{3,2,1,0:T(8,128)(2,1)S(1)}, u32[]{:S(2)}, u32[]{:S(2)}) async-start(bf16[8,3,128,256]{3,2,1,0:T(8,128)(2,1)} %get-tuple-element.21), calls=%async_computation | async-start | bytes 3145728 | tf_op jit(solution)/shard_map/all_to_all | solution.py:161
  10.1 4.9 %collective-permute-start = (bf16[2,1024,256]{2,1,0:T(8,128)(2,1)}, bf16[2,1024,256]{2,1,0:T(8,128)(2,1)}, u32[]{:S(2)}, u32[]{:S(2)}) collective-permute-start(bf16[2,1024,256]{2,1,0:T(8,128)(2,1)} %get-tuple-element.22), channel_id=1, source_target_pairs={{0,2},{2,4},{4,6},{6,8},{8,10},{10,12},{12,14},{1,3},{3,5},{5,7},{... | collective-permute-start | bytes 3145736 | tf_op jit(solution)/shard_map/ppermute | solution.py:19
  15.0 32.1 %all-to-all-done = bf16[8,3,128,256]{3,2,1,0:T(8,128)(2,1)S(1)} async-done(((bf16[8,3,128,256]{3,2,1,0:T(8,128)(2,1)}), bf16[8,3,128,256]{3,2,1,0:T(8,128)(2,1)S(1)}, u32[]{:S(2)}, u32[]{:S(2)}) %all-to-all-start) | async-done | bytes 1572896 | tf_op jit(solution)/shard_map/all_to_all | solution.py:161
  47.1 0.4 reshape.60
  47.6 1.2 %fusion.11 = (bf16[8,1,128,2,128]{4,3,2,1,0:T(2,128)(2,1)S(1)}, bf16[8,1,128,2,128]{4,3,2,1,0:T(2,128)(2,1)S(1)}, bf16[8,1,128,2,128]{4,3,2,1,0:T(2,128)(2,1)S(1)}) fusion(bf16[8,3,128,2,128]{4,3,2,1,0:T(2,128)(2,1)S(1)} %reshape.60), kind=kLoop, calls=%fused_computation.22 | loop fusion | bytes 3145728 | tf_op jit(solution)/shard_map/slice | solution.py:163
  48.7 0.7 fusion.4
  49.4 0.4 copy.17
  49.9 0.8 fusion.12
  50.7 0.4 copy.18
  51.2 0.0 copy-start.2
  51.2 1.3 %fusion.1 = bf16[8,128,2,128]{3,0,2,1:T(8,128)(2,1)} fusion(bf16[128,2,8,8]{3,2,1,0:T(8,128)(2,1)S(1)} %copy.18, bf16[8,1,128,2,128]{4,3,2,1,0:T(2,128)(2,1)S(1)} %get-tuple-element.25), kind=kOutput, calls=%fused_computation.2 | convolution fusion | flops 4456448 | bytes 1081344 | tf_op jit(solution)/shard_map/chrs,schd->rchd/dot_general | solution.py:36
  52.5 0.0 collective-permute-done.refs_1_.refs_3_
  52.5 2.4 %copy.19 = bf16[8,128,2,128]{1,3,2,0:T(8,128)(2,1)} copy(bf16[8,128,2,128]{3,0,2,1:T(8,128)(2,1)} %fusion.1) | data formatting | bytes 1048576 | tf_op jit(solution)/shard_map/optimization_barrier | solution.py:164
  54.8 19.9 %all-to-all-start.1 = ((bf16[8,128,256]{1,2,0:T(8,128)(2,1)}), bf16[8,128,256]{1,2,0:T(8,128)(2,1)}, u32[]{:S(2)}, u32[]{:S(2)}) async-start(bf16[8,128,256]{1,2,0:T(8,128)(2,1)} %bitcast.25), calls=%async_computation.1 | async-start | bytes 1048576 | tf_op jit(solution)/shard_map/all_to_all | solution.py:165
  74.7 0.0 copy-done.2
  74.7 0.8 slice_bitcast_fusion.2.refs_0_
  75.5 0.0 copy-done
  75.5 0.0 copy-done.1
  75.5 1.1 %slice_bitcast_fusion = (bf16[1024,256]{1,0:T(8,128)(2,1)}, bf16[1024,256]{1,0:T(8,128)(2,1)}) fusion(bf16[2,1024,256]{2,1,0:T(8,128)(2,1)S(1)} %copy-done.1, bf16[2,1024,256]{2,1,0:T(8,128)(2,1)S(1)} %copy-done), kind=kLoop, calls=%fused_computation.10 | loop fusion | bytes 2097152 | tf_op jit(solution)/shard_map/squeeze | solution.py:170
  76.6 6.0 %shard_map.38 = bf16[2,1024,256]{2,1,0:T(8,128)(2,1)} custom-call(s32[1]{0:T(128)} %bitcast.flag_ref, bf16[1024,256]{1,0:T(8,128)(2,1)} %slice_bitcast_fusion.2.refs_0_, bf16[2,1024,256]{2,1,0:T(8,128)(2,1)} %collective-permute-done.refs_1_.refs_3_, bf16[1024,256]{1,0:T(8,128)(2,1)} %get-tuple-element.31.refs_2_, ...), custom_call_target="tpu_custom_call" | custom-call | flops 1610612736 | bytes 3145728 | tf_op jit(solution)/shard_map/pallas_call | solution.py:95
  82.6 7.3 %all-to-all-done.1 = bf16[8,128,256]{1,2,0:T(8,128)(2,1)} async-done(((bf16[8,128,256]{1,2,0:T(8,128)(2,1)}), bf16[8,128,256]{1,2,0:T(8,128)(2,1)}, u32[]{:S(2)}, u32[]{:S(2)}) %all-to-all-start.1) | async-done | bytes 524320 | tf_op jit(solution)/shard_map/all_to_all | solution.py:165
  89.9 1.2 %copy.20 = bf16[8,128,256]{2,1,0:T(8,128)(2,1)S(1)} copy(bf16[8,128,256]{1,2,0:T(8,128)(2,1)} %all-to-all-done.1) | data formatting | bytes 1048576 | tf_op jit(solution)/shard_map/all_to_all | solution.py:165
  91.1 0.8 bitcast_dynamic-update-slice_fusion
  (4 shorter events, 0.0 us)
Async XLA Ops:
  2.8 44.3 %all-to-all-start = ((bf16[8,3,128,256]{3,2,1,0:T(8,128)(2,1)}), bf16[8,3,128,256]{3,2,1,0:T(8,128)(2,1)S(1)}, u32[]{:S(2)}, u32[]{:S(2)}) async-start(bf16[8,3,128,256]{3,2,1,0:T(8,128)(2,1)} %get-tuple-element.21), calls=%async_computation | async-start | bytes 3145728 | tf_op jit(solution)/shard_map/all_to_all | solution.py:161
  10.1 42.4 %collective-permute-start = (bf16[2,1024,256]{2,1,0:T(8,128)(2,1)}, bf16[2,1024,256]{2,1,0:T(8,128)(2,1)}, u32[]{:S(2)}, u32[]{:S(2)}) collective-permute-start(bf16[2,1024,256]{2,1,0:T(8,128)(2,1)} %get-tuple-element.22), channel_id=1, source_target_pairs={{0,2},{2,4},{4,6},{6,8},{8,10},{10,12},{12,14},{1,3},{3,5},{5,7},{... | collective-permute-start | bytes 3145736 | tf_op jit(solution)/shard_map/ppermute | solution.py:19
  51.2 23.5 %copy-start.2 = (bf16[2,1024,256]{2,1,0:T(8,128)(2,1)S(1)}, bf16[2,1024,256]{2,1,0:T(8,128)(2,1)}, u32[]{:S(2)}) copy-start(bf16[2,1024,256]{2,1,0:T(8,128)(2,1)} %q_ref.1) | copy-start | bytes 3145732
  52.5 23.1 %copy-start = (bf16[2,1024,256]{2,1,0:T(8,128)(2,1)S(1)}, bf16[2,1024,256]{2,1,0:T(8,128)(2,1)}, u32[]{:S(2)}) copy-start(bf16[2,1024,256]{2,1,0:T(8,128)(2,1)} %kp_ref.1) | copy-start | bytes 3145732
  52.5 23.1 %copy-start.1 = (bf16[2,1024,256]{2,1,0:T(8,128)(2,1)S(1)}, bf16[2,1024,256]{2,1,0:T(8,128)(2,1)}, u32[]{:S(2)}) copy-start(bf16[2,1024,256]{2,1,0:T(8,128)(2,1)} %vp_ref.1) | copy-start | bytes 3145732
  54.8 35.0 %all-to-all-start.1 = ((bf16[8,128,256]{1,2,0:T(8,128)(2,1)}), bf16[8,128,256]{1,2,0:T(8,128)(2,1)}, u32[]{:S(2)}, u32[]{:S(2)}) async-start(bf16[8,128,256]{1,2,0:T(8,128)(2,1)} %bitcast.25), calls=%async_computation.1 | async-start | bytes 1048576 | tf_op jit(solution)/shard_map/all_to_all | solution.py:165

commit v13 on v12

--- a/solution.py
+++ b/solution.py
@@ -38,7 +38,7 @@
     ).astype(jnp.bfloat16)
 
 
-def row_tiles(with_prev, q_ref, kp_ref, kc_ref, vp_ref, vc_ref, o_ref):
+def row_part(first_tile, with_prev, q_ref, kc_ref, vc_ref, prev_refs, o_ref):
     score_scale = 1.0 / math.sqrt(DH)
     dims = (((1,), (1,)), ((), ()))
     tq = QUERY_TILE
@@ -46,20 +46,27 @@
         jnp.int32, (tq, tq), 0
     )
 
-    def scores(q, k_ref, low, high):
-        return lax.dot_general(q, k_ref[low:high, :], dims, preferred_element_type=jnp.float32)
-
-    for tile in range(STRIDE // tq):
-        low, high = tile * tq, (tile + 1) * tq
-        q = q_ref[low:high, :]
+    def scores(q, k):
+        return lax.dot_general(q, k, dims, preferred_element_type=jnp.float32)
+
+    for local_tile in range(q_ref.shape[0] // tq):
+        low = (first_tile + local_tile) * tq
+        high = low + tq
+        q = q_ref[local_tile * tq : (local_tile + 1) * tq, :]
         parts = []
         if with_prev:
-            parts.append((jnp.where(upper, scores(q, kp_ref, low, high), -jnp.inf), vp_ref, low, high))
-            if high < STRIDE:
-                parts.append((scores(q, kp_ref, high, STRIDE), vp_ref, high, STRIDE))
+            for k_ref, v_ref, start in prev_refs:
+                end = start + k_ref.shape[0]
+                if start <= low < end:
+                    a, b = low - start, high - start
+                    parts.append((jnp.where(upper, scores(q, k_ref[a:b, :]), -jnp.inf), v_ref[a:b, :]))
+                    if b < end - start:
+                        parts.append((scores(q, k_ref[b:, :]), v_ref[b:, :]))
+                elif start >= high:
+                    parts.append((scores(q, k_ref[...]), v_ref[...]))
         if low > 0:
-            parts.append((scores(q, kc_ref, 0, low), vc_ref, 0, low))
-        parts.append((jnp.where(upper, -jnp.inf, scores(q, kc_ref, low, high)), vc_ref, low, high))
+            parts.append((scores(q, kc_ref[:low, :]), vc_ref[:low, :]))
+        parts.append((jnp.where(upper, -jnp.inf, scores(q, kc_ref[low:high, :])), vc_ref[low:high, :]))
         maxima = functools.reduce(
             jnp.maximum, [jnp.max(p[0], axis=1, keepdims=True) for p in parts]
         )
@@ -67,44 +74,62 @@
         total = functools.reduce(jnp.add, [jnp.sum(e, axis=1, keepdims=True) for e in expos])
         inverse = 1.0 / total
         out = None
-        for e, (_, v_ref, a, b) in zip(expos, parts):
-            term = jnp.dot((e * inverse).astype(jnp.bfloat16), v_ref[a:b, :], preferred_element_type=jnp.float32)
+        for e, (_, v) in zip(expos, parts):
+            term = jnp.dot((e * inverse).astype(jnp.bfloat16), v, preferred_element_type=jnp.float32)
             out = term if out is None else out + term
-        o_ref[low:high, :] = out.astype(o_ref.dtype)
-
-
-def row_kernel(flag_ref, *refs):
+        o_ref[local_tile * tq : (local_tile + 1) * tq, :] = out.astype(o_ref.dtype)
+
+
+def row_kernel(first_tile, starts, flag_ref, q_ref, kc_ref, vc_ref, *refs):
+    prev_refs = [(refs[2 * i], refs[2 * i + 1], start) for i, start in enumerate(starts)]
+    o_ref = refs[-1]
     has_prev = flag_ref[0] > 0
 
     @pl.when(has_prev)
     def _():
-        row_tiles(True, *refs)
+        row_part(first_tile, True, q_ref, kc_ref, vc_ref, prev_refs, o_ref)
 
     @pl.when(jnp.logical_not(has_prev))
     def _():
-        row_tiles(False, *refs)
-
-
-def attend_rows(has_prev, queries, prev_pair, keys, values):
+        row_part(first_tile, False, q_ref, kc_ref, vc_ref, prev_refs, o_ref)
+
+
+def attend_rows(has_prev, half, queries, keys, values, prev_halves, buffer=None):
     tokens, width = queries.shape
     heads = width // DH
-    spec = pl.BlockSpec((STRIDE, DH), lambda h, flag: (0, h))
-    prev_key_spec = pl.BlockSpec((None, STRIDE, DH), lambda h, flag: (0, 0, h))
-    prev_value_spec = pl.BlockSpec((None, STRIDE, DH), lambda h, flag: (1, 0, h))
-    scores = heads * tokens * (STRIDE + QUERY_TILE)
+    rows = tokens // 2
+    q_spec = pl.BlockSpec((rows, DH), lambda h, flag: (half, h))
+    kv_spec = pl.BlockSpec((rows * (half + 1), DH), lambda h, flag: (0, h))
+    key_spec = pl.BlockSpec((None, rows, DH), lambda h, flag: (0, 0, h))
+    value_spec = pl.BlockSpec((None, rows, DH), lambda h, flag: (1, 0, h))
+    prev_specs, prev_args, starts = [], [], []
+    for start, chunk in prev_halves:
+        prev_specs += [key_spec, value_spec]
+        prev_args += [chunk, chunk]
+        starts.append(start)
+    in_specs = [q_spec, kv_spec, kv_spec] + prev_specs
+    args = [has_prev, queries, keys, values] + prev_args
+    aliases = {}
+    if buffer is not None:
+        in_specs.append(pl.BlockSpec(memory_space=pl.ANY))
+        aliases = {len(args): 0}
+        args.append(buffer)
+    first_tile = half * (rows // QUERY_TILE)
+    scores = heads * rows * (STRIDE + QUERY_TILE)
     return pl.pallas_call(
-        row_kernel,
+        functools.partial(row_kernel, first_tile, tuple(starts)),
         out_shape=jax.ShapeDtypeStruct((2, tokens, width), jnp.bfloat16),
         grid_spec=pltpu.PrefetchScalarGridSpec(
             num_scalar_prefetch=1,
             grid=(heads,),
-            in_specs=[spec, prev_key_spec, spec, prev_value_spec, spec],
-            out_specs=prev_key_spec,
-        ),
+            in_specs=in_specs,
+            out_specs=pl.BlockSpec((None, rows, DH), lambda h, flag: (0, half, h)),
+        ),
+        input_output_aliases=aliases,
         cost_estimate=pl.CostEstimate(
-            flops=4 * scores * DH, transcendentals=scores, bytes_accessed=6 * tokens * width * 2
-        ),
-    )(has_prev, queries, prev_pair, keys, prev_pair, values)
+            flops=4 * scores * DH, transcendentals=scores, bytes_accessed=4 * rows * width * 2
+        ),
+    )(*args)
 
 
 def pack_kernel(q_ref, k_ref, v_ref, kp_ref, vp_ref, o_ref, pair_ref):
@@ -126,13 +151,13 @@
         pack_kernel,
         out_shape=(
             jax.ShapeDtypeStruct((blocks, 3, size, width), query_vectors.dtype),
-            jax.ShapeDtypeStruct((2, tokens, width), query_vectors.dtype),
+            jax.ShapeDtypeStruct((steps, 2, rows, width), query_vectors.dtype),
         ),
         grid=(steps,),
         in_specs=[column, column, column, row, row],
         out_specs=(
             pl.BlockSpec((blocks // steps, 3, size, width), lambda b: (b, 0, 0, 0)),
-            pl.BlockSpec((2, rows, width), lambda b: (0, b, 0)),
+            pl.BlockSpec((None, 2, rows, width), lambda b: (b, 0, 0, 0)),
         ),
     )(query_vectors, key_vectors, value_vectors, key_vectors, value_vectors)
 
@@ -145,10 +170,12 @@
     blocks = lax.axis_size("seq")
     width = STRIDE // blocks
     seq_index = lax.axis_index("seq")
+    half_rows = STRIDE // 2
     if width % 16 == 0:
         stacked, pair = pack(query_vectors, key_vectors, value_vectors, blocks)
     else:
-        pair = jnp.stack([key_vectors[0], value_vectors[0]])
+        pair = jnp.stack([key_vectors[0], value_vectors[0]]).reshape(2, 2, half_rows, feature_width)
+        pair = jnp.moveaxis(pair, 1, 0)
         stacked = jnp.stack(
             [
                 query_vectors[1].reshape(blocks, width, feature_width),
@@ -157,17 +184,30 @@
             ],
             axis=1,
         )
-    prev_pair = shifted(pair, "seq", 1)
+    forward = [(i, i + 1) for i in range(blocks - 1)]
+    prev_high = lax.ppermute(pair[1], "seq", forward)
+    prev_low = lax.ppermute(pair[0], "seq", forward)
     moved = lax.all_to_all(stacked, "seq", split_axis=0, concat_axis=0, tiled=True)
+    moved, prev_high = lax.optimization_barrier((moved, prev_high))
     grid = moved.reshape(blocks, 3, width, heads_here, DH)
     result = attend_columns(grid[:, 0], grid[:, 1], grid[:, 2])
-    result, prev_pair = lax.optimization_barrier((result, prev_pair))
     context = lax.all_to_all(
         result.reshape(blocks, width, feature_width), "seq", split_axis=0, concat_axis=0, tiled=True
     )
     column_out = context.reshape(local_tokens, feature_width)
     has_prev = (seq_index > 0).astype(jnp.int32).reshape(1)
-    both = attend_rows(has_prev, query_vectors[0], prev_pair, key_vectors[0], value_vectors[0])
+    both = attend_rows(
+        has_prev, 1, query_vectors[0], key_vectors[0], value_vectors[0], [(half_rows, prev_high)]
+    )
+    both = attend_rows(
+        has_prev,
+        0,
+        query_vectors[0],
+        key_vectors[0],
+        value_vectors[0],
+        [(0, prev_low), (half_rows, prev_high)],
+        both,
+    )
     return both.at[1].set(column_out)
 
 

time: 92.3 us -> 104 us (1.13)
  the two profiles are of different devices: /device:TPU:0 before, /device:TPU:17 now
where the time goes in v13:
time: 104 us
  waiting for transfers between devices  57.6 us (55%)
  starting transfers between devices  15.5 us (15%)
  Pallas kernels  15.1 us (15%)
  local copies, waits for them, and re-layouts  12.8 us (12%)
  matrix products  1.97 us (2%)
    ppermute x1, waiting for transfers between devices, local(): prev_high = lax.ppermute(pair[1], 'seq', forward)  43.6 us
    ppermute x1, waiting for transfers between devices, local(): prev_low = lax.ppermute(pair[0], 'seq', forward)  14 us
    pallas_call x2, Pallas kernels, attend_rows(): pl.pallas_call(functools.partial(row_kernel, first_tile, tuple(starts)),...  12.2 us
    all_to_all x1, starting transfers between devices, local(): lax.all_to_all(stacked, 'seq', split_axis=0, concat_axis=0, tiled=True)  5.71 us
    all_to_all x1, starting transfers between devices, local(): lax.all_to_all(result.reshape(blocks, width, feature_width), 'seq', split...  4.1 us
    ppermute x1, starting transfers between devices, local(): prev_high = lax.ppermute(pair[1], 'seq', forward)  3.08 us
    pallas_call x1, Pallas kernels, pack(): pl.pallas_call(pack_kernel, out_shape=(jax.ShapeDtypeStruct((blocks, 3, s...  2.85 us
    slice x1, local copies, waits for them, and re-layouts, local(): result = attend_columns(grid[:, 0], grid[:, 1], grid[:, 2])  2.67 us
  transfers between devices with their start and end apart: 4, of which 2 were waited for; matrix products, arithmetic and copies ran while one was open for 3% of the time, Pallas kernels for 12%

profile of v13, /device:TPU:17, one launch (start us, length us, event | category | flops | bytes accessed | tf_op | source)
XLA Modules:
  0.0 103.9 jit_solution(17295711978571802867)
XLA Ops:
  0.0 2.8 %shard_map.37 = (bf16[8,3,128,256]{3,2,1,0:T(8,128)(2,1)}, bf16[2,2,512,256]{3,2,1,0:T(8,128)(2,1)}) custom-call(bf16[2,1024,256]{2,1,0:T(8,128)(2,1)} %q_ref.1, bf16[2,1024,256]{2,1,0:T(8,128)(2,1)} %kp_ref.1, bf16[2,1024,256]{2,1,0:T(8,128)(2,1)} %vp_ref.1, bf16[2,1024,256]{2,1,0:T(8,128)(2,1)} %kp_ref.1, bf16[2,1024,256]{2,1,0:T(8,128)(2,1)} %vp_ref.1), custom_call_target="tpu_custom_call" | custom-call | tf_op jit(solution)/shard_map/pallas_call | solution.py:150
  2.9 5.7 %all-to-all-start = ((bf16[8,3,128,256]{3,2,1,0:T(8,128)(2,1)}), bf16[8,3,128,256]{3,2,1,0:T(8,128)(2,1)S(1)}, u32[]{:S(2)}, u32[]{:S(2)}) async-start(bf16[8,3,128,256]{3,2,1,0:T(8,128)(2,1)} %get-tuple-element.22), calls=%async_computation | async-start | bytes 3145728 | tf_op jit(solution)/shard_map/all_to_all | solution.py:190
  8.6 0.9 slice_bitcast_fusion
  9.4 3.1 %collective-permute-start.1 = (bf16[2,512,256]{2,1,0:T(8,128)(2,1)S(1)}, bf16[2,512,256]{2,1,0:T(8,128)(2,1)S(1)}, u32[]{:S(2)}, u32[]{:S(2)}) collective-permute-start(bf16[2,512,256]{2,1,0:T(8,128)(2,1)S(1)} %get-tuple-element.28), channel_id=1, source_target_pairs={{0,2},{2,4},{4,6},{6,8},{8,10},{10,12},{12,14},{1,3},{3,5},{5,7},{... | collective-permute-start | bytes 1572872 | tf_op jit(solution)/shard_map/ppermute | solution.py:188
  12.5 43.6 %collective-permute-done.1.refs_0_.refs_1_.refs_2_.refs_3_ = bf16[2,512,256]{2,1,0:T(8,128)(2,1)S(1)} collective-permute-done((bf16[2,512,256]{2,1,0:T(8,128)(2,1)S(1)}, bf16[2,512,256]{2,1,0:T(8,128)(2,1)S(1)}, u32[]{:S(2)}, u32[]{:S(2)}) %collective-permute-start.1) | collective-permute-done | bytes 524320 | tf_op jit(solution)/shard_map/ppermute | solution.py:188
  56.1 2.0 %reshape.60 = bf16[8,3,128,2,128]{4,3,2,1,0:T(2,128)(2,1)} reshape(bf16[8,3,128,256]{3,2,1,0:T(8,128)(2,1)S(1)} %all-to-all-done) | data formatting | bytes 3145728 | tf_op jit(solution)/shard_map/reshape | solution.py:192
  58.1 2.7 %fusion.11 = (bf16[8,1,128,2,128]{4,3,2,1,0:T(2,128)(2,1)S(1)}, bf16[8,1,128,2,128]{4,3,2,1,0:T(2,128)(2,1)S(1)}, bf16[8,1,128,2,128]{4,3,2,1,0:T(2,128)(2,1)S(1)}) fusion(bf16[8,3,128,2,128]{4,3,2,1,0:T(2,128)(2,1)} %reshape.60), kind=kLoop, calls=%fused_computation.24 | loop fusion | bytes 3145728 | tf_op jit(solution)/shard_map/slice | solution.py:193
  60.8 0.7 fusion.4
  61.5 0.4 copy.18
  61.9 0.8 fusion.12
  62.8 0.4 copy.19
  63.2 0.0 copy-start.3
  63.2 1.3 %fusion.1 = bf16[8,128,2,128]{3,0,2,1:T(8,128)(2,1)} fusion(bf16[128,2,8,8]{3,2,1,0:T(8,128)(2,1)S(1)} %copy.19, bf16[8,1,128,2,128]{4,3,2,1,0:T(2,128)(2,1)S(1)} %get-tuple-element.25), kind=kOutput, calls=%fused_computation.2 | convolution fusion | flops 4456448 | bytes 1081344 | tf_op jit(solution)/shard_map/chrs,schd->rchd/dot_general | solution.py:36
  64.5 2.4 %copy.20 = bf16[8,128,2,128]{1,3,2,0:T(8,128)(2,1)} copy(bf16[8,128,2,128]{3,0,2,1:T(8,128)(2,1)} %fusion.1) | data formatting | bytes 1048576 | tf_op jit(solution)/shard_map/convert_element_type | solution.py:38
  66.9 4.1 %all-to-all-start.1 = ((bf16[8,128,256]{1,2,0:T(8,128)(2,1)}), bf16[8,128,256]{1,2,0:T(8,128)(2,1)}, u32[]{:S(2)}, u32[]{:S(2)}) async-start(bf16[8,128,256]{1,2,0:T(8,128)(2,1)} %bitcast.29), calls=%async_computation.1 | async-start | bytes 1048576 | tf_op jit(solution)/shard_map/all_to_all | solution.py:194
  71.0 2.6 %collective-permute-start = (bf16[2,512,256]{2,1,0:T(8,128)(2,1)}, bf16[2,512,256]{2,1,0:T(8,128)(2,1)}, u32[]{:S(2)}, u32[]{:S(2)}) collective-permute-start(bf16[2,512,256]{2,1,0:T(8,128)(2,1)} %get-tuple-element.29), channel_id=1, source_target_pairs={{0,2},{2,4},{4,6},{6,8},{8,10},{10,12},{12,14},{1,3},{3,5},{5,7},{... | collective-permute-start | bytes 1572872 | tf_op jit(solution)/shard_map/ppermute | solution.py:189
  73.6 0.9 slice_bitcast_fusion.4.q_ref
  74.5 1.1 %slice_bitcast_fusion.2 = (bf16[1024,256]{1,0:T(8,128)(2,1)}, bf16[1024,256]{1,0:T(8,128)(2,1)}) fusion(bf16[2,1024,256]{2,1,0:T(8,128)(2,1)S(1)} %copy-done.1, bf16[2,1024,256]{2,1,0:T(8,128)(2,1)S(1)} %copy-done.2), kind=kLoop, calls=%fused_computation.12 | loop fusion | bytes 2097152 | tf_op jit(solution)/shard_map/squeeze | solution.py:207
  75.6 6.1 %shard_map.38.refs_4_ = bf16[2,1024,256]{2,1,0:T(8,128)(2,1)} custom-call(s32[1]{0:T(128)} %bitcast.flag_ref, bf16[1024,256]{1,0:T(8,128)(2,1)} %slice_bitcast_fusion.4.q_ref, bf16[1024,256]{1,0:T(8,128)(2,1)} %get-tuple-element.33.kc_ref, bf16[1024,256]{1,0:T(8,128)(2,1)} %get-tuple-element.32.vc_ref, bf16[2,512,256]{2,1,0:T(8,128)(2,1)} %copy-done, ...), custom_call_target="tpu_custom_call" | custom-call | flops 805306368 | bytes 1048576 | tf_op jit(solution)/shard_map/pallas_call | solution.py:119
  81.6 14.0 %collective-permute-done.refs_0_.refs_1_ = bf16[2,512,256]{2,1,0:T(8,128)(2,1)} collective-permute-done((bf16[2,512,256]{2,1,0:T(8,128)(2,1)}, bf16[2,512,256]{2,1,0:T(8,128)(2,1)}, u32[]{:S(2)}, u32[]{:S(2)}) %collective-permute-start) | collective-permute-done | bytes 524320 | tf_op jit(solution)/shard_map/ppermute | solution.py:189
  95.7 6.2 %shard_map.39 = bf16[2,1024,256]{2,1,0:T(8,128)(2,1)} custom-call(s32[1]{0:T(128)} %bitcast.flag_ref, bf16[1024,256]{1,0:T(8,128)(2,1)} %slice_bitcast_fusion.4.q_ref, bf16[1024,256]{1,0:T(8,128)(2,1)} %get-tuple-element.33.kc_ref, bf16[1024,256]{1,0:T(8,128)(2,1)} %get-tuple-element.32.vc_ref, ...), custom_call_target="tpu_custom_call", output_to_operand_aliasing={{}: (8, {})} | custom-call | flops 805306368 | bytes 1048576 | tf_op jit(solution)/shard_map/pallas_call | solution.py:119
  101.8 0.0 all-to-all-done.1
  101.8 1.2 %copy.21 = bf16[8,128,256]{2,1,0:T(8,128)(2,1)S(1)} copy(bf16[8,128,256]{1,2,0:T(8,128)(2,1)} %all-to-all-done.1) | data formatting | bytes 1048576 | tf_op jit(solution)/shard_map/all_to_all | solution.py:194
  103.1 0.8 bitcast_dynamic-update-slice_fusion
  (12 shorter events, 0.0 us)
Async XLA Ops:
  2.8 5.7 %copy-start.4 = (bf16[2,2,512,256]{3,2,1,0:T(8,128)(2,1)S(1)}, bf16[2,2,512,256]{3,2,1,0:T(8,128)(2,1)}, u32[]{:S(2)}) copy-start(bf16[2,2,512,256]{3,2,1,0:T(8,128)(2,1)} %get-tuple-element.21) | copy-start | bytes 3145732
  2.9 53.3 %all-to-all-start = ((bf16[8,3,128,256]{3,2,1,0:T(8,128)(2,1)}), bf16[8,3,128,256]{3,2,1,0:T(8,128)(2,1)S(1)}, u32[]{:S(2)}, u32[]{:S(2)}) async-start(bf16[8,3,128,256]{3,2,1,0:T(8,128)(2,1)} %get-tuple-element.22), calls=%async_computation | async-start | bytes 3145728 | tf_op jit(solution)/shard_map/all_to_all | solution.py:190
  9.4 46.7 %collective-permute-start.1 = (bf16[2,512,256]{2,1,0:T(8,128)(2,1)S(1)}, bf16[2,512,256]{2,1,0:T(8,128)(2,1)S(1)}, u32[]{:S(2)}, u32[]{:S(2)}) collective-permute-start(bf16[2,512,256]{2,1,0:T(8,128)(2,1)S(1)} %get-tuple-element.28), channel_id=1, source_target_pairs={{0,2},{2,4},{4,6},{6,8},{8,10},{10,12},{12,14},{1,3},{3,5},{5,7},{... | collective-permute-start | bytes 1572872 | tf_op jit(solution)/shard_map/ppermute | solution.py:188
  56.1 2.0 %copy-start = (bf16[2,512,256]{2,1,0:T(8,128)(2,1)}, bf16[2,512,256]{2,1,0:T(8,128)(2,1)S(1)}, u32[]{:S(2)}) copy-start(bf16[2,512,256]{2,1,0:T(8,128)(2,1)S(1)} %collective-permute-done.1.refs_0_.refs_1_.refs_2_.refs_3_) | copy-start | bytes 1572868
  63.2 10.4 %copy-start.3 = (bf16[2,1024,256]{2,1,0:T(8,128)(2,1)S(1)}, bf16[2,1024,256]{2,1,0:T(8,128)(2,1)}, u32[]{:S(2)}) copy-start(bf16[2,1024,256]{2,1,0:T(8,128)(2,1)} %q_ref.1) | copy-start | bytes 3145732
  64.5 10.0 %copy-start.1 = (bf16[2,1024,256]{2,1,0:T(8,128)(2,1)S(1)}, bf16[2,1024,256]{2,1,0:T(8,128)(2,1)}, u32[]{:S(2)}) copy-start(bf16[2,1024,256]{2,1,0:T(8,128)(2,1)} %vp_ref.1) | copy-start | bytes 3145732
  64.5 10.0 %copy-start.2 = (bf16[2,1024,256]{2,1,0:T(8,128)(2,1)S(1)}, bf16[2,1024,256]{2,1,0:T(8,128)(2,1)}, u32[]{:S(2)}) copy-start(bf16[2,1024,256]{2,1,0:T(8,128)(2,1)} %kp_ref.1) | copy-start | bytes 3145732
  66.9 35.0 %all-to-all-start.1 = ((bf16[8,128,256]{1,2,0:T(8,128)(2,1)}), bf16[8,128,256]{1,2,0:T(8,128)(2,1)}, u32[]{:S(2)}, u32[]{:S(2)}) async-start(bf16[8,128,256]{1,2,0:T(8,128)(2,1)} %bitcast.29), calls=%async_computation.1 | async-start | bytes 1048576 | tf_op jit(solution)/shard_map/all_to_all | solution.py:194
  71.0 24.7 %collective-permute-start = (bf16[2,512,256]{2,1,0:T(8,128)(2,1)}, bf16[2,512,256]{2,1,0:T(8,128)(2,1)}, u32[]{:S(2)}, u32[]{:S(2)}) collective-permute-start(bf16[2,512,256]{2,1,0:T(8,128)(2,1)} %get-tuple-element.29), channel_id=1, source_target_pairs={{0,2},{2,4},{4,6},{6,8},{8,10},{10,12},{12,14},{1,3},{3,5},{5,7},{... | collective-permute-start | bytes 1572872 | tf_op jit(solution)/shard_map/ppermute | solution.py:189

commit v14 on v11

--- a/solution.py
+++ b/solution.py
@@ -49,6 +49,9 @@
     def scores(q, k_ref, low, high):
         return lax.dot_general(q, k_ref[low:high, :], dims, preferred_element_type=jnp.float32)
 
+    def scores_t(q, kt_ref, low, high):
+        return jnp.dot(q, kt_ref[:, low:high], preferred_element_type=jnp.float32)
+
     for tile in range(STRIDE // tq):
         low, high = tile * tq, (tile + 1) * tq
         q = q_ref[low:high, :]
@@ -58,8 +61,8 @@
             if high < STRIDE:
                 parts.append((scores(q, kp_ref, high, STRIDE), vp_ref, high, STRIDE))
         if low > 0:
-            parts.append((scores(q, kc_ref, 0, low), vc_ref, 0, low))
-        parts.append((jnp.where(upper, -jnp.inf, scores(q, kc_ref, low, high)), vc_ref, low, high))
+            parts.append((scores_t(q, kc_ref, 0, low), vc_ref, 0, low))
+        parts.append((jnp.where(upper, -jnp.inf, scores_t(q, kc_ref, low, high)), vc_ref, low, high))
         maxima = functools.reduce(
             jnp.maximum, [jnp.max(p[0], axis=1, keepdims=True) for p in parts]
         )
@@ -91,6 +94,7 @@
     spec = pl.BlockSpec((STRIDE, DH), lambda h, flag: (0, h))
     prev_key_spec = pl.BlockSpec((None, STRIDE, DH), lambda h, flag: (0, 0, h))
     prev_value_spec = pl.BlockSpec((None, STRIDE, DH), lambda h, flag: (1, 0, h))
+    key_t_spec = pl.BlockSpec((DH, STRIDE), lambda h, flag: (h, 0))
     scores = heads * tokens * (STRIDE + QUERY_TILE)
     return pl.pallas_call(
         row_kernel,
@@ -98,7 +102,7 @@
         grid_spec=pltpu.PrefetchScalarGridSpec(
             num_scalar_prefetch=1,
             grid=(heads,),
-            in_specs=[spec, prev_key_spec, spec, prev_value_spec, spec],
+            in_specs=[spec, prev_key_spec, key_t_spec, prev_value_spec, spec],
             out_specs=prev_key_spec,
         ),
         cost_estimate=pl.CostEstimate(
@@ -167,7 +171,7 @@
     )
     column_out = context.reshape(local_tokens, feature_width)
     has_prev = (seq_index > 0).astype(jnp.int32).reshape(1)
-    both = attend_rows(has_prev, query_vectors[0], prev_pair, key_vectors[0], value_vectors[0])
+    both = attend_rows(has_prev, query_vectors[0], prev_pair, key_vectors[0].T, value_vectors[0])
     return both.at[1].set(column_out)
 
 

time: 83.8 us -> 82.2 us (0.981)
  local copies, waits for them, and re-layouts: 8.8 us -> 6.78 us
  waiting for transfers between devices: 44.3 us -> 45.9 us
    ppermute x1, waiting for transfers between devices: 14.3 us -> 15.8 us  [shifted(): return lax.ppermute(block, axis, route)]
    convert_element_type x1, local copies, waits for them, and re-layouts: 2.38 us -> 1.23 us  [attend_columns(): return jnp.einsum('chrs,schd->rchd', weights, value_cols, preferred_eleme...]
    all_to_all x1, local copies, waits for them, and re-layouts: 1.24 us -> 0.21 us  [local(): lax.all_to_all(result.reshape(blocks, width, feature_width), 'seq', split...]
    unnamed x6 -> x5, local copies, waits for them, and re-layouts: 0.01 us -> 1.02 us
  transfers between devices with their start and end apart: 3 -> 3, of which waited for: 2 -> 2; matrix products, arithmetic and copies ran while one was open for 11% -> 9% of each run, Pallas kernels for 10% -> 9%
where the time goes in v14:
time: 82.2 us; the launch traced here: 81.8 us
  waiting for transfers between devices  45.9 us (56%)
  starting transfers between devices  16.5 us (20%)
  Pallas kernels  10.6 us (13%)
  local copies, waits for them, and re-layouts  6.78 us (8%)
  matrix products  1.18 us (1%)
  other arithmetic  0.84 us (1%)
    all_to_all x1, waiting for transfers between devices, local(): lax.all_to_all(stacked, 'seq', split_axis=0, concat_axis=0, tiled=True)  30 us
    ppermute x1, waiting for transfers between devices, shifted(): return lax.ppermute(block, axis, route)  15.8 us
    all_to_all x1, starting transfers between devices, local(): lax.all_to_all(result.reshape(blocks, width, feature_width), 'seq', split...  7.85 us
    pallas_call x1, Pallas kernels, attend_rows(): pl.pallas_call(row_kernel, out_shape=jax.ShapeDtypeStruct((2, tokens, wid...  7.74 us
    all_to_all x1, starting transfers between devices, local(): lax.all_to_all(stacked, 'seq', split_axis=0, concat_axis=0, tiled=True)  5.58 us
    ppermute x1, starting transfers between devices, shifted(): return lax.ppermute(block, axis, route)  3.08 us
    pallas_call x1, Pallas kernels, pack(): pl.pallas_call(pack_kernel, out_shape=(jax.ShapeDtypeStruct((blocks, 3, s...  2.85 us
  transfers between devices with their start and end apart: 3, of which 2 were waited for; matrix products, arithmetic and copies ran while one was open for 9% of the time, Pallas kernels for 9%

profile of v14, /device:TPU:17, one launch (start us, length us, event | category | flops | bytes accessed | tf_op | source)
XLA Modules:
  0.0 81.8 jit_solution(161742312115032207)
XLA Ops:
  0.0 2.8 %shard_map.37 = (bf16[8,3,128,256]{3,2,1,0:T(8,128)(2,1)}, bf16[2,1024,256]{2,1,0:T(8,128)(2,1)}) custom-call(bf16[2,1024,256]{2,1,0:T(8,128)(2,1)} %q_ref.1, bf16[2,1024,256]{2,1,0:T(8,128)(2,1)} %kp_ref.1, bf16[2,1024,256]{2,1,0:T(8,128)(2,1)} %vp_ref.1, bf16[2,1024,256]{2,1,0:T(8,128)(2,1)} %kp_ref.1, bf16[2,1024,256]{2,1,0:T(8,128)(2,1)} %vp_ref.1), custom_call_target="tpu_custom_call" | custom-call | tf_op jit(solution)/shard_map/pallas_call | solution.py:129
  2.8 5.6 %all-to-all-start = ((bf16[8,3,128,256]{3,2,1,0:T(8,128)(2,1)}), bf16[8,3,128,256]{3,2,1,0:T(8,128)(2,1)S(1)}, u32[]{:S(2)}, u32[]{:S(2)}) async-start(bf16[8,3,128,256]{3,2,1,0:T(8,128)(2,1)} %get-tuple-element.20), calls=%async_computation | async-start | bytes 3145728 | tf_op jit(solution)/shard_map/all_to_all | solution.py:165
  8.4 3.1 %collective-permute-start = (bf16[2,1024,256]{2,1,0:T(8,128)(2,1)}, bf16[2,1024,256]{2,1,0:T(8,128)(2,1)}, u32[]{:S(2)}, u32[]{:S(2)}) collective-permute-start(bf16[2,1024,256]{2,1,0:T(8,128)(2,1)} %get-tuple-element.21), channel_id=1, source_target_pairs={{0,2},{2,4},{4,6},{6,8},{8,10},{10,12},{12,14},{1,3},{3,5},{5,7},{... | collective-permute-start | bytes 3145736 | tf_op jit(solution)/shard_map/ppermute | solution.py:19
  11.5 30.0 %all-to-all-done = bf16[8,3,128,256]{3,2,1,0:T(8,128)(2,1)S(1)} async-done(((bf16[8,3,128,256]{3,2,1,0:T(8,128)(2,1)}), bf16[8,3,128,256]{3,2,1,0:T(8,128)(2,1)S(1)}, u32[]{:S(2)}, u32[]{:S(2)}) %all-to-all-start) | async-done | bytes 1572896 | tf_op jit(solution)/shard_map/all_to_all | solution.py:165
  41.6 0.4 reshape.60
  42.0 1.2 %fusion.11 = (bf16[8,1,128,2,128]{4,3,2,1,0:T(2,128)(2,1)S(1)}, bf16[8,1,128,2,128]{4,3,2,1,0:T(2,128)(2,1)S(1)}, bf16[8,1,128,2,128]{4,3,2,1,0:T(2,128)(2,1)S(1)}) fusion(bf16[8,3,128,2,128]{4,3,2,1,0:T(2,128)(2,1)S(1)} %reshape.60), kind=kLoop, calls=%fused_computation.21 | loop fusion | bytes 3145728 | tf_op jit(solution)/shard_map/slice | solution.py:168
  43.2 0.7 fusion.4
  43.9 0.4 copy.20
  44.3 0.8 fusion.12
  45.1 0.4 copy.21
  45.6 0.5 fusion.1
  46.1 0.0 slice-start
  46.1 1.2 %copy.22 = bf16[8,128,2,128]{1,3,2,0:T(8,128)(2,1)} copy(bf16[8,128,2,128]{3,0,2,1:T(8,128)(2,1)S(1)} %fusion.1) | data formatting | bytes 1048576 | tf_op jit(solution)/shard_map/convert_element_type | solution.py:38
  47.3 7.8 %all-to-all-start.1 = ((bf16[8,128,256]{1,2,0:T(8,128)(2,1)}), bf16[8,128,256]{1,2,0:T(8,128)(2,1)S(1)}, u32[]{:S(2)}, u32[]{:S(2)}) async-start(bf16[8,128,256]{1,2,0:T(8,128)(2,1)} %bitcast.26), calls=%async_computation.1 | async-start | bytes 1048576 | tf_op jit(solution)/shard_map/all_to_all | solution.py:169
  55.2 0.0 slice-done
  55.2 1.0 %copy.24 = bf16[1,1024,256]{1,2,0:T(8,128)(2,1)} copy(bf16[1,1024,256]{2,1,0:T(8,128)(2,1)S(1)} %slice-done) | data formatting | bytes 1048576
  56.2 0.0 copy-done
  56.2 0.0 copy-done.1
  56.2 1.0 %slice_bitcast_fusion = (bf16[1024,256]{1,0:T(8,128)(2,1)}, bf16[1024,256]{1,0:T(8,128)(2,1)}) fusion(bf16[2,1024,256]{2,1,0:T(8,128)(2,1)S(1)} %copy-done, bf16[2,1024,256]{2,1,0:T(8,128)(2,1)S(1)} %copy-done.1), kind=kLoop, calls=%fused_computation.10 | loop fusion | bytes 2097152 | tf_op jit(solution)/shard_map/squeeze | solution.py:174
  57.2 15.8 %collective-permute-done.refs_1_.refs_3_ = bf16[2,1024,256]{2,1,0:T(8,128)(2,1)} collective-permute-done((bf16[2,1024,256]{2,1,0:T(8,128)(2,1)}, bf16[2,1024,256]{2,1,0:T(8,128)(2,1)}, u32[]{:S(2)}, u32[]{:S(2)}) %collective-permute-start) | collective-permute-done | bytes 1048608 | tf_op jit(solution)/shard_map/ppermute | solution.py:19
  73.0 7.7 %shard_map.38 = bf16[2,1024,256]{2,1,0:T(8,128)(2,1)} custom-call(s32[1]{0:T(128)} %bitcast.flag_ref, bf16[1024,256]{1,0:T(8,128)(2,1)} %get-tuple-element.29.refs_0_, bf16[2,1024,256]{2,1,0:T(8,128)(2,1)} %collective-permute-done.refs_1_.refs_3_, bf16[256,1024]{1,0:T(8,128)(2,1)} %bitcast.28, bf16[2,1024,256]{2,1,0:T(8,128)(2,1)} %collective-permute-done.refs_1_.refs_3_, ...), custom_call_target="tpu_custom_call" | custom-call | flops 1610612736 | bytes 3145728 | tf_op jit(solution)/shard_map/pallas_call | solution.py:99
  80.8 0.0 all-to-all-done.1
  80.8 0.2 copy.23
  81.0 0.8 %bitcast_dynamic-update-slice_fusion = bf16[2,1024,256]{2,1,0:T(8,128)(2,1)} fusion(bf16[2,1024,256]{2,1,0:T(8,128)(2,1)} %shard_map.38, bf16[1,1024,256]{2,1,0:T(8,128)(2,1)S(1)} %bitcast.27), kind=kLoop, calls=%fused_computation.9 | loop fusion | bytes 1048576 | tf_op jit(solution)/shard_map/scatter | solution.py:175
  (4 shorter events, 0.0 us)
Async XLA Ops:
  2.8 38.7 %all-to-all-start = ((bf16[8,3,128,256]{3,2,1,0:T(8,128)(2,1)}), bf16[8,3,128,256]{3,2,1,0:T(8,128)(2,1)S(1)}, u32[]{:S(2)}, u32[]{:S(2)}) async-start(bf16[8,3,128,256]{3,2,1,0:T(8,128)(2,1)} %get-tuple-element.20), calls=%async_computation | async-start | bytes 3145728 | tf_op jit(solution)/shard_map/all_to_all | solution.py:165
  8.4 64.6 %collective-permute-start = (bf16[2,1024,256]{2,1,0:T(8,128)(2,1)}, bf16[2,1024,256]{2,1,0:T(8,128)(2,1)}, u32[]{:S(2)}, u32[]{:S(2)}) collective-permute-start(bf16[2,1024,256]{2,1,0:T(8,128)(2,1)} %get-tuple-element.21), channel_id=1, source_target_pairs={{0,2},{2,4},{4,6},{6,8},{8,10},{10,12},{12,14},{1,3},{3,5},{5,7},{... | collective-permute-start | bytes 3145736 | tf_op jit(solution)/shard_map/ppermute | solution.py:19
  46.1 9.1 %slice-start = ((bf16[2,1024,256]{2,1,0:T(8,128)(2,1)}), bf16[1,1024,256]{2,1,0:T(8,128)(2,1)S(1)}, s32[]{:S(2)}) async-start(bf16[2,1024,256]{2,1,0:T(8,128)(2,1)} %kp_ref.1), calls=%async_computation.2 | async-start | bytes 1048576 | tf_op jit(solution)/shard_map/slice | solution.py:174
  47.3 8.9 %copy-start = (bf16[2,1024,256]{2,1,0:T(8,128)(2,1)S(1)}, bf16[2,1024,256]{2,1,0:T(8,128)(2,1)}, u32[]{:S(2)}) copy-start(bf16[2,1024,256]{2,1,0:T(8,128)(2,1)} %vp_ref.1) | copy-start | bytes 3145732
  47.3 8.9 %copy-start.1 = (bf16[2,1024,256]{2,1,0:T(8,128)(2,1)S(1)}, bf16[2,1024,256]{2,1,0:T(8,128)(2,1)}, u32[]{:S(2)}) copy-start(bf16[2,1024,256]{2,1,0:T(8,128)(2,1)} %q_ref.1) | copy-start | bytes 3145732
  47.3 33.5 %all-to-all-start.1 = ((bf16[8,128,256]{1,2,0:T(8,128)(2,1)}), bf16[8,128,256]{1,2,0:T(8,128)(2,1)S(1)}, u32[]{:S(2)}, u32[]{:S(2)}) async-start(bf16[8,128,256]{1,2,0:T(8,128)(2,1)} %bitcast.26), calls=%async_computation.1 | async-start | bytes 1048576 | tf_op jit(solution)/shard_map/all_to_all | solution.py:169

commit v15 on v14

--- a/solution.py
+++ b/solution.py
@@ -10,7 +10,7 @@
 
 DH = 128
 STRIDE = 1024
-QUERY_TILE = 512
+QUERY_TILE = 256
 
 
 def shifted(block, axis, distance):

time: 82.2 us -> 82.5 us (level)
  transfers between devices with their start and end apart: 3 -> 3, of which waited for: 2 -> 2; matrix products, arithmetic and copies ran while one was open for 9% -> 9% of each run, Pallas kernels for 9% -> 10%
where the time goes in v15:
time: 82.5 us; the launch traced here: 82.1 us
  waiting for transfers between devices  45.9 us (56%)
  starting transfers between devices  16.5 us (20%)
  Pallas kernels  10.9 us (13%)
  local copies, waits for them, and re-layouts  6.78 us (8%)
  matrix products  1.18 us (1%)
  other arithmetic  0.84 us (1%)
    all_to_all x1, waiting for transfers between devices, local(): lax.all_to_all(stacked, 'seq', split_axis=0, concat_axis=0, tiled=True)  30 us
    ppermute x1, waiting for transfers between devices, shifted(): return lax.ppermute(block, axis, route)  15.8 us
    pallas_call x1, Pallas kernels, attend_rows(): pl.pallas_call(row_kernel, out_shape=jax.ShapeDtypeStruct((2, tokens, wid...  8.04 us
    all_to_all x1, starting transfers between devices, local(): lax.all_to_all(result.reshape(blocks, width, feature_width), 'seq', split...  7.85 us
    all_to_all x1, starting transfers between devices, local(): lax.all_to_all(stacked, 'seq', split_axis=0, concat_axis=0, tiled=True)  5.58 us
    ppermute x1, starting transfers between devices, shifted(): return lax.ppermute(block, axis, route)  3.08 us
    pallas_call x1, Pallas kernels, pack(): pl.pallas_call(pack_kernel, out_shape=(jax.ShapeDtypeStruct((blocks, 3, s...  2.85 us
  transfers between devices with their start and end apart: 3, of which 2 were waited for; matrix products, arithmetic and copies ran while one was open for 9% of the time, Pallas kernels for 10%

profile of v15, /device:TPU:17, one launch (start us, length us, event | category | flops | bytes accessed | tf_op | source)
XLA Modules:
  0.0 82.1 jit_solution(7368804681776982411)
XLA Ops:
  0.0 2.8 %shard_map.37 = (bf16[8,3,128,256]{3,2,1,0:T(8,128)(2,1)}, bf16[2,1024,256]{2,1,0:T(8,128)(2,1)}) custom-call(bf16[2,1024,256]{2,1,0:T(8,128)(2,1)} %q_ref.1, bf16[2,1024,256]{2,1,0:T(8,128)(2,1)} %kp_ref.1, bf16[2,1024,256]{2,1,0:T(8,128)(2,1)} %vp_ref.1, bf16[2,1024,256]{2,1,0:T(8,128)(2,1)} %kp_ref.1, bf16[2,1024,256]{2,1,0:T(8,128)(2,1)} %vp_ref.1), custom_call_target="tpu_custom_call" | custom-call | tf_op jit(solution)/shard_map/pallas_call | solution.py:129
  2.8 5.6 %all-to-all-start = ((bf16[8,3,128,256]{3,2,1,0:T(8,128)(2,1)}), bf16[8,3,128,256]{3,2,1,0:T(8,128)(2,1)S(1)}, u32[]{:S(2)}, u32[]{:S(2)}) async-start(bf16[8,3,128,256]{3,2,1,0:T(8,128)(2,1)} %get-tuple-element.20), calls=%async_computation | async-start | bytes 3145728 | tf_op jit(solution)/shard_map/all_to_all | solution.py:165
  8.4 3.1 %collective-permute-start = (bf16[2,1024,256]{2,1,0:T(8,128)(2,1)}, bf16[2,1024,256]{2,1,0:T(8,128)(2,1)}, u32[]{:S(2)}, u32[]{:S(2)}) collective-permute-start(bf16[2,1024,256]{2,1,0:T(8,128)(2,1)} %get-tuple-element.21), channel_id=1, source_target_pairs={{0,2},{2,4},{4,6},{6,8},{8,10},{10,12},{12,14},{1,3},{3,5},{5,7},{... | collective-permute-start | bytes 3145736 | tf_op jit(solution)/shard_map/ppermute | solution.py:19
  11.5 30.0 %all-to-all-done = bf16[8,3,128,256]{3,2,1,0:T(8,128)(2,1)S(1)} async-done(((bf16[8,3,128,256]{3,2,1,0:T(8,128)(2,1)}), bf16[8,3,128,256]{3,2,1,0:T(8,128)(2,1)S(1)}, u32[]{:S(2)}, u32[]{:S(2)}) %all-to-all-start) | async-done | bytes 1572896 | tf_op jit(solution)/shard_map/all_to_all | solution.py:165
  41.6 0.4 reshape.60
  42.0 1.2 %fusion.11 = (bf16[8,1,128,2,128]{4,3,2,1,0:T(2,128)(2,1)S(1)}, bf16[8,1,128,2,128]{4,3,2,1,0:T(2,128)(2,1)S(1)}, bf16[8,1,128,2,128]{4,3,2,1,0:T(2,128)(2,1)S(1)}) fusion(bf16[8,3,128,2,128]{4,3,2,1,0:T(2,128)(2,1)S(1)} %reshape.60), kind=kLoop, calls=%fused_computation.21 | loop fusion | bytes 3145728 | tf_op jit(solution)/shard_map/slice | solution.py:168
  43.2 0.7 fusion.4
  43.9 0.4 copy.20
  44.3 0.8 fusion.12
  45.1 0.4 copy.21
  45.6 0.5 fusion.1
  46.1 0.0 slice-start
  46.1 1.2 %copy.22 = bf16[8,128,2,128]{1,3,2,0:T(8,128)(2,1)} copy(bf16[8,128,2,128]{3,0,2,1:T(8,128)(2,1)S(1)} %fusion.1) | data formatting | bytes 1048576 | tf_op jit(solution)/shard_map/convert_element_type | solution.py:38
  47.3 7.8 %all-to-all-start.1 = ((bf16[8,128,256]{1,2,0:T(8,128)(2,1)}), bf16[8,128,256]{1,2,0:T(8,128)(2,1)S(1)}, u32[]{:S(2)}, u32[]{:S(2)}) async-start(bf16[8,128,256]{1,2,0:T(8,128)(2,1)} %bitcast.26), calls=%async_computation.1 | async-start | bytes 1048576 | tf_op jit(solution)/shard_map/all_to_all | solution.py:169
  55.2 0.0 slice-done
  55.2 1.0 %copy.24 = bf16[1,1024,256]{1,2,0:T(8,128)(2,1)} copy(bf16[1,1024,256]{2,1,0:T(8,128)(2,1)S(1)} %slice-done) | data formatting | bytes 1048576
  56.2 0.0 copy-done
  56.2 0.0 copy-done.1
  56.2 1.0 %slice_bitcast_fusion = (bf16[1024,256]{1,0:T(8,128)(2,1)}, bf16[1024,256]{1,0:T(8,128)(2,1)}) fusion(bf16[2,1024,256]{2,1,0:T(8,128)(2,1)S(1)} %copy-done, bf16[2,1024,256]{2,1,0:T(8,128)(2,1)S(1)} %copy-done.1), kind=kLoop, calls=%fused_computation.10 | loop fusion | bytes 2097152 | tf_op jit(solution)/shard_map/squeeze | solution.py:174
  57.2 15.8 %collective-permute-done.refs_1_.refs_3_ = bf16[2,1024,256]{2,1,0:T(8,128)(2,1)} collective-permute-done((bf16[2,1024,256]{2,1,0:T(8,128)(2,1)}, bf16[2,1024,256]{2,1,0:T(8,128)(2,1)}, u32[]{:S(2)}, u32[]{:S(2)}) %collective-permute-start) | collective-permute-done | bytes 1048608 | tf_op jit(solution)/shard_map/ppermute | solution.py:19
  73.0 8.0 %shard_map.38 = bf16[2,1024,256]{2,1,0:T(8,128)(2,1)} custom-call(s32[1]{0:T(128)} %bitcast.flag_ref, bf16[1024,256]{1,0:T(8,128)(2,1)} %get-tuple-element.29.refs_0_, bf16[2,1024,256]{2,1,0:T(8,128)(2,1)} %collective-permute-done.refs_1_.refs_3_, bf16[256,1024]{1,0:T(8,128)(2,1)} %bitcast.28, bf16[2,1024,256]{2,1,0:T(8,128)(2,1)} %collective-permute-done.refs_1_.refs_3_, ...), custom_call_target="tpu_custom_call" | custom-call | flops 1342177280 | bytes 3145728 | tf_op jit(solution)/shard_map/pallas_call | solution.py:99
  81.1 0.0 all-to-all-done.1
  81.1 0.2 copy.23
  81.3 0.8 %bitcast_dynamic-update-slice_fusion = bf16[2,1024,256]{2,1,0:T(8,128)(2,1)} fusion(bf16[2,1024,256]{2,1,0:T(8,128)(2,1)} %shard_map.38, bf16[1,1024,256]{2,1,0:T(8,128)(2,1)S(1)} %bitcast.27), kind=kLoop, calls=%fused_computation.9 | loop fusion | bytes 1048576 | tf_op jit(solution)/shard_map/scatter | solution.py:175
  (4 shorter events, 0.0 us)
Async XLA Ops:
  2.8 38.7 %all-to-all-start = ((bf16[8,3,128,256]{3,2,1,0:T(8,128)(2,1)}), bf16[8,3,128,256]{3,2,1,0:T(8,128)(2,1)S(1)}, u32[]{:S(2)}, u32[]{:S(2)}) async-start(bf16[8,3,128,256]{3,2,1,0:T(8,128)(2,1)} %get-tuple-element.20), calls=%async_computation | async-start | bytes 3145728 | tf_op jit(solution)/shard_map/all_to_all | solution.py:165
  8.4 64.6 %collective-permute-start = (bf16[2,1024,256]{2,1,0:T(8,128)(2,1)}, bf16[2,1024,256]{2,1,0:T(8,128)(2,1)}, u32[]{:S(2)}, u32[]{:S(2)}) collective-permute-start(bf16[2,1024,256]{2,1,0:T(8,128)(2,1)} %get-tuple-element.21), channel_id=1, source_target_pairs={{0,2},{2,4},{4,6},{6,8},{8,10},{10,12},{12,14},{1,3},{3,5},{5,7},{... | collective-permute-start | bytes 3145736 | tf_op jit(solution)/shard_map/ppermute | solution.py:19
  46.1 9.1 %slice-start = ((bf16[2,1024,256]{2,1,0:T(8,128)(2,1)}), bf16[1,1024,256]{2,1,0:T(8,128)(2,1)S(1)}, s32[]{:S(2)}) async-start(bf16[2,1024,256]{2,1,0:T(8,128)(2,1)} %kp_ref.1), calls=%async_computation.2 | async-start | bytes 1048576 | tf_op jit(solution)/shard_map/slice | solution.py:174
  47.3 8.9 %copy-start = (bf16[2,1024,256]{2,1,0:T(8,128)(2,1)S(1)}, bf16[2,1024,256]{2,1,0:T(8,128)(2,1)}, u32[]{:S(2)}) copy-start(bf16[2,1024,256]{2,1,0:T(8,128)(2,1)} %vp_ref.1) | copy-start | bytes 3145732
  47.3 8.9 %copy-start.1 = (bf16[2,1024,256]{2,1,0:T(8,128)(2,1)S(1)}, bf16[2,1024,256]{2,1,0:T(8,128)(2,1)}, u32[]{:S(2)}) copy-start(bf16[2,1024,256]{2,1,0:T(8,128)(2,1)} %q_ref.1) | copy-start | bytes 3145732
  47.3 33.8 %all-to-all-start.1 = ((bf16[8,128,256]{1,2,0:T(8,128)(2,1)}), bf16[8,128,256]{1,2,0:T(8,128)(2,1)S(1)}, u32[]{:S(2)}, u32[]{:S(2)}) async-start(bf16[8,128,256]{1,2,0:T(8,128)(2,1)} %bitcast.26), calls=%async_computation.1 | async-start | bytes 1048576 | tf_op jit(solution)/shard_map/all_to_all | solution.py:169

commit v16 on v14

--- a/solution.py
+++ b/solution.py
@@ -120,7 +120,7 @@
     pair_ref[1] = vp_ref[...]
 
 
-def pack(query_vectors, key_vectors, value_vectors, blocks, steps=2):
+def pack(query_vectors, key_vectors, value_vectors, blocks, steps=1):
     _, tokens, width = query_vectors.shape
     size = tokens // blocks
     rows = tokens // steps

time: 82.2 us -> 82.6 us (level)
  no operation moved by 1% of the time
where the time goes in v16:
time: 82.6 us; the launch traced here: 82.3 us
  waiting for transfers between devices  45.9 us (56%)
  starting transfers between devices  16.5 us (20%)
  Pallas kernels  11 us (13%)
  local copies, waits for them, and re-layouts  6.78 us (8%)
  matrix products  1.17 us (1%)
  other arithmetic  0.84 us (1%)
    all_to_all x1, waiting for transfers between devices, local(): lax.all_to_all(stacked, 'seq', split_axis=0, concat_axis=0, tiled=True)  30 us
    ppermute x1, waiting for transfers between devices, shifted(): return lax.ppermute(block, axis, route)  15.8 us
    all_to_all x1, starting transfers between devices, local(): lax.all_to_all(result.reshape(blocks, width, feature_width), 'seq', split...  7.85 us
    pallas_call x1, Pallas kernels, attend_rows(): pl.pallas_call(row_kernel, out_shape=jax.ShapeDtypeStruct((2, tokens, wid...  7.75 us
    all_to_all x1, starting transfers between devices, local(): lax.all_to_all(stacked, 'seq', split_axis=0, concat_axis=0, tiled=True)  5.58 us
    pallas_call x1, Pallas kernels, pack(): pl.pallas_call(pack_kernel, out_shape=(jax.ShapeDtypeStruct((blocks, 3, s...  3.26 us
    ppermute x1, starting transfers between devices, shifted(): return lax.ppermute(block, axis, route)  3.08 us
  transfers between devices with their start and end apart: 3, of which 2 were waited for; matrix products, arithmetic and copies ran while one was open for 9% of the time, Pallas kernels for 9%

profile of v16, /device:TPU:17, one launch (start us, length us, event | category | flops | bytes accessed | tf_op | source)
XLA Modules:
  0.0 82.3 jit_solution(16403890457863004167)
XLA Ops:
  0.0 3.3 %shard_map.37 = (bf16[8,3,128,256]{3,2,1,0:T(8,128)(2,1)}, bf16[2,1024,256]{2,1,0:T(8,128)(2,1)}) custom-call(bf16[2,1024,256]{2,1,0:T(8,128)(2,1)} %q_ref.1, bf16[2,1024,256]{2,1,0:T(8,128)(2,1)} %kp_ref.1, bf16[2,1024,256]{2,1,0:T(8,128)(2,1)} %vp_ref.1, bf16[2,1024,256]{2,1,0:T(8,128)(2,1)} %kp_ref.1, bf16[2,1024,256]{2,1,0:T(8,128)(2,1)} %vp_ref.1), custom_call_target="tpu_custom_call" | custom-call | tf_op jit(solution)/shard_map/pallas_call | solution.py:129
  3.3 5.6 %all-to-all-start = ((bf16[8,3,128,256]{3,2,1,0:T(8,128)(2,1)}), bf16[8,3,128,256]{3,2,1,0:T(8,128)(2,1)S(1)}, u32[]{:S(2)}, u32[]{:S(2)}) async-start(bf16[8,3,128,256]{3,2,1,0:T(8,128)(2,1)} %get-tuple-element.20), calls=%async_computation | async-start | bytes 3145728 | tf_op jit(solution)/shard_map/all_to_all | solution.py:165
  8.8 3.1 %collective-permute-start = (bf16[2,1024,256]{2,1,0:T(8,128)(2,1)}, bf16[2,1024,256]{2,1,0:T(8,128)(2,1)}, u32[]{:S(2)}, u32[]{:S(2)}) collective-permute-start(bf16[2,1024,256]{2,1,0:T(8,128)(2,1)} %get-tuple-element.21), channel_id=1, source_target_pairs={{0,2},{2,4},{4,6},{6,8},{8,10},{10,12},{12,14},{1,3},{3,5},{5,7},{... | collective-permute-start | bytes 3145736 | tf_op jit(solution)/shard_map/ppermute | solution.py:19
  11.9 30.0 %all-to-all-done = bf16[8,3,128,256]{3,2,1,0:T(8,128)(2,1)S(1)} async-done(((bf16[8,3,128,256]{3,2,1,0:T(8,128)(2,1)}), bf16[8,3,128,256]{3,2,1,0:T(8,128)(2,1)S(1)}, u32[]{:S(2)}, u32[]{:S(2)}) %all-to-all-start) | async-done | bytes 1572896 | tf_op jit(solution)/shard_map/all_to_all | solution.py:165
  42.0 0.4 reshape.60
  42.4 1.2 %fusion.11 = (bf16[8,1,128,2,128]{4,3,2,1,0:T(2,128)(2,1)S(1)}, bf16[8,1,128,2,128]{4,3,2,1,0:T(2,128)(2,1)S(1)}, bf16[8,1,128,2,128]{4,3,2,1,0:T(2,128)(2,1)S(1)}) fusion(bf16[8,3,128,2,128]{4,3,2,1,0:T(2,128)(2,1)S(1)} %reshape.60), kind=kLoop, calls=%fused_computation.21 | loop fusion | bytes 3145728 | tf_op jit(solution)/shard_map/slice | solution.py:168
  43.6 0.7 fusion.4
  44.3 0.4 copy.20
  44.7 0.8 fusion.12
  45.6 0.4 copy.21
  46.0 0.5 fusion.1
  46.5 0.0 slice-start
  46.5 1.2 %copy.22 = bf16[8,128,2,128]{1,3,2,0:T(8,128)(2,1)} copy(bf16[8,128,2,128]{3,0,2,1:T(8,128)(2,1)S(1)} %fusion.1) | data formatting | bytes 1048576 | tf_op jit(solution)/shard_map/convert_element_type | solution.py:38
  47.7 7.9 %all-to-all-start.1 = ((bf16[8,128,256]{1,2,0:T(8,128)(2,1)}), bf16[8,128,256]{1,2,0:T(8,128)(2,1)S(1)}, u32[]{:S(2)}, u32[]{:S(2)}) async-start(bf16[8,128,256]{1,2,0:T(8,128)(2,1)} %bitcast.26), calls=%async_computation.1 | async-start | bytes 1048576 | tf_op jit(solution)/shard_map/all_to_all | solution.py:169
  55.6 0.0 slice-done
  55.6 1.0 %copy.24 = bf16[1,1024,256]{1,2,0:T(8,128)(2,1)} copy(bf16[1,1024,256]{2,1,0:T(8,128)(2,1)S(1)} %slice-done) | data formatting | bytes 1048576
  56.6 0.0 copy-done
  56.6 0.0 copy-done.1
  56.6 1.0 %slice_bitcast_fusion = (bf16[1024,256]{1,0:T(8,128)(2,1)}, bf16[1024,256]{1,0:T(8,128)(2,1)}) fusion(bf16[2,1024,256]{2,1,0:T(8,128)(2,1)S(1)} %copy-done, bf16[2,1024,256]{2,1,0:T(8,128)(2,1)S(1)} %copy-done.1), kind=kLoop, calls=%fused_computation.10 | loop fusion | bytes 2097152 | tf_op jit(solution)/shard_map/squeeze | solution.py:174
  57.6 15.8 %collective-permute-done.refs_1_.refs_3_ = bf16[2,1024,256]{2,1,0:T(8,128)(2,1)} collective-permute-done((bf16[2,1024,256]{2,1,0:T(8,128)(2,1)}, bf16[2,1024,256]{2,1,0:T(8,128)(2,1)}, u32[]{:S(2)}, u32[]{:S(2)}) %collective-permute-start) | collective-permute-done | bytes 1048608 | tf_op jit(solution)/shard_map/ppermute | solution.py:19
  73.5 7.7 %shard_map.38 = bf16[2,1024,256]{2,1,0:T(8,128)(2,1)} custom-call(s32[1]{0:T(128)} %bitcast.flag_ref, bf16[1024,256]{1,0:T(8,128)(2,1)} %get-tuple-element.29.refs_0_, bf16[2,1024,256]{2,1,0:T(8,128)(2,1)} %collective-permute-done.refs_1_.refs_3_, bf16[256,1024]{1,0:T(8,128)(2,1)} %bitcast.28, bf16[2,1024,256]{2,1,0:T(8,128)(2,1)} %collective-permute-done.refs_1_.refs_3_, ...), custom_call_target="tpu_custom_call" | custom-call | flops 1610612736 | bytes 3145728 | tf_op jit(solution)/shard_map/pallas_call | solution.py:99
  81.2 0.0 all-to-all-done.1
  81.2 0.2 copy.23
  81.4 0.8 %bitcast_dynamic-update-slice_fusion = bf16[2,1024,256]{2,1,0:T(8,128)(2,1)} fusion(bf16[2,1024,256]{2,1,0:T(8,128)(2,1)} %shard_map.38, bf16[1,1024,256]{2,1,0:T(8,128)(2,1)S(1)} %bitcast.27), kind=kLoop, calls=%fused_computation.9 | loop fusion | bytes 1048576 | tf_op jit(solution)/shard_map/scatter | solution.py:175
  (4 shorter events, 0.0 us)
Async XLA Ops:
  3.3 38.7 %all-to-all-start = ((bf16[8,3,128,256]{3,2,1,0:T(8,128)(2,1)}), bf16[8,3,128,256]{3,2,1,0:T(8,128)(2,1)S(1)}, u32[]{:S(2)}, u32[]{:S(2)}) async-start(bf16[8,3,128,256]{3,2,1,0:T(8,128)(2,1)} %get-tuple-element.20), calls=%async_computation | async-start | bytes 3145728 | tf_op jit(solution)/shard_map/all_to_all | solution.py:165
  8.8 64.6 %collective-permute-start = (bf16[2,1024,256]{2,1,0:T(8,128)(2,1)}, bf16[2,1024,256]{2,1,0:T(8,128)(2,1)}, u32[]{:S(2)}, u32[]{:S(2)}) collective-permute-start(bf16[2,1024,256]{2,1,0:T(8,128)(2,1)} %get-tuple-element.21), channel_id=1, source_target_pairs={{0,2},{2,4},{4,6},{6,8},{8,10},{10,12},{12,14},{1,3},{3,5},{5,7},{... | collective-permute-start | bytes 3145736 | tf_op jit(solution)/shard_map/ppermute | solution.py:19
  46.5 9.1 %slice-start = ((bf16[2,1024,256]{2,1,0:T(8,128)(2,1)}), bf16[1,1024,256]{2,1,0:T(8,128)(2,1)S(1)}, s32[]{:S(2)}) async-start(bf16[2,1024,256]{2,1,0:T(8,128)(2,1)} %kp_ref.1), calls=%async_computation.2 | async-start | bytes 1048576 | tf_op jit(solution)/shard_map/slice | solution.py:174
  47.7 8.9 %copy-start = (bf16[2,1024,256]{2,1,0:T(8,128)(2,1)S(1)}, bf16[2,1024,256]{2,1,0:T(8,128)(2,1)}, u32[]{:S(2)}) copy-start(bf16[2,1024,256]{2,1,0:T(8,128)(2,1)} %vp_ref.1) | copy-start | bytes 3145732
  47.7 8.9 %copy-start.1 = (bf16[2,1024,256]{2,1,0:T(8,128)(2,1)S(1)}, bf16[2,1024,256]{2,1,0:T(8,128)(2,1)}, u32[]{:S(2)}) copy-start(bf16[2,1024,256]{2,1,0:T(8,128)(2,1)} %q_ref.1) | copy-start | bytes 3145732
  47.7 33.5 %all-to-all-start.1 = ((bf16[8,128,256]{1,2,0:T(8,128)(2,1)}), bf16[8,128,256]{1,2,0:T(8,128)(2,1)S(1)}, u32[]{:S(2)}, u32[]{:S(2)}) async-start(bf16[8,128,256]{1,2,0:T(8,128)(2,1)} %bitcast.26), calls=%async_computation.1 | async-start | bytes 1048576 | tf_op jit(solution)/shard_map/all_to_all | solution.py:169

commit v17 on v14

--- a/solution.py
+++ b/solution.py
@@ -40,10 +40,12 @@
 
 def row_tiles(with_prev, q_ref, kp_ref, kc_ref, vp_ref, vc_ref, o_ref):
     score_scale = 1.0 / math.sqrt(DH)
+    factor = score_scale * math.log2(math.e)
     dims = (((1,), (1,)), ((), ()))
     tq = QUERY_TILE
-    upper = lax.broadcasted_iota(jnp.int32, (tq, tq), 1) > lax.broadcasted_iota(
-        jnp.int32, (tq, tq), 0
+    half = tq // 2
+    upper = lax.broadcasted_iota(jnp.int32, (half, half), 1) > lax.broadcasted_iota(
+        jnp.int32, (half, half), 0
     )
 
     def scores(q, k_ref, low, high):
@@ -54,25 +56,58 @@
 
     for tile in range(STRIDE // tq):
         low, high = tile * tq, (tile + 1) * tq
+        mid = low + half
         q = q_ref[low:high, :]
-        parts = []
+        top, bottom = q[:half], q[half:]
+        full, top_parts, bottom_parts = [], [], []
         if with_prev:
-            parts.append((jnp.where(upper, scores(q, kp_ref, low, high), -jnp.inf), vp_ref, low, high))
+            top_parts.append((jnp.where(upper, scores(top, kp_ref, low, mid), -jnp.inf), vp_ref[low:mid, :]))
+            top_parts.append((scores(top, kp_ref, mid, high), vp_ref[mid:high, :]))
+            bottom_parts.append((jnp.where(upper, scores(bottom, kp_ref, mid, high), -jnp.inf), vp_ref[mid:high, :]))
             if high < STRIDE:
-                parts.append((scores(q, kp_ref, high, STRIDE), vp_ref, high, STRIDE))
+                full.append((scores(q, kp_ref, high, STRIDE), vp_ref[high:, :]))
         if low > 0:
-            parts.append((scores_t(q, kc_ref, 0, low), vc_ref, 0, low))
-        parts.append((jnp.where(upper, -jnp.inf, scores_t(q, kc_ref, low, high)), vc_ref, low, high))
-        maxima = functools.reduce(
-            jnp.maximum, [jnp.max(p[0], axis=1, keepdims=True) for p in parts]
-        )
-        expos = [jnp.exp2((p[0] - maxima) * (score_scale * math.log2(math.e))) for p in parts]
-        total = functools.reduce(jnp.add, [jnp.sum(e, axis=1, keepdims=True) for e in expos])
-        inverse = 1.0 / total
-        out = None
-        for e, (_, v_ref, a, b) in zip(expos, parts):
-            term = jnp.dot((e * inverse).astype(jnp.bfloat16), v_ref[a:b, :], preferred_element_type=jnp.float32)
-            out = term if out is None else out + term
+            full.append((scores_t(q, kc_ref, 0, low), vc_ref[:low, :]))
+        top_parts.append((jnp.where(upper, -jnp.inf, scores_t(top, kc_ref, low, mid)), vc_ref[low:mid, :]))
+        bottom_parts.append((scores_t(bottom, kc_ref, low, mid), vc_ref[low:mid, :]))
+        bottom_parts.append((jnp.where(upper, -jnp.inf, scores_t(bottom, kc_ref, mid, high)), vc_ref[mid:high, :]))
+
+        def row_max(parts, rows):
+            return [jnp.max(p[0][rows] if rows is not None else p[0], axis=1, keepdims=True) for p in parts]
+
+        max_top = functools.reduce(
+            jnp.maximum, row_max(top_parts, None) + [m[:half] for m in row_max(full, None)]
+        )
+        max_bottom = functools.reduce(
+            jnp.maximum, row_max(bottom_parts, None) + [m[half:] for m in row_max(full, None)]
+        )
+        maxima = jnp.concatenate([max_top, max_bottom], axis=0)
+        full_e = [jnp.exp2((p[0] - maxima) * factor) for p in full]
+        top_e = [jnp.exp2((p[0] - max_top) * factor) for p in top_parts]
+        bottom_e = [jnp.exp2((p[0] - max_bottom) * factor) for p in bottom_parts]
+        full_sums = [jnp.sum(e, axis=1, keepdims=True) for e in full_e]
+        total_top = functools.reduce(
+            jnp.add, [jnp.sum(e, axis=1, keepdims=True) for e in top_e] + [t[:half] for t in full_sums]
+        )
+        total_bottom = functools.reduce(
+            jnp.add, [jnp.sum(e, axis=1, keepdims=True) for e in bottom_e] + [t[half:] for t in full_sums]
+        )
+        inv_top = 1.0 / total_top
+        inv_bottom = 1.0 / total_bottom
+        inverse = jnp.concatenate([inv_top, inv_bottom], axis=0)
+
+        def weighted(es, parts, inv):
+            out = None
+            for e, (_, v) in zip(es, parts):
+                term = jnp.dot((e * inv).astype(jnp.bfloat16), v, preferred_element_type=jnp.float32)
+                out = term if out is None else out + term
+            return out
+
+        out_top = weighted(top_e, top_parts, inv_top)
+        out_bottom = weighted(bottom_e, bottom_parts, inv_bottom)
+        out = jnp.concatenate([out_top, out_bottom], axis=0)
+        if full:
+            out = out + weighted(full_e, full, inverse)
         o_ref[low:high, :] = out.astype(o_ref.dtype)
 
 

time: 82.2 us -> 83.5 us (1.016)
  Pallas kernels: 10.6 us -> 11.9 us
    pallas_call x1, Pallas kernels: 7.74 us -> 9.06 us  [attend_rows(): pl.pallas_call(row_kernel, out_shape=jax.ShapeDtypeStruct((2, tokens, wid...]
  transfers between devices with their start and end apart: 3 -> 3, of which waited for: 2 -> 2; matrix products, arithmetic and copies ran while one was open for 9% -> 9% of each run, Pallas kernels for 9% -> 11%
where the time goes in v17:
time: 83.5 us; the launch traced here: 83.1 us
  waiting for transfers between devices  45.9 us (55%)
  starting transfers between devices  16.5 us (20%)
  Pallas kernels  11.9 us (14%)
  local copies, waits for them, and re-layouts  6.78 us (8%)
  matrix products  1.18 us (1%)
  other arithmetic  0.84 us (1%)
    all_to_all x1, waiting for transfers between devices, local(): lax.all_to_all(stacked, 'seq', split_axis=0, concat_axis=0, tiled=True)  30 us
    ppermute x1, waiting for transfers between devices, shifted(): return lax.ppermute(block, axis, route)  15.8 us
    pallas_call x1, Pallas kernels, attend_rows(): pl.pallas_call(row_kernel, out_shape=jax.ShapeDtypeStruct((2, tokens, wid...  9.06 us
    all_to_all x1, starting transfers between devices, local(): lax.all_to_all(result.reshape(blocks, width, feature_width), 'seq', split...  7.85 us
    all_to_all x1, starting transfers between devices, local(): lax.all_to_all(stacked, 'seq', split_axis=0, concat_axis=0, tiled=True)  5.58 us
    ppermute x1, starting transfers between devices, shifted(): return lax.ppermute(block, axis, route)  3.08 us
    pallas_call x1, Pallas kernels, pack(): pl.pallas_call(pack_kernel, out_shape=(jax.ShapeDtypeStruct((blocks, 3, s...  2.85 us
  transfers between devices with their start and end apart: 3, of which 2 were waited for; matrix products, arithmetic and copies ran while one was open for 9% of the time, Pallas kernels for 11%

profile of v17, /device:TPU:17, one launch (start us, length us, event | category | flops | bytes accessed | tf_op | source)
XLA Modules:
  0.0 83.1 jit_solution(5996749407277875321)
XLA Ops:
  0.0 2.8 %shard_map.37 = (bf16[8,3,128,256]{3,2,1,0:T(8,128)(2,1)}, bf16[2,1024,256]{2,1,0:T(8,128)(2,1)}) custom-call(bf16[2,1024,256]{2,1,0:T(8,128)(2,1)} %q_ref.1, bf16[2,1024,256]{2,1,0:T(8,128)(2,1)} %kp_ref.1, bf16[2,1024,256]{2,1,0:T(8,128)(2,1)} %vp_ref.1, bf16[2,1024,256]{2,1,0:T(8,128)(2,1)} %kp_ref.1, bf16[2,1024,256]{2,1,0:T(8,128)(2,1)} %vp_ref.1), custom_call_target="tpu_custom_call" | custom-call | tf_op jit(solution)/shard_map/pallas_call | solution.py:164
  2.8 5.6 %all-to-all-start = ((bf16[8,3,128,256]{3,2,1,0:T(8,128)(2,1)}), bf16[8,3,128,256]{3,2,1,0:T(8,128)(2,1)S(1)}, u32[]{:S(2)}, u32[]{:S(2)}) async-start(bf16[8,3,128,256]{3,2,1,0:T(8,128)(2,1)} %get-tuple-element.20), calls=%async_computation | async-start | bytes 3145728 | tf_op jit(solution)/shard_map/all_to_all | solution.py:200
  8.4 3.1 %collective-permute-start = (bf16[2,1024,256]{2,1,0:T(8,128)(2,1)}, bf16[2,1024,256]{2,1,0:T(8,128)(2,1)}, u32[]{:S(2)}, u32[]{:S(2)}) collective-permute-start(bf16[2,1024,256]{2,1,0:T(8,128)(2,1)} %get-tuple-element.21), channel_id=1, source_target_pairs={{0,2},{2,4},{4,6},{6,8},{8,10},{10,12},{12,14},{1,3},{3,5},{5,7},{... | collective-permute-start | bytes 3145736 | tf_op jit(solution)/shard_map/ppermute | solution.py:19
  11.5 30.0 %all-to-all-done = bf16[8,3,128,256]{3,2,1,0:T(8,128)(2,1)S(1)} async-done(((bf16[8,3,128,256]{3,2,1,0:T(8,128)(2,1)}), bf16[8,3,128,256]{3,2,1,0:T(8,128)(2,1)S(1)}, u32[]{:S(2)}, u32[]{:S(2)}) %all-to-all-start) | async-done | bytes 1572896 | tf_op jit(solution)/shard_map/all_to_all | solution.py:200
  41.6 0.4 reshape.60
  42.0 1.2 %fusion.11 = (bf16[8,1,128,2,128]{4,3,2,1,0:T(2,128)(2,1)S(1)}, bf16[8,1,128,2,128]{4,3,2,1,0:T(2,128)(2,1)S(1)}, bf16[8,1,128,2,128]{4,3,2,1,0:T(2,128)(2,1)S(1)}) fusion(bf16[8,3,128,2,128]{4,3,2,1,0:T(2,128)(2,1)S(1)} %reshape.60), kind=kLoop, calls=%fused_computation.21 | loop fusion | bytes 3145728 | tf_op jit(solution)/shard_map/slice | solution.py:203
  43.2 0.7 fusion.4
  43.9 0.4 copy.20
  44.3 0.8 fusion.12
  45.1 0.4 copy.21
  45.6 0.5 fusion.1
  46.1 0.0 slice-start
  46.1 1.2 %copy.22 = bf16[8,128,2,128]{1,3,2,0:T(8,128)(2,1)} copy(bf16[8,128,2,128]{3,0,2,1:T(8,128)(2,1)S(1)} %fusion.1) | data formatting | bytes 1048576 | tf_op jit(solution)/shard_map/convert_element_type | solution.py:38
  47.3 7.8 %all-to-all-start.1 = ((bf16[8,128,256]{1,2,0:T(8,128)(2,1)}), bf16[8,128,256]{1,2,0:T(8,128)(2,1)S(1)}, u32[]{:S(2)}, u32[]{:S(2)}) async-start(bf16[8,128,256]{1,2,0:T(8,128)(2,1)} %bitcast.26), calls=%async_computation.1 | async-start | bytes 1048576 | tf_op jit(solution)/shard_map/all_to_all | solution.py:204
  55.2 0.0 slice-done
  55.2 1.0 %copy.24 = bf16[1,1024,256]{1,2,0:T(8,128)(2,1)} copy(bf16[1,1024,256]{2,1,0:T(8,128)(2,1)S(1)} %slice-done) | data formatting | bytes 1048576
  56.2 0.0 copy-done
  56.2 0.0 copy-done.1
  56.2 1.0 %slice_bitcast_fusion = (bf16[1024,256]{1,0:T(8,128)(2,1)}, bf16[1024,256]{1,0:T(8,128)(2,1)}) fusion(bf16[2,1024,256]{2,1,0:T(8,128)(2,1)S(1)} %copy-done, bf16[2,1024,256]{2,1,0:T(8,128)(2,1)S(1)} %copy-done.1), kind=kLoop, calls=%fused_computation.10 | loop fusion | bytes 2097152 | tf_op jit(solution)/shard_map/squeeze | solution.py:209
  57.2 15.8 %collective-permute-done.refs_1_.refs_3_ = bf16[2,1024,256]{2,1,0:T(8,128)(2,1)} collective-permute-done((bf16[2,1024,256]{2,1,0:T(8,128)(2,1)}, bf16[2,1024,256]{2,1,0:T(8,128)(2,1)}, u32[]{:S(2)}, u32[]{:S(2)}) %collective-permute-start) | collective-permute-done | bytes 1048608 | tf_op jit(solution)/shard_map/ppermute | solution.py:19
  73.0 9.1 %shard_map.38 = bf16[2,1024,256]{2,1,0:T(8,128)(2,1)} custom-call(s32[1]{0:T(128)} %bitcast.flag_ref, bf16[1024,256]{1,0:T(8,128)(2,1)} %get-tuple-element.29.refs_0_, bf16[2,1024,256]{2,1,0:T(8,128)(2,1)} %collective-permute-done.refs_1_.refs_3_, bf16[256,1024]{1,0:T(8,128)(2,1)} %bitcast.28, bf16[2,1024,256]{2,1,0:T(8,128)(2,1)} %collective-permute-done.refs_1_.refs_3_, ...), custom_call_target="tpu_custom_call" | custom-call | flops 1610612736 | bytes 3145728 | tf_op jit(solution)/shard_map/pallas_call | solution.py:134
  82.1 0.0 all-to-all-done.1
  82.1 0.2 copy.23
  82.3 0.8 bitcast_dynamic-update-slice_fusion
  (4 shorter events, 0.0 us)
Async XLA Ops:
  2.8 38.7 %all-to-all-start = ((bf16[8,3,128,256]{3,2,1,0:T(8,128)(2,1)}), bf16[8,3,128,256]{3,2,1,0:T(8,128)(2,1)S(1)}, u32[]{:S(2)}, u32[]{:S(2)}) async-start(bf16[8,3,128,256]{3,2,1,0:T(8,128)(2,1)} %get-tuple-element.20), calls=%async_computation | async-start | bytes 3145728 | tf_op jit(solution)/shard_map/all_to_all | solution.py:200
  8.4 64.6 %collective-permute-start = (bf16[2,1024,256]{2,1,0:T(8,128)(2,1)}, bf16[2,1024,256]{2,1,0:T(8,128)(2,1)}, u32[]{:S(2)}, u32[]{:S(2)}) collective-permute-start(bf16[2,1024,256]{2,1,0:T(8,128)(2,1)} %get-tuple-element.21), channel_id=1, source_target_pairs={{0,2},{2,4},{4,6},{6,8},{8,10},{10,12},{12,14},{1,3},{3,5},{5,7},{... | collective-permute-start | bytes 3145736 | tf_op jit(solution)/shard_map/ppermute | solution.py:19
  46.1 9.1 %slice-start = ((bf16[2,1024,256]{2,1,0:T(8,128)(2,1)}), bf16[1,1024,256]{2,1,0:T(8,128)(2,1)S(1)}, s32[]{:S(2)}) async-start(bf16[2,1024,256]{2,1,0:T(8,128)(2,1)} %kp_ref.1), calls=%async_computation.2 | async-start | bytes 1048576 | tf_op jit(solution)/shard_map/slice | solution.py:209
  47.3 8.9 %copy-start = (bf16[2,1024,256]{2,1,0:T(8,128)(2,1)S(1)}, bf16[2,1024,256]{2,1,0:T(8,128)(2,1)}, u32[]{:S(2)}) copy-start(bf16[2,1024,256]{2,1,0:T(8,128)(2,1)} %vp_ref.1) | copy-start | bytes 3145732
  47.3 8.9 %copy-start.1 = (bf16[2,1024,256]{2,1,0:T(8,128)(2,1)S(1)}, bf16[2,1024,256]{2,1,0:T(8,128)(2,1)}, u32[]{:S(2)}) copy-start(bf16[2,1024,256]{2,1,0:T(8,128)(2,1)} %q_ref.1) | copy-start | bytes 3145732
  47.3 34.8 %all-to-all-start.1 = ((bf16[8,128,256]{1,2,0:T(8,128)(2,1)}), bf16[8,128,256]{1,2,0:T(8,128)(2,1)S(1)}, u32[]{:S(2)}, u32[]{:S(2)}) async-start(bf16[8,128,256]{1,2,0:T(8,128)(2,1)} %bitcast.26), calls=%async_computation.1 | async-start | bytes 1048576 | tf_op jit(solution)/shard_map/all_to_all | solution.py:204

commit v18 on v15

--- a/solution.py
+++ b/solution.py
@@ -10,7 +10,7 @@
 
 DH = 128
 STRIDE = 1024
-QUERY_TILE = 256
+QUERY_TILE = 1024
 
 
 def shifted(block, axis, distance):

time: 82.5 us -> 85.1 us (1.032)
  Pallas kernels: 10.9 us -> 13.5 us
    pallas_call x1, Pallas kernels: 8.04 us -> 10.6 us  [attend_rows(): pl.pallas_call(row_kernel, out_shape=jax.ShapeDtypeStruct((2, tokens, wid...]
  transfers between devices with their start and end apart: 3 -> 3, of which waited for: 2 -> 2; matrix products, arithmetic and copies ran while one was open for 9% -> 9% of each run, Pallas kernels for 10% -> 13%
where the time goes in v18:
time: 85.1 us; the launch traced here: 84.7 us
  waiting for transfers between devices  45.9 us (54%)
  starting transfers between devices  16.5 us (19%)
  Pallas kernels  13.5 us (16%)
  local copies, waits for them, and re-layouts  6.78 us (8%)
  matrix products  1.18 us (1%)
    all_to_all x1, waiting for transfers between devices, local(): lax.all_to_all(stacked, 'seq', split_axis=0, concat_axis=0, tiled=True)  30 us
    ppermute x1, waiting for transfers between devices, shifted(): return lax.ppermute(block, axis, route)  15.8 us
    pallas_call x1, Pallas kernels, attend_rows(): pl.pallas_call(row_kernel, out_shape=jax.ShapeDtypeStruct((2, tokens, wid...  10.6 us
    all_to_all x1, starting transfers between devices, local(): lax.all_to_all(result.reshape(blocks, width, feature_width), 'seq', split...  7.85 us
    all_to_all x1, starting transfers between devices, local(): lax.all_to_all(stacked, 'seq', split_axis=0, concat_axis=0, tiled=True)  5.58 us
    ppermute x1, starting transfers between devices, shifted(): return lax.ppermute(block, axis, route)  3.08 us
    pallas_call x1, Pallas kernels, pack(): pl.pallas_call(pack_kernel, out_shape=(jax.ShapeDtypeStruct((blocks, 3, s...  2.85 us
  transfers between devices with their start and end apart: 3, of which 2 were waited for; matrix products, arithmetic and copies ran while one was open for 9% of the time, Pallas kernels for 13%

profile of v18, /device:TPU:17, one launch (start us, length us, event | category | flops | bytes accessed | tf_op | source)
XLA Modules:
  0.0 84.7 jit_solution(4694046573558035935)
XLA Ops:
  0.0 2.8 %shard_map.37 = (bf16[8,3,128,256]{3,2,1,0:T(8,128)(2,1)}, bf16[2,1024,256]{2,1,0:T(8,128)(2,1)}) custom-call(bf16[2,1024,256]{2,1,0:T(8,128)(2,1)} %q_ref.1, bf16[2,1024,256]{2,1,0:T(8,128)(2,1)} %kp_ref.1, bf16[2,1024,256]{2,1,0:T(8,128)(2,1)} %vp_ref.1, bf16[2,1024,256]{2,1,0:T(8,128)(2,1)} %kp_ref.1, bf16[2,1024,256]{2,1,0:T(8,128)(2,1)} %vp_ref.1), custom_call_target="tpu_custom_call" | custom-call | tf_op jit(solution)/shard_map/pallas_call | solution.py:129
  2.8 5.6 %all-to-all-start = ((bf16[8,3,128,256]{3,2,1,0:T(8,128)(2,1)}), bf16[8,3,128,256]{3,2,1,0:T(8,128)(2,1)S(1)}, u32[]{:S(2)}, u32[]{:S(2)}) async-start(bf16[8,3,128,256]{3,2,1,0:T(8,128)(2,1)} %get-tuple-element.20), calls=%async_computation | async-start | bytes 3145728 | tf_op jit(solution)/shard_map/all_to_all | solution.py:165
  8.4 3.1 %collective-permute-start = (bf16[2,1024,256]{2,1,0:T(8,128)(2,1)}, bf16[2,1024,256]{2,1,0:T(8,128)(2,1)}, u32[]{:S(2)}, u32[]{:S(2)}) collective-permute-start(bf16[2,1024,256]{2,1,0:T(8,128)(2,1)} %get-tuple-element.21), channel_id=1, source_target_pairs={{0,2},{2,4},{4,6},{6,8},{8,10},{10,12},{12,14},{1,3},{3,5},{5,7},{... | collective-permute-start | bytes 3145736 | tf_op jit(solution)/shard_map/ppermute | solution.py:19
  11.5 30.0 %all-to-all-done = bf16[8,3,128,256]{3,2,1,0:T(8,128)(2,1)S(1)} async-done(((bf16[8,3,128,256]{3,2,1,0:T(8,128)(2,1)}), bf16[8,3,128,256]{3,2,1,0:T(8,128)(2,1)S(1)}, u32[]{:S(2)}, u32[]{:S(2)}) %all-to-all-start) | async-done | bytes 1572896 | tf_op jit(solution)/shard_map/all_to_all | solution.py:165
  41.6 0.4 reshape.60
  42.0 1.2 %fusion.11 = (bf16[8,1,128,2,128]{4,3,2,1,0:T(2,128)(2,1)S(1)}, bf16[8,1,128,2,128]{4,3,2,1,0:T(2,128)(2,1)S(1)}, bf16[8,1,128,2,128]{4,3,2,1,0:T(2,128)(2,1)S(1)}) fusion(bf16[8,3,128,2,128]{4,3,2,1,0:T(2,128)(2,1)S(1)} %reshape.60), kind=kLoop, calls=%fused_computation.21 | loop fusion | bytes 3145728 | tf_op jit(solution)/shard_map/slice | solution.py:168
  43.2 0.7 fusion.4
  43.9 0.4 copy.20
  44.3 0.8 fusion.12
  45.1 0.4 copy.21
  45.6 0.5 fusion.1
  46.1 0.0 slice-start
  46.1 1.2 %copy.22 = bf16[8,128,2,128]{1,3,2,0:T(8,128)(2,1)} copy(bf16[8,128,2,128]{3,0,2,1:T(8,128)(2,1)S(1)} %fusion.1) | data formatting | bytes 1048576 | tf_op jit(solution)/shard_map/convert_element_type | solution.py:38
  47.3 7.8 %all-to-all-start.1 = ((bf16[8,128,256]{1,2,0:T(8,128)(2,1)}), bf16[8,128,256]{1,2,0:T(8,128)(2,1)S(1)}, u32[]{:S(2)}, u32[]{:S(2)}) async-start(bf16[8,128,256]{1,2,0:T(8,128)(2,1)} %bitcast.26), calls=%async_computation.1 | async-start | bytes 1048576 | tf_op jit(solution)/shard_map/all_to_all | solution.py:169
  55.2 0.0 slice-done
  55.2 1.0 %copy.24 = bf16[1,1024,256]{1,2,0:T(8,128)(2,1)} copy(bf16[1,1024,256]{2,1,0:T(8,128)(2,1)S(1)} %slice-done) | data formatting | bytes 1048576
  56.2 0.0 copy-done
  56.2 0.0 copy-done.1
  56.2 1.0 %slice_bitcast_fusion = (bf16[1024,256]{1,0:T(8,128)(2,1)}, bf16[1024,256]{1,0:T(8,128)(2,1)}) fusion(bf16[2,1024,256]{2,1,0:T(8,128)(2,1)S(1)} %copy-done, bf16[2,1024,256]{2,1,0:T(8,128)(2,1)S(1)} %copy-done.1), kind=kLoop, calls=%fused_computation.10 | loop fusion | bytes 2097152 | tf_op jit(solution)/shard_map/squeeze | solution.py:174
  57.2 15.8 %collective-permute-done.refs_1_.refs_3_ = bf16[2,1024,256]{2,1,0:T(8,128)(2,1)} collective-permute-done((bf16[2,1024,256]{2,1,0:T(8,128)(2,1)}, bf16[2,1024,256]{2,1,0:T(8,128)(2,1)}, u32[]{:S(2)}, u32[]{:S(2)}) %collective-permute-start) | collective-permute-done | bytes 1048608 | tf_op jit(solution)/shard_map/ppermute | solution.py:19
  73.0 10.6 %shard_map.38 = bf16[2,1024,256]{2,1,0:T(8,128)(2,1)} custom-call(s32[1]{0:T(128)} %bitcast.flag_ref, bf16[1024,256]{1,0:T(8,128)(2,1)} %get-tuple-element.29.refs_0_, bf16[2,1024,256]{2,1,0:T(8,128)(2,1)} %collective-permute-done.refs_1_.refs_3_, bf16[256,1024]{1,0:T(8,128)(2,1)} %bitcast.28, bf16[2,1024,256]{2,1,0:T(8,128)(2,1)} %collective-permute-done.refs_1_.refs_3_, ...), custom_call_target="tpu_custom_call" | custom-call | flops 2147483648 | bytes 3145728 | tf_op jit(solution)/shard_map/pallas_call | solution.py:99
  83.7 0.0 all-to-all-done.1
  83.7 0.2 copy.23
  83.9 0.8 bitcast_dynamic-update-slice_fusion
  (4 shorter events, 0.0 us)
Async XLA Ops:
  2.8 38.7 %all-to-all-start = ((bf16[8,3,128,256]{3,2,1,0:T(8,128)(2,1)}), bf16[8,3,128,256]{3,2,1,0:T(8,128)(2,1)S(1)}, u32[]{:S(2)}, u32[]{:S(2)}) async-start(bf16[8,3,128,256]{3,2,1,0:T(8,128)(2,1)} %get-tuple-element.20), calls=%async_computation | async-start | bytes 3145728 | tf_op jit(solution)/shard_map/all_to_all | solution.py:165
  8.4 64.6 %collective-permute-start = (bf16[2,1024,256]{2,1,0:T(8,128)(2,1)}, bf16[2,1024,256]{2,1,0:T(8,128)(2,1)}, u32[]{:S(2)}, u32[]{:S(2)}) collective-permute-start(bf16[2,1024,256]{2,1,0:T(8,128)(2,1)} %get-tuple-element.21), channel_id=1, source_target_pairs={{0,2},{2,4},{4,6},{6,8},{8,10},{10,12},{12,14},{1,3},{3,5},{5,7},{... | collective-permute-start | bytes 3145736 | tf_op jit(solution)/shard_map/ppermute | solution.py:19
  46.1 9.1 %slice-start = ((bf16[2,1024,256]{2,1,0:T(8,128)(2,1)}), bf16[1,1024,256]{2,1,0:T(8,128)(2,1)S(1)}, s32[]{:S(2)}) async-start(bf16[2,1024,256]{2,1,0:T(8,128)(2,1)} %kp_ref.1), calls=%async_computation.2 | async-start | bytes 1048576 | tf_op jit(solution)/shard_map/slice | solution.py:174
  47.3 8.9 %copy-start = (bf16[2,1024,256]{2,1,0:T(8,128)(2,1)S(1)}, bf16[2,1024,256]{2,1,0:T(8,128)(2,1)}, u32[]{:S(2)}) copy-start(bf16[2,1024,256]{2,1,0:T(8,128)(2,1)} %vp_ref.1) | copy-start | bytes 3145732
  47.3 8.9 %copy-start.1 = (bf16[2,1024,256]{2,1,0:T(8,128)(2,1)S(1)}, bf16[2,1024,256]{2,1,0:T(8,128)(2,1)}, u32[]{:S(2)}) copy-start(bf16[2,1024,256]{2,1,0:T(8,128)(2,1)} %q_ref.1) | copy-start | bytes 3145732
  47.3 36.4 %all-to-all-start.1 = ((bf16[8,128,256]{1,2,0:T(8,128)(2,1)}), bf16[8,128,256]{1,2,0:T(8,128)(2,1)S(1)}, u32[]{:S(2)}, u32[]{:S(2)}) async-start(bf16[8,128,256]{1,2,0:T(8,128)(2,1)} %bitcast.26), calls=%async_computation.1 | async-start | bytes 1048576 | tf_op jit(solution)/shard_map/all_to_all | solution.py:169

commit v19 on v14

--- a/solution.py
+++ b/solution.py
@@ -42,27 +42,20 @@
     score_scale = 1.0 / math.sqrt(DH)
     dims = (((1,), (1,)), ((), ()))
     tq = QUERY_TILE
-    upper = lax.broadcasted_iota(jnp.int32, (tq, tq), 1) > lax.broadcasted_iota(
-        jnp.int32, (tq, tq), 0
-    )
-
-    def scores(q, k_ref, low, high):
-        return lax.dot_general(q, k_ref[low:high, :], dims, preferred_element_type=jnp.float32)
-
-    def scores_t(q, kt_ref, low, high):
-        return jnp.dot(q, kt_ref[:, low:high], preferred_element_type=jnp.float32)
 
     for tile in range(STRIDE // tq):
         low, high = tile * tq, (tile + 1) * tq
         q = q_ref[low:high, :]
         parts = []
         if with_prev:
-            parts.append((jnp.where(upper, scores(q, kp_ref, low, high), -jnp.inf), vp_ref, low, high))
-            if high < STRIDE:
-                parts.append((scores(q, kp_ref, high, STRIDE), vp_ref, high, STRIDE))
-        if low > 0:
-            parts.append((scores_t(q, kc_ref, 0, low), vc_ref, 0, low))
-        parts.append((jnp.where(upper, -jnp.inf, scores_t(q, kc_ref, low, high)), vc_ref, low, high))
+            s = lax.dot_general(q, kp_ref[low:, :], dims, preferred_element_type=jnp.float32)
+            shape = (tq, STRIDE - low)
+            ok = lax.broadcasted_iota(jnp.int32, shape, 1) > lax.broadcasted_iota(jnp.int32, shape, 0)
+            parts.append((jnp.where(ok, s, -jnp.inf), vp_ref[low:, :]))
+        s = jnp.dot(q, kc_ref[:, :high], preferred_element_type=jnp.float32)
+        shape = (tq, high)
+        ok = lax.broadcasted_iota(jnp.int32, shape, 1) <= lax.broadcasted_iota(jnp.int32, shape, 0) + low
+        parts.append((jnp.where(ok, s, -jnp.inf), vc_ref[:high, :]))
         maxima = functools.reduce(
             jnp.maximum, [jnp.max(p[0], axis=1, keepdims=True) for p in parts]
         )
@@ -70,8 +63,8 @@
         total = functools.reduce(jnp.add, [jnp.sum(e, axis=1, keepdims=True) for e in expos])
         inverse = 1.0 / total
         out = None
-        for e, (_, v_ref, a, b) in zip(expos, parts):
-            term = jnp.dot((e * inverse).astype(jnp.bfloat16), v_ref[a:b, :], preferred_element_type=jnp.float32)
+        for e, (_, v) in zip(expos, parts):
+            term = jnp.dot((e * inverse).astype(jnp.bfloat16), v, preferred_element_type=jnp.float32)
             out = term if out is None else out + term
         o_ref[low:high, :] = out.astype(o_ref.dtype)
 

time: 82.2 us -> 82.2 us (level)
  transfers between devices with their start and end apart: 3 -> 3, of which waited for: 2 -> 2; matrix products, arithmetic and copies ran while one was open for 9% -> 9% of each run, Pallas kernels for 9% -> 10%
where the time goes in v19:
time: 82.2 us; the launch traced here: 81.9 us
  waiting for transfers between devices  45.9 us (56%)
  starting transfers between devices  16.5 us (20%)
  Pallas kernels  10.6 us (13%)
  local copies, waits for them, and re-layouts  6.78 us (8%)
  matrix products  1.18 us (1%)
  other arithmetic  0.84 us (1%)
    all_to_all x1, waiting for transfers between devices, local(): lax.all_to_all(stacked, 'seq', split_axis=0, concat_axis=0, tiled=True)  30 us
    ppermute x1, waiting for transfers between devices, shifted(): return lax.ppermute(block, axis, route)  15.8 us
    all_to_all x1, starting transfers between devices, local(): lax.all_to_all(result.reshape(blocks, width, feature_width), 'seq', split...  7.85 us
    pallas_call x1, Pallas kernels, attend_rows(): pl.pallas_call(row_kernel, out_shape=jax.ShapeDtypeStruct((2, tokens, wid...  7.78 us
    all_to_all x1, starting transfers between devices, local(): lax.all_to_all(stacked, 'seq', split_axis=0, concat_axis=0, tiled=True)  5.58 us
    ppermute x1, starting transfers between devices, shifted(): return lax.ppermute(block, axis, route)  3.08 us
    pallas_call x1, Pallas kernels, pack(): pl.pallas_call(pack_kernel, out_shape=(jax.ShapeDtypeStruct((blocks, 3, s...  2.85 us
  transfers between devices with their start and end apart: 3, of which 2 were waited for; matrix products, arithmetic and copies ran while one was open for 9% of the time, Pallas kernels for 10%

profile of v19, /device:TPU:17, one launch (start us, length us, event | category | flops | bytes accessed | tf_op | source)
XLA Modules:
  0.0 81.9 jit_solution(13015119126762522345)
XLA Ops:
  0.0 2.8 %shard_map.37 = (bf16[8,3,128,256]{3,2,1,0:T(8,128)(2,1)}, bf16[2,1024,256]{2,1,0:T(8,128)(2,1)}) custom-call(bf16[2,1024,256]{2,1,0:T(8,128)(2,1)} %q_ref.1, bf16[2,1024,256]{2,1,0:T(8,128)(2,1)} %kp_ref.1, bf16[2,1024,256]{2,1,0:T(8,128)(2,1)} %vp_ref.1, bf16[2,1024,256]{2,1,0:T(8,128)(2,1)} %kp_ref.1, bf16[2,1024,256]{2,1,0:T(8,128)(2,1)} %vp_ref.1), custom_call_target="tpu_custom_call" | custom-call | tf_op jit(solution)/shard_map/pallas_call | solution.py:122
  2.8 5.6 %all-to-all-start = ((bf16[8,3,128,256]{3,2,1,0:T(8,128)(2,1)}), bf16[8,3,128,256]{3,2,1,0:T(8,128)(2,1)S(1)}, u32[]{:S(2)}, u32[]{:S(2)}) async-start(bf16[8,3,128,256]{3,2,1,0:T(8,128)(2,1)} %get-tuple-element.20), calls=%async_computation | async-start | bytes 3145728 | tf_op jit(solution)/shard_map/all_to_all | solution.py:158
  8.4 3.1 %collective-permute-start = (bf16[2,1024,256]{2,1,0:T(8,128)(2,1)}, bf16[2,1024,256]{2,1,0:T(8,128)(2,1)}, u32[]{:S(2)}, u32[]{:S(2)}) collective-permute-start(bf16[2,1024,256]{2,1,0:T(8,128)(2,1)} %get-tuple-element.21), channel_id=1, source_target_pairs={{0,2},{2,4},{4,6},{6,8},{8,10},{10,12},{12,14},{1,3},{3,5},{5,7},{... | collective-permute-start | bytes 3145736 | tf_op jit(solution)/shard_map/ppermute | solution.py:19
  11.5 30.0 %all-to-all-done = bf16[8,3,128,256]{3,2,1,0:T(8,128)(2,1)S(1)} async-done(((bf16[8,3,128,256]{3,2,1,0:T(8,128)(2,1)}), bf16[8,3,128,256]{3,2,1,0:T(8,128)(2,1)S(1)}, u32[]{:S(2)}, u32[]{:S(2)}) %all-to-all-start) | async-done | bytes 1572896 | tf_op jit(solution)/shard_map/all_to_all | solution.py:158
  41.6 0.4 reshape.60
  42.0 1.2 %fusion.11 = (bf16[8,1,128,2,128]{4,3,2,1,0:T(2,128)(2,1)S(1)}, bf16[8,1,128,2,128]{4,3,2,1,0:T(2,128)(2,1)S(1)}, bf16[8,1,128,2,128]{4,3,2,1,0:T(2,128)(2,1)S(1)}) fusion(bf16[8,3,128,2,128]{4,3,2,1,0:T(2,128)(2,1)S(1)} %reshape.60), kind=kLoop, calls=%fused_computation.21 | loop fusion | bytes 3145728 | tf_op jit(solution)/shard_map/slice | solution.py:161
  43.2 0.7 fusion.4
  43.9 0.4 copy.20
  44.3 0.8 fusion.12
  45.1 0.4 copy.21
  45.6 0.5 fusion.1
  46.1 0.0 slice-start
  46.1 1.2 %copy.22 = bf16[8,128,2,128]{1,3,2,0:T(8,128)(2,1)} copy(bf16[8,128,2,128]{3,0,2,1:T(8,128)(2,1)S(1)} %fusion.1) | data formatting | bytes 1048576 | tf_op jit(solution)/shard_map/convert_element_type | solution.py:38
  47.3 7.8 %all-to-all-start.1 = ((bf16[8,128,256]{1,2,0:T(8,128)(2,1)}), bf16[8,128,256]{1,2,0:T(8,128)(2,1)S(1)}, u32[]{:S(2)}, u32[]{:S(2)}) async-start(bf16[8,128,256]{1,2,0:T(8,128)(2,1)} %bitcast.26), calls=%async_computation.1 | async-start | bytes 1048576 | tf_op jit(solution)/shard_map/all_to_all | solution.py:162
  55.2 0.0 slice-done
  55.2 1.0 %copy.24 = bf16[1,1024,256]{1,2,0:T(8,128)(2,1)} copy(bf16[1,1024,256]{2,1,0:T(8,128)(2,1)S(1)} %slice-done) | data formatting | bytes 1048576
  56.2 0.0 copy-done
  56.2 0.0 copy-done.1
  56.2 1.0 %slice_bitcast_fusion = (bf16[1024,256]{1,0:T(8,128)(2,1)}, bf16[1024,256]{1,0:T(8,128)(2,1)}) fusion(bf16[2,1024,256]{2,1,0:T(8,128)(2,1)S(1)} %copy-done, bf16[2,1024,256]{2,1,0:T(8,128)(2,1)S(1)} %copy-done.1), kind=kLoop, calls=%fused_computation.10 | loop fusion | bytes 2097152 | tf_op jit(solution)/shard_map/squeeze | solution.py:167
  57.2 15.8 %collective-permute-done.refs_1_.refs_3_ = bf16[2,1024,256]{2,1,0:T(8,128)(2,1)} collective-permute-done((bf16[2,1024,256]{2,1,0:T(8,128)(2,1)}, bf16[2,1024,256]{2,1,0:T(8,128)(2,1)}, u32[]{:S(2)}, u32[]{:S(2)}) %collective-permute-start) | collective-permute-done | bytes 1048608 | tf_op jit(solution)/shard_map/ppermute | solution.py:19
  73.0 7.8 %shard_map.38 = bf16[2,1024,256]{2,1,0:T(8,128)(2,1)} custom-call(s32[1]{0:T(128)} %bitcast.flag_ref, bf16[1024,256]{1,0:T(8,128)(2,1)} %get-tuple-element.29.refs_0_, bf16[2,1024,256]{2,1,0:T(8,128)(2,1)} %collective-permute-done.refs_1_.refs_3_, bf16[256,1024]{1,0:T(8,128)(2,1)} %bitcast.28, bf16[2,1024,256]{2,1,0:T(8,128)(2,1)} %collective-permute-done.refs_1_.refs_3_, ...), custom_call_target="tpu_custom_call" | custom-call | flops 1610612736 | bytes 3145728 | tf_op jit(solution)/shard_map/pallas_call | solution.py:92
  80.8 0.0 all-to-all-done.1
  80.8 0.2 copy.23
  81.0 0.8 %bitcast_dynamic-update-slice_fusion = bf16[2,1024,256]{2,1,0:T(8,128)(2,1)} fusion(bf16[2,1024,256]{2,1,0:T(8,128)(2,1)} %shard_map.38, bf16[1,1024,256]{2,1,0:T(8,128)(2,1)S(1)} %bitcast.27), kind=kLoop, calls=%fused_computation.9 | loop fusion | bytes 1048576 | tf_op jit(solution)/shard_map/scatter | solution.py:168
  (4 shorter events, 0.0 us)
Async XLA Ops:
  2.8 38.7 %all-to-all-start = ((bf16[8,3,128,256]{3,2,1,0:T(8,128)(2,1)}), bf16[8,3,128,256]{3,2,1,0:T(8,128)(2,1)S(1)}, u32[]{:S(2)}, u32[]{:S(2)}) async-start(bf16[8,3,128,256]{3,2,1,0:T(8,128)(2,1)} %get-tuple-element.20), calls=%async_computation | async-start | bytes 3145728 | tf_op jit(solution)/shard_map/all_to_all | solution.py:158
  8.4 64.6 %collective-permute-start = (bf16[2,1024,256]{2,1,0:T(8,128)(2,1)}, bf16[2,1024,256]{2,1,0:T(8,128)(2,1)}, u32[]{:S(2)}, u32[]{:S(2)}) collective-permute-start(bf16[2,1024,256]{2,1,0:T(8,128)(2,1)} %get-tuple-element.21), channel_id=1, source_target_pairs={{0,2},{2,4},{4,6},{6,8},{8,10},{10,12},{12,14},{1,3},{3,5},{5,7},{... | collective-permute-start | bytes 3145736 | tf_op jit(solution)/shard_map/ppermute | solution.py:19
  46.1 9.1 %slice-start = ((bf16[2,1024,256]{2,1,0:T(8,128)(2,1)}), bf16[1,1024,256]{2,1,0:T(8,128)(2,1)S(1)}, s32[]{:S(2)}) async-start(bf16[2,1024,256]{2,1,0:T(8,128)(2,1)} %kp_ref.1), calls=%async_computation.2 | async-start | bytes 1048576 | tf_op jit(solution)/shard_map/slice | solution.py:167
  47.3 8.9 %copy-start = (bf16[2,1024,256]{2,1,0:T(8,128)(2,1)S(1)}, bf16[2,1024,256]{2,1,0:T(8,128)(2,1)}, u32[]{:S(2)}) copy-start(bf16[2,1024,256]{2,1,0:T(8,128)(2,1)} %vp_ref.1) | copy-start | bytes 3145732
  47.3 8.9 %copy-start.1 = (bf16[2,1024,256]{2,1,0:T(8,128)(2,1)S(1)}, bf16[2,1024,256]{2,1,0:T(8,128)(2,1)}, u32[]{:S(2)}) copy-start(bf16[2,1024,256]{2,1,0:T(8,128)(2,1)} %q_ref.1) | copy-start | bytes 3145732
  47.3 33.5 %all-to-all-start.1 = ((bf16[8,128,256]{1,2,0:T(8,128)(2,1)}), bf16[8,128,256]{1,2,0:T(8,128)(2,1)S(1)}, u32[]{:S(2)}, u32[]{:S(2)}) async-start(bf16[8,128,256]{1,2,0:T(8,128)(2,1)} %bitcast.26), calls=%async_computation.1 | async-start | bytes 1048576 | tf_op jit(solution)/shard_map/all_to_all | solution.py:162

commit v20 on v14

--- a/solution.py
+++ b/solution.py
@@ -21,21 +21,20 @@
 
 def attend_columns(query_cols, key_cols, value_cols):
     score_scale = 1.0 / math.sqrt(DH)
-    scores = (
-        jnp.einsum("rchd,schd->chrs", query_cols, key_cols, preferred_element_type=jnp.float32)
-        * score_scale
+    queries = query_cols.astype(jnp.float32)
+    keys = key_cols.astype(jnp.float32)
+    scores = jnp.sum(queries[:, None] * keys[None, :], axis=-1) * score_scale
+    count = query_cols.shape[0]
+    row_pos = jnp.arange(count, dtype=jnp.int32)[:, None, None, None]
+    other_pos = jnp.arange(count, dtype=jnp.int32)[None, :, None, None]
+    scores = jnp.where(other_pos <= row_pos, scores, -jnp.inf)
+    maxima = jnp.max(scores, axis=1, keepdims=True)
+    expo = jnp.exp(scores - maxima)
+    weights = (expo / jnp.sum(expo, axis=1, keepdims=True)).astype(jnp.bfloat16)
+    out = jnp.sum(
+        weights.astype(jnp.float32)[..., None] * value_cols.astype(jnp.float32)[None], axis=1
     )
-    count = query_cols.shape[0]
-    row_pos = jnp.arange(count, dtype=jnp.int32)[:, None]
-    other_pos = jnp.arange(count, dtype=jnp.int32)[None, :]
-    allowed = other_pos <= row_pos
-    scores = jnp.where(allowed[None, None], scores, -jnp.inf)
-    maxima = jnp.max(scores, axis=-1, keepdims=True)
-    expo = jnp.exp(scores - maxima)
-    weights = (expo / jnp.sum(expo, axis=-1, keepdims=True)).astype(jnp.bfloat16)
-    return jnp.einsum(
-        "chrs,schd->rchd", weights, value_cols, preferred_element_type=jnp.float32
-    ).astype(jnp.bfloat16)
+    return out.astype(jnp.bfloat16)
 
 
 def row_tiles(with_prev, q_ref, kp_ref, kc_ref, vp_ref, vc_ref, o_ref):

time: 82.2 us -> 82.1 us (level)
  other arithmetic: 0.84 us -> 6.53 us
  waiting for transfers between devices: 45.9 us -> 43.2 us
  local copies, waits for them, and re-layouts: 6.78 us -> 4.85 us
  matrix products: 1.18 us -> 0 us
    reduce_sum x0 -> x3, other arithmetic: none -> 5.12 us  [the longest x1 2.62 us: attend_columns(): jnp.sum(weights.astype(jnp.float32)[..., None] * value_cols.astype(jnp.fl...]
    ppermute x1, waiting for transfers between devices: 15.8 us -> 13.1 us  [shifted(): return lax.ppermute(block, axis, route)]
    slice x1 -> x0, local copies, waits for them, and re-layouts: 1.18 us -> none  [local(): result = attend_columns(grid[:, 0], grid[:, 1], grid[:, 2])]
    dot_general x2 -> x0, matrix products: 1.18 us -> none  [the longest x1 0.69 us: attend_columns(): jnp.einsum('rchd,schd->chrs', query_cols, key_cols, preferred_element_typ...]
    mul x0 -> x1, other arithmetic: none -> 1.12 us  [attend_columns(): scores = jnp.sum(queries[:, None] * keys[None, :], axis=-1) * score_scale]
    convert_element_type x2 -> x3, local copies, waits for them, and re-layouts: 1.65 us -> 1.21 us  [the longest x1 1 us: attend_columns(): return out.astype(jnp.bfloat16)]
  transfers between devices with their start and end apart: 3 -> 3, of which waited for: 2 -> 2; matrix products, arithmetic and copies ran while one was open for 9% -> 13% of each run, Pallas kernels for 9% -> 9%
where the time goes in v20:
time: 82.1 us; the launch traced here: 81.8 us
  waiting for transfers between devices  43.2 us (53%)
  starting transfers between devices  16.5 us (20%)
  Pallas kernels  10.6 us (13%)
  other arithmetic  6.53 us (8%)
  local copies, waits for them, and re-layouts  4.85 us (6%)
    all_to_all x1, waiting for transfers between devices, local(): lax.all_to_all(stacked, 'seq', split_axis=0, concat_axis=0, tiled=True)  30 us
    ppermute x1, waiting for transfers between devices, shifted(): return lax.ppermute(block, axis, route)  13.1 us
    all_to_all x1, starting transfers between devices, local(): lax.all_to_all(result.reshape(blocks, width, feature_width), 'seq', split...  7.85 us
    pallas_call x1, Pallas kernels, attend_rows(): pl.pallas_call(row_kernel, out_shape=jax.ShapeDtypeStruct((2, tokens, wid...  7.74 us
    all_to_all x1, starting transfers between devices, local(): lax.all_to_all(stacked, 'seq', split_axis=0, concat_axis=0, tiled=True)  5.58 us
    ppermute x1, starting transfers between devices, shifted(): return lax.ppermute(block, axis, route)  3.08 us
    pallas_call x1, Pallas kernels, pack(): pl.pallas_call(pack_kernel, out_shape=(jax.ShapeDtypeStruct((blocks, 3, s...  2.85 us
    reduce_sum x1, other arithmetic, attend_columns(): jnp.sum(weights.astype(jnp.float32)[..., None] * value_cols.astype(jnp.fl...  2.62 us
  transfers between devices with their start and end apart: 3, of which 2 were waited for; matrix products, arithmetic and copies ran while one was open for 13% of the time, Pallas kernels for 9%

profile of v20, /device:TPU:17, one launch (start us, length us, event | category | flops | bytes accessed | tf_op | source)
XLA Modules:
  0.0 81.8 jit_solution(9578795945195940426)
XLA Ops:
  0.0 2.8 %shard_map.37 = (bf16[8,3,128,256]{3,2,1,0:T(8,128)(2,1)}, bf16[2,1024,256]{2,1,0:T(8,128)(2,1)}) custom-call(bf16[2,1024,256]{2,1,0:T(8,128)(2,1)} %q_ref.1, bf16[2,1024,256]{2,1,0:T(8,128)(2,1)} %kp_ref.1, bf16[2,1024,256]{2,1,0:T(8,128)(2,1)} %vp_ref.1, bf16[2,1024,256]{2,1,0:T(8,128)(2,1)} %kp_ref.1, bf16[2,1024,256]{2,1,0:T(8,128)(2,1)} %vp_ref.1), custom_call_target="tpu_custom_call" | custom-call | tf_op jit(solution)/shard_map/pallas_call | solution.py:128
  2.8 5.6 %all-to-all-start = ((bf16[8,3,128,256]{3,2,1,0:T(8,128)(2,1)}), bf16[8,3,128,256]{3,2,1,0:T(8,128)(2,1)S(1)}, u32[]{:S(2)}, u32[]{:S(2)}) async-start(bf16[8,3,128,256]{3,2,1,0:T(8,128)(2,1)} %get-tuple-element.20), calls=%async_computation | async-start | bytes 3145728 | tf_op jit(solution)/shard_map/all_to_all | solution.py:164
  8.4 3.1 %collective-permute-start = (bf16[2,1024,256]{2,1,0:T(8,128)(2,1)}, bf16[2,1024,256]{2,1,0:T(8,128)(2,1)}, u32[]{:S(2)}, u32[]{:S(2)}) collective-permute-start(bf16[2,1024,256]{2,1,0:T(8,128)(2,1)} %get-tuple-element.21), channel_id=1, source_target_pairs={{0,2},{2,4},{4,6},{6,8},{8,10},{10,12},{12,14},{1,3},{3,5},{5,7},{... | collective-permute-start | bytes 3145736 | tf_op jit(solution)/shard_map/ppermute | solution.py:19
  11.5 30.0 %all-to-all-done = bf16[8,3,128,256]{3,2,1,0:T(8,128)(2,1)S(1)} async-done(((bf16[8,3,128,256]{3,2,1,0:T(8,128)(2,1)}), bf16[8,3,128,256]{3,2,1,0:T(8,128)(2,1)S(1)}, u32[]{:S(2)}, u32[]{:S(2)}) %all-to-all-start) | async-done | bytes 1572896 | tf_op jit(solution)/shard_map/all_to_all | solution.py:164
  41.6 0.4 reshape.86
  42.0 1.1 %fusion.2 = (f32[8,128,2,128]{3,2,1,0:T(2,128)S(1)}, f32[8,128,2,128]{3,2,1,0:T(2,128)S(1)}, f32[8,128,2,128]{3,2,1,0:T(2,128)S(1)}) fusion(bf16[8,3,128,2,128]{4,3,2,1,0:T(2,128)(2,1)S(1)} %reshape.86), kind=kLoop, calls=%fused_computation.7 | loop fusion | flops 786432 | bytes 4718592 | tf_op jit(solution)/shard_map/mul | solution.py:26
  43.1 0.1 copy.13
  43.2 0.1 copy.12
  43.3 2.3 %multiply_reduce_fusion.1 = f32[8,8,128,2]{2,3,1,0:T(2,128)S(1)} fusion(f32[8,128,2,128]{3,1,2,0:T(8,128)S(1)} %copy.13, f32[8,128,2,128]{3,1,2,0:T(8,128)S(1)} %copy.12), kind=kLoop, calls=%fused_computation.1 | loop fusion | flops 4177920 | bytes 2162688 | tf_op jit(solution)/shard_map/reduce_sum | solution.py:26
  45.7 0.1 fusion.5
  45.8 0.2 fusion.3
  46.0 0.1 fusion.4
  46.1 0.1 copy.16
  46.3 2.6 %multiply_reduce_fusion = bf16[8,128,2,128]{3,1,2,0:T(8,128)(2,1)S(1)} fusion(f32[8,128,2,128]{3,1,2,0:T(8,128)S(1)} %copy.16, f32[8,8,128,2]{2,3,1,0:T(2,128)S(1)} %fusion.4), kind=kLoop, calls=%fused_computation | loop fusion | flops 3932160 | bytes 1638400 | tf_op jit(solution)/shard_map/reduce_sum | solution.py:34
  48.9 0.0 slice-start
  48.9 1.0 %copy.17 = bf16[8,128,2,128]{1,3,2,0:T(8,128)(2,1)} copy(bf16[8,128,2,128]{3,1,2,0:T(8,128)(2,1)S(1)} %multiply_reduce_fusion) | data formatting | bytes 1048576 | tf_op jit(solution)/shard_map/convert_element_type | solution.py:37
  49.9 7.9 %all-to-all-start.1 = ((bf16[8,128,256]{1,2,0:T(8,128)(2,1)}), bf16[8,128,256]{1,2,0:T(8,128)(2,1)S(1)}, u32[]{:S(2)}, u32[]{:S(2)}) async-start(bf16[8,128,256]{1,2,0:T(8,128)(2,1)} %bitcast.29), calls=%async_computation.1 | async-start | bytes 1048576 | tf_op jit(solution)/shard_map/all_to_all | solution.py:168
  57.8 1.0 %copy.21 = bf16[1,1024,256]{1,2,0:T(8,128)(2,1)} copy(bf16[1,1024,256]{2,1,0:T(8,128)(2,1)S(1)} %slice-done) | data formatting | bytes 1048576
  58.8 1.0 %slice_bitcast_fusion.3 = (bf16[1024,256]{1,0:T(8,128)(2,1)}, bf16[1024,256]{1,0:T(8,128)(2,1)}) fusion(bf16[2,1024,256]{2,1,0:T(8,128)(2,1)S(1)} %copy-done, bf16[2,1024,256]{2,1,0:T(8,128)(2,1)S(1)} %copy-done.1), kind=kLoop, calls=%fused_computation.9 | loop fusion | bytes 2097152 | tf_op jit(solution)/shard_map/squeeze | solution.py:173
  59.8 13.1 %collective-permute-done.refs_1_.refs_3_ = bf16[2,1024,256]{2,1,0:T(8,128)(2,1)} collective-permute-done((bf16[2,1024,256]{2,1,0:T(8,128)(2,1)}, bf16[2,1024,256]{2,1,0:T(8,128)(2,1)}, u32[]{:S(2)}, u32[]{:S(2)}) %collective-permute-start) | collective-permute-done | bytes 1048608 | tf_op jit(solution)/shard_map/ppermute | solution.py:19
  73.0 7.7 %shard_map.38 = bf16[2,1024,256]{2,1,0:T(8,128)(2,1)} custom-call(s32[1]{0:T(128)} %bitcast.flag_ref, bf16[1024,256]{1,0:T(8,128)(2,1)} %get-tuple-element.27.refs_0_, bf16[2,1024,256]{2,1,0:T(8,128)(2,1)} %collective-permute-done.refs_1_.refs_3_, bf16[256,1024]{1,0:T(8,128)(2,1)} %bitcast.31, bf16[2,1024,256]{2,1,0:T(8,128)(2,1)} %collective-permute-done.refs_1_.refs_3_, ...), custom_call_target="tpu_custom_call" | custom-call | flops 1610612736 | bytes 3145728 | tf_op jit(solution)/shard_map/pallas_call | solution.py:98
  80.7 0.0 all-to-all-done.1
  80.7 0.2 copy.18
  80.9 0.8 %bitcast_dynamic-update-slice_fusion = bf16[2,1024,256]{2,1,0:T(8,128)(2,1)} fusion(bf16[2,1024,256]{2,1,0:T(8,128)(2,1)} %shard_map.38, bf16[1,1024,256]{2,1,0:T(8,128)(2,1)S(1)} %bitcast.30), kind=kLoop, calls=%fused_computation.8 | loop fusion | bytes 1048576 | tf_op jit(solution)/shard_map/scatter | solution.py:174
  (6 shorter events, 0.0 us)
Async XLA Ops:
  2.8 38.7 %all-to-all-start = ((bf16[8,3,128,256]{3,2,1,0:T(8,128)(2,1)}), bf16[8,3,128,256]{3,2,1,0:T(8,128)(2,1)S(1)}, u32[]{:S(2)}, u32[]{:S(2)}) async-start(bf16[8,3,128,256]{3,2,1,0:T(8,128)(2,1)} %get-tuple-element.20), calls=%async_computation | async-start | bytes 3145728 | tf_op jit(solution)/shard_map/all_to_all | solution.py:164
  8.4 64.5 %collective-permute-start = (bf16[2,1024,256]{2,1,0:T(8,128)(2,1)}, bf16[2,1024,256]{2,1,0:T(8,128)(2,1)}, u32[]{:S(2)}, u32[]{:S(2)}) collective-permute-start(bf16[2,1024,256]{2,1,0:T(8,128)(2,1)} %get-tuple-element.21), channel_id=1, source_target_pairs={{0,2},{2,4},{4,6},{6,8},{8,10},{10,12},{12,14},{1,3},{3,5},{5,7},{... | collective-permute-start | bytes 3145736 | tf_op jit(solution)/shard_map/ppermute | solution.py:19
  48.9 8.9 %slice-start = ((bf16[2,1024,256]{2,1,0:T(8,128)(2,1)}), bf16[1,1024,256]{2,1,0:T(8,128)(2,1)S(1)}, s32[]{:S(2)}) async-start(bf16[2,1024,256]{2,1,0:T(8,128)(2,1)} %kp_ref.1), calls=%async_computation.2 | async-start | bytes 1048576 | tf_op jit(solution)/shard_map/slice | solution.py:173
  49.9 8.9 %copy-start = (bf16[2,1024,256]{2,1,0:T(8,128)(2,1)S(1)}, bf16[2,1024,256]{2,1,0:T(8,128)(2,1)}, u32[]{:S(2)}) copy-start(bf16[2,1024,256]{2,1,0:T(8,128)(2,1)} %vp_ref.1) | copy-start | bytes 3145732
  49.9 8.9 %copy-start.1 = (bf16[2,1024,256]{2,1,0:T(8,128)(2,1)S(1)}, bf16[2,1024,256]{2,1,0:T(8,128)(2,1)}, u32[]{:S(2)}) copy-start(bf16[2,1024,256]{2,1,0:T(8,128)(2,1)} %q_ref.1) | copy-start | bytes 3145732
  49.9 30.8 %all-to-all-start.1 = ((bf16[8,128,256]{1,2,0:T(8,128)(2,1)}), bf16[8,128,256]{1,2,0:T(8,128)(2,1)S(1)}, u32[]{:S(2)}, u32[]{:S(2)}) async-start(bf16[8,128,256]{1,2,0:T(8,128)(2,1)} %bitcast.29), calls=%async_computation.1 | async-start | bytes 1048576 | tf_op jit(solution)/shard_map/all_to_all | solution.py:168

commit v21 on v19

--- a/solution.py
+++ b/solution.py
@@ -10,7 +10,7 @@
 
 DH = 128
 STRIDE = 1024
-QUERY_TILE = 512
+QUERY_TILE = 256
 
 
 def shifted(block, axis, distance):

time: 82.2 us -> 82.6 us (level)
  no operation moved by 1% of the time
where the time goes in v21:
time: 82.6 us; the launch traced here: 82.2 us
  waiting for transfers between devices  45.9 us (56%)
  starting transfers between devices  16.5 us (20%)
  Pallas kernels  11 us (13%)
  local copies, waits for them, and re-layouts  6.78 us (8%)
  matrix products  1.18 us (1%)
  other arithmetic  0.84 us (1%)
    all_to_all x1, waiting for transfers between devices, local(): lax.all_to_all(stacked, 'seq', split_axis=0, concat_axis=0, tiled=True)  30 us
    ppermute x1, waiting for transfers between devices, shifted(): return lax.ppermute(block, axis, route)  15.8 us
    pallas_call x1, Pallas kernels, attend_rows(): pl.pallas_call(row_kernel, out_shape=jax.ShapeDtypeStruct((2, tokens, wid...  8.14 us
    all_to_all x1, starting transfers between devices, local(): lax.all_to_all(result.reshape(blocks, width, feature_width), 'seq', split...  7.85 us
    all_to_all x1, starting transfers between devices, local(): lax.all_to_all(stacked, 'seq', split_axis=0, concat_axis=0, tiled=True)  5.58 us
    ppermute x1, starting transfers between devices, shifted(): return lax.ppermute(block, axis, route)  3.08 us
    pallas_call x1, Pallas kernels, pack(): pl.pallas_call(pack_kernel, out_shape=(jax.ShapeDtypeStruct((blocks, 3, s...  2.85 us
  transfers between devices with their start and end apart: 3, of which 2 were waited for; matrix products, arithmetic and copies ran while one was open for 9% of the time, Pallas kernels for 10%

profile of v21, /device:TPU:17, one launch (start us, length us, event | category | flops | bytes accessed | tf_op | source)
XLA Modules:
  0.0 82.2 jit_solution(12620264859502922549)
XLA Ops:
  0.0 2.8 %shard_map.37 = (bf16[8,3,128,256]{3,2,1,0:T(8,128)(2,1)}, bf16[2,1024,256]{2,1,0:T(8,128)(2,1)}) custom-call(bf16[2,1024,256]{2,1,0:T(8,128)(2,1)} %q_ref.1, bf16[2,1024,256]{2,1,0:T(8,128)(2,1)} %kp_ref.1, bf16[2,1024,256]{2,1,0:T(8,128)(2,1)} %vp_ref.1, bf16[2,1024,256]{2,1,0:T(8,128)(2,1)} %kp_ref.1, bf16[2,1024,256]{2,1,0:T(8,128)(2,1)} %vp_ref.1), custom_call_target="tpu_custom_call" | custom-call | tf_op jit(solution)/shard_map/pallas_call | solution.py:122
  2.8 5.6 %all-to-all-start = ((bf16[8,3,128,256]{3,2,1,0:T(8,128)(2,1)}), bf16[8,3,128,256]{3,2,1,0:T(8,128)(2,1)S(1)}, u32[]{:S(2)}, u32[]{:S(2)}) async-start(bf16[8,3,128,256]{3,2,1,0:T(8,128)(2,1)} %get-tuple-element.20), calls=%async_computation | async-start | bytes 3145728 | tf_op jit(solution)/shard_map/all_to_all | solution.py:158
  8.4 3.1 %collective-permute-start = (bf16[2,1024,256]{2,1,0:T(8,128)(2,1)}, bf16[2,1024,256]{2,1,0:T(8,128)(2,1)}, u32[]{:S(2)}, u32[]{:S(2)}) collective-permute-start(bf16[2,1024,256]{2,1,0:T(8,128)(2,1)} %get-tuple-element.21), channel_id=1, source_target_pairs={{0,2},{2,4},{4,6},{6,8},{8,10},{10,12},{12,14},{1,3},{3,5},{5,7},{... | collective-permute-start | bytes 3145736 | tf_op jit(solution)/shard_map/ppermute | solution.py:19
  11.5 30.0 %all-to-all-done = bf16[8,3,128,256]{3,2,1,0:T(8,128)(2,1)S(1)} async-done(((bf16[8,3,128,256]{3,2,1,0:T(8,128)(2,1)}), bf16[8,3,128,256]{3,2,1,0:T(8,128)(2,1)S(1)}, u32[]{:S(2)}, u32[]{:S(2)}) %all-to-all-start) | async-done | bytes 1572896 | tf_op jit(solution)/shard_map/all_to_all | solution.py:158
  41.6 0.4 reshape.60
  42.0 1.2 %fusion.11 = (bf16[8,1,128,2,128]{4,3,2,1,0:T(2,128)(2,1)S(1)}, bf16[8,1,128,2,128]{4,3,2,1,0:T(2,128)(2,1)S(1)}, bf16[8,1,128,2,128]{4,3,2,1,0:T(2,128)(2,1)S(1)}) fusion(bf16[8,3,128,2,128]{4,3,2,1,0:T(2,128)(2,1)S(1)} %reshape.60), kind=kLoop, calls=%fused_computation.21 | loop fusion | bytes 3145728 | tf_op jit(solution)/shard_map/slice | solution.py:161
  43.2 0.7 fusion.4
  43.9 0.4 copy.20
  44.3 0.8 fusion.12
  45.1 0.4 copy.21
  45.6 0.5 fusion.1
  46.1 0.0 slice-start
  46.1 1.2 %copy.22 = bf16[8,128,2,128]{1,3,2,0:T(8,128)(2,1)} copy(bf16[8,128,2,128]{3,0,2,1:T(8,128)(2,1)S(1)} %fusion.1) | data formatting | bytes 1048576 | tf_op jit(solution)/shard_map/convert_element_type | solution.py:38
  47.3 7.8 %all-to-all-start.1 = ((bf16[8,128,256]{1,2,0:T(8,128)(2,1)}), bf16[8,128,256]{1,2,0:T(8,128)(2,1)S(1)}, u32[]{:S(2)}, u32[]{:S(2)}) async-start(bf16[8,128,256]{1,2,0:T(8,128)(2,1)} %bitcast.26), calls=%async_computation.1 | async-start | bytes 1048576 | tf_op jit(solution)/shard_map/all_to_all | solution.py:162
  55.2 0.0 slice-done
  55.2 1.0 %copy.24 = bf16[1,1024,256]{1,2,0:T(8,128)(2,1)} copy(bf16[1,1024,256]{2,1,0:T(8,128)(2,1)S(1)} %slice-done) | data formatting | bytes 1048576
  56.2 0.0 copy-done
  56.2 0.0 copy-done.1
  56.2 1.0 %slice_bitcast_fusion = (bf16[1024,256]{1,0:T(8,128)(2,1)}, bf16[1024,256]{1,0:T(8,128)(2,1)}) fusion(bf16[2,1024,256]{2,1,0:T(8,128)(2,1)S(1)} %copy-done, bf16[2,1024,256]{2,1,0:T(8,128)(2,1)S(1)} %copy-done.1), kind=kLoop, calls=%fused_computation.10 | loop fusion | bytes 2097152 | tf_op jit(solution)/shard_map/squeeze | solution.py:167
  57.2 15.8 %collective-permute-done.refs_1_.refs_3_ = bf16[2,1024,256]{2,1,0:T(8,128)(2,1)} collective-permute-done((bf16[2,1024,256]{2,1,0:T(8,128)(2,1)}, bf16[2,1024,256]{2,1,0:T(8,128)(2,1)}, u32[]{:S(2)}, u32[]{:S(2)}) %collective-permute-start) | collective-permute-done | bytes 1048608 | tf_op jit(solution)/shard_map/ppermute | solution.py:19
  73.0 8.1 %shard_map.38 = bf16[2,1024,256]{2,1,0:T(8,128)(2,1)} custom-call(s32[1]{0:T(128)} %bitcast.flag_ref, bf16[1024,256]{1,0:T(8,128)(2,1)} %get-tuple-element.29.refs_0_, bf16[2,1024,256]{2,1,0:T(8,128)(2,1)} %collective-permute-done.refs_1_.refs_3_, bf16[256,1024]{1,0:T(8,128)(2,1)} %bitcast.28, bf16[2,1024,256]{2,1,0:T(8,128)(2,1)} %collective-permute-done.refs_1_.refs_3_, ...), custom_call_target="tpu_custom_call" | custom-call | flops 1342177280 | bytes 3145728 | tf_op jit(solution)/shard_map/pallas_call | solution.py:92
  81.2 0.0 all-to-all-done.1
  81.2 0.2 copy.23
  81.4 0.8 %bitcast_dynamic-update-slice_fusion = bf16[2,1024,256]{2,1,0:T(8,128)(2,1)} fusion(bf16[2,1024,256]{2,1,0:T(8,128)(2,1)} %shard_map.38, bf16[1,1024,256]{2,1,0:T(8,128)(2,1)S(1)} %bitcast.27), kind=kLoop, calls=%fused_computation.9 | loop fusion | bytes 1048576 | tf_op jit(solution)/shard_map/scatter | solution.py:168
  (4 shorter events, 0.0 us)
Async XLA Ops:
  2.8 38.7 %all-to-all-start = ((bf16[8,3,128,256]{3,2,1,0:T(8,128)(2,1)}), bf16[8,3,128,256]{3,2,1,0:T(8,128)(2,1)S(1)}, u32[]{:S(2)}, u32[]{:S(2)}) async-start(bf16[8,3,128,256]{3,2,1,0:T(8,128)(2,1)} %get-tuple-element.20), calls=%async_computation | async-start | bytes 3145728 | tf_op jit(solution)/shard_map/all_to_all | solution.py:158
  8.4 64.6 %collective-permute-start = (bf16[2,1024,256]{2,1,0:T(8,128)(2,1)}, bf16[2,1024,256]{2,1,0:T(8,128)(2,1)}, u32[]{:S(2)}, u32[]{:S(2)}) collective-permute-start(bf16[2,1024,256]{2,1,0:T(8,128)(2,1)} %get-tuple-element.21), channel_id=1, source_target_pairs={{0,2},{2,4},{4,6},{6,8},{8,10},{10,12},{12,14},{1,3},{3,5},{5,7},{... | collective-permute-start | bytes 3145736 | tf_op jit(solution)/shard_map/ppermute | solution.py:19
  46.1 9.1 %slice-start = ((bf16[2,1024,256]{2,1,0:T(8,128)(2,1)}), bf16[1,1024,256]{2,1,0:T(8,128)(2,1)S(1)}, s32[]{:S(2)}) async-start(bf16[2,1024,256]{2,1,0:T(8,128)(2,1)} %kp_ref.1), calls=%async_computation.2 | async-start | bytes 1048576 | tf_op jit(solution)/shard_map/slice | solution.py:167
  47.3 8.9 %copy-start = (bf16[2,1024,256]{2,1,0:T(8,128)(2,1)S(1)}, bf16[2,1024,256]{2,1,0:T(8,128)(2,1)}, u32[]{:S(2)}) copy-start(bf16[2,1024,256]{2,1,0:T(8,128)(2,1)} %vp_ref.1) | copy-start | bytes 3145732
  47.3 8.9 %copy-start.1 = (bf16[2,1024,256]{2,1,0:T(8,128)(2,1)S(1)}, bf16[2,1024,256]{2,1,0:T(8,128)(2,1)}, u32[]{:S(2)}) copy-start(bf16[2,1024,256]{2,1,0:T(8,128)(2,1)} %q_ref.1) | copy-start | bytes 3145732
  47.3 33.9 %all-to-all-start.1 = ((bf16[8,128,256]{1,2,0:T(8,128)(2,1)}), bf16[8,128,256]{1,2,0:T(8,128)(2,1)S(1)}, u32[]{:S(2)}, u32[]{:S(2)}) async-start(bf16[8,128,256]{1,2,0:T(8,128)(2,1)} %bitcast.26), calls=%async_computation.1 | async-start | bytes 1048576 | tf_op jit(solution)/shard_map/all_to_all | solution.py:162

commit v22 on v16

--- a/solution.py
+++ b/solution.py
@@ -120,7 +120,7 @@
     pair_ref[1] = vp_ref[...]
 
 
-def pack(query_vectors, key_vectors, value_vectors, blocks, steps=1):
+def pack(query_vectors, key_vectors, value_vectors, blocks, steps=4):
     _, tokens, width = query_vectors.shape
     size = tokens // blocks
     rows = tokens // steps

time: 82.6 us -> 83.4 us (level)
  no operation moved by 1% of the time
where the time goes in v22:
time: 83.4 us; the launch traced here: 83 us
  waiting for transfers between devices  45.9 us (55%)
  starting transfers between devices  16.5 us (20%)
  Pallas kernels  11.8 us (14%)
  local copies, waits for them, and re-layouts  6.78 us (8%)
  matrix products  1.17 us (1%)
  other arithmetic  0.84 us (1%)
    all_to_all x1, waiting for transfers between devices, local(): lax.all_to_all(stacked, 'seq', split_axis=0, concat_axis=0, tiled=True)  30 us
    ppermute x1, waiting for transfers between devices, shifted(): return lax.ppermute(block, axis, route)  15.8 us
    all_to_all x1, starting transfers between devices, local(): lax.all_to_all(result.reshape(blocks, width, feature_width), 'seq', split...  7.85 us
    pallas_call x1, Pallas kernels, attend_rows(): pl.pallas_call(row_kernel, out_shape=jax.ShapeDtypeStruct((2, tokens, wid...  7.74 us
    all_to_all x1, starting transfers between devices, local(): lax.all_to_all(stacked, 'seq', split_axis=0, concat_axis=0, tiled=True)  5.58 us
    pallas_call x1, Pallas kernels, pack(): pl.pallas_call(pack_kernel, out_shape=(jax.ShapeDtypeStruct((blocks, 3, s...  4.03 us
    ppermute x1, starting transfers between devices, shifted(): return lax.ppermute(block, axis, route)  3.08 us
  transfers between devices with their start and end apart: 3, of which 2 were waited for; matrix products, arithmetic and copies ran while one was open for 9% of the time, Pallas kernels for 9%

profile of v22, /device:TPU:17, one launch (start us, length us, event | category | flops | bytes accessed | tf_op | source)
XLA Modules:
  0.0 83.0 jit_solution(17394308404607180914)
XLA Ops:
  0.0 4.0 %shard_map.37 = (bf16[8,3,128,256]{3,2,1,0:T(8,128)(2,1)}, bf16[2,1024,256]{2,1,0:T(8,128)(2,1)}) custom-call(bf16[2,1024,256]{2,1,0:T(8,128)(2,1)} %q_ref.1, bf16[2,1024,256]{2,1,0:T(8,128)(2,1)} %kp_ref.1, bf16[2,1024,256]{2,1,0:T(8,128)(2,1)} %vp_ref.1, bf16[2,1024,256]{2,1,0:T(8,128)(2,1)} %kp_ref.1, bf16[2,1024,256]{2,1,0:T(8,128)(2,1)} %vp_ref.1), custom_call_target="tpu_custom_call" | custom-call | tf_op jit(solution)/shard_map/pallas_call | solution.py:129
  4.0 5.6 %all-to-all-start = ((bf16[8,3,128,256]{3,2,1,0:T(8,128)(2,1)}), bf16[8,3,128,256]{3,2,1,0:T(8,128)(2,1)S(1)}, u32[]{:S(2)}, u32[]{:S(2)}) async-start(bf16[8,3,128,256]{3,2,1,0:T(8,128)(2,1)} %get-tuple-element.20), calls=%async_computation | async-start | bytes 3145728 | tf_op jit(solution)/shard_map/all_to_all | solution.py:165
  9.6 3.1 %collective-permute-start = (bf16[2,1024,256]{2,1,0:T(8,128)(2,1)}, bf16[2,1024,256]{2,1,0:T(8,128)(2,1)}, u32[]{:S(2)}, u32[]{:S(2)}) collective-permute-start(bf16[2,1024,256]{2,1,0:T(8,128)(2,1)} %get-tuple-element.21), channel_id=1, source_target_pairs={{0,2},{2,4},{4,6},{6,8},{8,10},{10,12},{12,14},{1,3},{3,5},{5,7},{... | collective-permute-start | bytes 3145736 | tf_op jit(solution)/shard_map/ppermute | solution.py:19
  12.7 30.0 %all-to-all-done = bf16[8,3,128,256]{3,2,1,0:T(8,128)(2,1)S(1)} async-done(((bf16[8,3,128,256]{3,2,1,0:T(8,128)(2,1)}), bf16[8,3,128,256]{3,2,1,0:T(8,128)(2,1)S(1)}, u32[]{:S(2)}, u32[]{:S(2)}) %all-to-all-start) | async-done | bytes 1572896 | tf_op jit(solution)/shard_map/all_to_all | solution.py:165
  42.8 0.4 reshape.60
  43.2 1.2 %fusion.11 = (bf16[8,1,128,2,128]{4,3,2,1,0:T(2,128)(2,1)S(1)}, bf16[8,1,128,2,128]{4,3,2,1,0:T(2,128)(2,1)S(1)}, bf16[8,1,128,2,128]{4,3,2,1,0:T(2,128)(2,1)S(1)}) fusion(bf16[8,3,128,2,128]{4,3,2,1,0:T(2,128)(2,1)S(1)} %reshape.60), kind=kLoop, calls=%fused_computation.21 | loop fusion | bytes 3145728 | tf_op jit(solution)/shard_map/slice | solution.py:168
  44.4 0.7 fusion.4
  45.0 0.4 copy.20
  45.5 0.8 fusion.12
  46.3 0.4 copy.21
  46.8 0.5 fusion.1
  47.2 0.0 slice-start
  47.3 1.2 %copy.22 = bf16[8,128,2,128]{1,3,2,0:T(8,128)(2,1)} copy(bf16[8,128,2,128]{3,0,2,1:T(8,128)(2,1)S(1)} %fusion.1) | data formatting | bytes 1048576 | tf_op jit(solution)/shard_map/convert_element_type | solution.py:38
  48.5 7.9 %all-to-all-start.1 = ((bf16[8,128,256]{1,2,0:T(8,128)(2,1)}), bf16[8,128,256]{1,2,0:T(8,128)(2,1)S(1)}, u32[]{:S(2)}, u32[]{:S(2)}) async-start(bf16[8,128,256]{1,2,0:T(8,128)(2,1)} %bitcast.26), calls=%async_computation.1 | async-start | bytes 1048576 | tf_op jit(solution)/shard_map/all_to_all | solution.py:169
  56.3 0.0 slice-done
  56.3 1.0 %copy.24 = bf16[1,1024,256]{1,2,0:T(8,128)(2,1)} copy(bf16[1,1024,256]{2,1,0:T(8,128)(2,1)S(1)} %slice-done) | data formatting | bytes 1048576
  57.4 0.0 copy-done
  57.4 0.0 copy-done.1
  57.4 1.0 %slice_bitcast_fusion = (bf16[1024,256]{1,0:T(8,128)(2,1)}, bf16[1024,256]{1,0:T(8,128)(2,1)}) fusion(bf16[2,1024,256]{2,1,0:T(8,128)(2,1)S(1)} %copy-done, bf16[2,1024,256]{2,1,0:T(8,128)(2,1)S(1)} %copy-done.1), kind=kLoop, calls=%fused_computation.10 | loop fusion | bytes 2097152 | tf_op jit(solution)/shard_map/squeeze | solution.py:174
  58.4 15.8 %collective-permute-done.refs_1_.refs_3_ = bf16[2,1024,256]{2,1,0:T(8,128)(2,1)} collective-permute-done((bf16[2,1024,256]{2,1,0:T(8,128)(2,1)}, bf16[2,1024,256]{2,1,0:T(8,128)(2,1)}, u32[]{:S(2)}, u32[]{:S(2)}) %collective-permute-start) | collective-permute-done | bytes 1048608 | tf_op jit(solution)/shard_map/ppermute | solution.py:19
  74.2 7.7 %shard_map.38 = bf16[2,1024,256]{2,1,0:T(8,128)(2,1)} custom-call(s32[1]{0:T(128)} %bitcast.flag_ref, bf16[1024,256]{1,0:T(8,128)(2,1)} %get-tuple-element.29.refs_0_, bf16[2,1024,256]{2,1,0:T(8,128)(2,1)} %collective-permute-done.refs_1_.refs_3_, bf16[256,1024]{1,0:T(8,128)(2,1)} %bitcast.28, bf16[2,1024,256]{2,1,0:T(8,128)(2,1)} %collective-permute-done.refs_1_.refs_3_, ...), custom_call_target="tpu_custom_call" | custom-call | flops 1610612736 | bytes 3145728 | tf_op jit(solution)/shard_map/pallas_call | solution.py:99
  82.0 0.0 all-to-all-done.1
  82.0 0.2 copy.23
  82.2 0.8 %bitcast_dynamic-update-slice_fusion = bf16[2,1024,256]{2,1,0:T(8,128)(2,1)} fusion(bf16[2,1024,256]{2,1,0:T(8,128)(2,1)} %shard_map.38, bf16[1,1024,256]{2,1,0:T(8,128)(2,1)S(1)} %bitcast.27), kind=kLoop, calls=%fused_computation.9 | loop fusion | bytes 1048576 | tf_op jit(solution)/shard_map/scatter | solution.py:175
  (4 shorter events, 0.0 us)
Async XLA Ops:
  4.0 38.7 %all-to-all-start = ((bf16[8,3,128,256]{3,2,1,0:T(8,128)(2,1)}), bf16[8,3,128,256]{3,2,1,0:T(8,128)(2,1)S(1)}, u32[]{:S(2)}, u32[]{:S(2)}) async-start(bf16[8,3,128,256]{3,2,1,0:T(8,128)(2,1)} %get-tuple-element.20), calls=%async_computation | async-start | bytes 3145728 | tf_op jit(solution)/shard_map/all_to_all | solution.py:165
  9.6 64.6 %collective-permute-start = (bf16[2,1024,256]{2,1,0:T(8,128)(2,1)}, bf16[2,1024,256]{2,1,0:T(8,128)(2,1)}, u32[]{:S(2)}, u32[]{:S(2)}) collective-permute-start(bf16[2,1024,256]{2,1,0:T(8,128)(2,1)} %get-tuple-element.21), channel_id=1, source_target_pairs={{0,2},{2,4},{4,6},{6,8},{8,10},{10,12},{12,14},{1,3},{3,5},{5,7},{... | collective-permute-start | bytes 3145736 | tf_op jit(solution)/shard_map/ppermute | solution.py:19
  47.2 9.1 %slice-start = ((bf16[2,1024,256]{2,1,0:T(8,128)(2,1)}), bf16[1,1024,256]{2,1,0:T(8,128)(2,1)S(1)}, s32[]{:S(2)}) async-start(bf16[2,1024,256]{2,1,0:T(8,128)(2,1)} %kp_ref.1), calls=%async_computation.2 | async-start | bytes 1048576 | tf_op jit(solution)/shard_map/slice | solution.py:174
  48.5 8.9 %copy-start = (bf16[2,1024,256]{2,1,0:T(8,128)(2,1)S(1)}, bf16[2,1024,256]{2,1,0:T(8,128)(2,1)}, u32[]{:S(2)}) copy-start(bf16[2,1024,256]{2,1,0:T(8,128)(2,1)} %vp_ref.1) | copy-start | bytes 3145732
  48.5 8.9 %copy-start.1 = (bf16[2,1024,256]{2,1,0:T(8,128)(2,1)S(1)}, bf16[2,1024,256]{2,1,0:T(8,128)(2,1)}, u32[]{:S(2)}) copy-start(bf16[2,1024,256]{2,1,0:T(8,128)(2,1)} %q_ref.1) | copy-start | bytes 3145732
  48.5 33.5 %all-to-all-start.1 = ((bf16[8,128,256]{1,2,0:T(8,128)(2,1)}), bf16[8,128,256]{1,2,0:T(8,128)(2,1)S(1)}, u32[]{:S(2)}, u32[]{:S(2)}) async-start(bf16[8,128,256]{1,2,0:T(8,128)(2,1)} %bitcast.26), calls=%async_computation.1 | async-start | bytes 1048576 | tf_op jit(solution)/shard_map/all_to_all | solution.py:169

commit v23 on v14

--- a/solution.py
+++ b/solution.py
@@ -166,9 +166,7 @@
     _, prev_pair = lax.optimization_barrier((moved, prev_pair))
     grid = moved.reshape(blocks, 3, width, heads_here, DH)
     result = attend_columns(grid[:, 0], grid[:, 1], grid[:, 2])
-    context = lax.all_to_all(
-        result.reshape(blocks, width, feature_width), "seq", split_axis=0, concat_axis=0, tiled=True
-    )
+    context = lax.all_to_all(result, "seq", split_axis=0, concat_axis=0, tiled=True)
     column_out = context.reshape(local_tokens, feature_width)
     has_prev = (seq_index > 0).astype(jnp.int32).reshape(1)
     both = attend_rows(has_prev, query_vectors[0], prev_pair, key_vectors[0].T, value_vectors[0])

time: 82.2 us -> 82.3 us (level)
  no operation moved by 1% of the time
where the time goes in v23:
time: 82.3 us; the launch traced here: 82 us
  waiting for transfers between devices  45.9 us (56%)
  starting transfers between devices  16.5 us (20%)
  Pallas kernels  10.6 us (13%)
  local copies, waits for them, and re-layouts  6.87 us (8%)
  matrix products  1.18 us (1%)
  other arithmetic  0.84 us (1%)
    all_to_all x1, waiting for transfers between devices, local(): lax.all_to_all(stacked, 'seq', split_axis=0, concat_axis=0, tiled=True)  30 us
    ppermute x1, waiting for transfers between devices, shifted(): return lax.ppermute(block, axis, route)  15.8 us
    all_to_all x1, starting transfers between devices, local(): lax.all_to_all(result, 'seq', split_axis=0, concat_axis=0, tiled=True)  7.85 us
    pallas_call x1, Pallas kernels, attend_rows(): pl.pallas_call(row_kernel, out_shape=jax.ShapeDtypeStruct((2, tokens, wid...  7.74 us
    all_to_all x1, starting transfers between devices, local(): lax.all_to_all(stacked, 'seq', split_axis=0, concat_axis=0, tiled=True)  5.58 us
    ppermute x1, starting transfers between devices, shifted(): return lax.ppermute(block, axis, route)  3.08 us
    pallas_call x1, Pallas kernels, pack(): pl.pallas_call(pack_kernel, out_shape=(jax.ShapeDtypeStruct((blocks, 3, s...  2.85 us
  transfers between devices with their start and end apart: 3, of which 2 were waited for; matrix products, arithmetic and copies ran while one was open for 9% of the time, Pallas kernels for 9%

profile of v23, /device:TPU:17, one launch (start us, length us, event | category | flops | bytes accessed | tf_op | source)
XLA Modules:
  0.0 82.0 jit_solution(1060449377457592721)
XLA Ops:
  0.0 2.8 %shard_map.37 = (bf16[8,3,128,256]{3,2,1,0:T(8,128)(2,1)}, bf16[2,1024,256]{2,1,0:T(8,128)(2,1)}) custom-call(bf16[2,1024,256]{2,1,0:T(8,128)(2,1)} %q_ref.1, bf16[2,1024,256]{2,1,0:T(8,128)(2,1)} %kp_ref.1, bf16[2,1024,256]{2,1,0:T(8,128)(2,1)} %vp_ref.1, bf16[2,1024,256]{2,1,0:T(8,128)(2,1)} %kp_ref.1, bf16[2,1024,256]{2,1,0:T(8,128)(2,1)} %vp_ref.1), custom_call_target="tpu_custom_call" | custom-call | tf_op jit(solution)/shard_map/pallas_call | solution.py:129
  2.8 5.6 %all-to-all-start = ((bf16[8,3,128,256]{3,2,1,0:T(8,128)(2,1)}), bf16[8,3,128,256]{3,2,1,0:T(8,128)(2,1)S(1)}, u32[]{:S(2)}, u32[]{:S(2)}) async-start(bf16[8,3,128,256]{3,2,1,0:T(8,128)(2,1)} %get-tuple-element.20), calls=%async_computation | async-start | bytes 3145728 | tf_op jit(solution)/shard_map/all_to_all | solution.py:165
  8.4 3.1 %collective-permute-start = (bf16[2,1024,256]{2,1,0:T(8,128)(2,1)}, bf16[2,1024,256]{2,1,0:T(8,128)(2,1)}, u32[]{:S(2)}, u32[]{:S(2)}) collective-permute-start(bf16[2,1024,256]{2,1,0:T(8,128)(2,1)} %get-tuple-element.21), channel_id=1, source_target_pairs={{0,2},{2,4},{4,6},{6,8},{8,10},{10,12},{12,14},{1,3},{3,5},{5,7},{... | collective-permute-start | bytes 3145736 | tf_op jit(solution)/shard_map/ppermute | solution.py:19
  11.5 30.0 %all-to-all-done = bf16[8,3,128,256]{3,2,1,0:T(8,128)(2,1)S(1)} async-done(((bf16[8,3,128,256]{3,2,1,0:T(8,128)(2,1)}), bf16[8,3,128,256]{3,2,1,0:T(8,128)(2,1)S(1)}, u32[]{:S(2)}, u32[]{:S(2)}) %all-to-all-start) | async-done | bytes 1572896 | tf_op jit(solution)/shard_map/all_to_all | solution.py:165
  41.6 0.4 reshape.57
  42.0 1.2 %fusion.11 = (bf16[8,1,128,2,128]{4,3,2,1,0:T(2,128)(2,1)S(1)}, bf16[8,1,128,2,128]{4,3,2,1,0:T(2,128)(2,1)S(1)}, bf16[8,1,128,2,128]{4,3,2,1,0:T(2,128)(2,1)S(1)}) fusion(bf16[8,3,128,2,128]{4,3,2,1,0:T(2,128)(2,1)S(1)} %reshape.57), kind=kLoop, calls=%fused_computation.21 | loop fusion | bytes 3145728 | tf_op jit(solution)/shard_map/slice | solution.py:168
  43.2 0.7 fusion.4
  43.9 0.4 copy.20
  44.3 0.8 fusion.12
  45.1 0.4 copy.21
  45.6 0.5 fusion.1
  46.1 0.0 slice-start
  46.1 1.2 %copy.22 = bf16[8,128,2,128]{3,2,1,0:T(2,128)(2,1)} copy(bf16[8,128,2,128]{3,0,2,1:T(8,128)(2,1)S(1)} %fusion.1) | data formatting | bytes 1048576 | tf_op jit(solution)/shard_map/convert_element_type | solution.py:38
  47.3 7.8 %all-to-all-start.1 = ((bf16[8,128,2,128]{3,2,1,0:T(2,128)(2,1)}), bf16[8,128,2,128]{3,2,1,0:T(2,128)(2,1)S(1)}, u32[]{:S(2)}, u32[]{:S(2)}) async-start(bf16[8,128,2,128]{3,2,1,0:T(2,128)(2,1)} %copy.22), calls=%async_computation.1 | async-start | bytes 1048576 | tf_op jit(solution)/shard_map/all_to_all | solution.py:169
  55.1 0.0 slice-done
  55.1 1.0 %copy.23 = bf16[1,1024,256]{1,2,0:T(8,128)(2,1)} copy(bf16[1,1024,256]{2,1,0:T(8,128)(2,1)S(1)} %slice-done) | data formatting | bytes 1048576
  56.1 0.0 copy-done
  56.1 0.0 copy-done.1
  56.1 1.0 %slice_bitcast_fusion = (bf16[1024,256]{1,0:T(8,128)(2,1)}, bf16[1024,256]{1,0:T(8,128)(2,1)}) fusion(bf16[2,1024,256]{2,1,0:T(8,128)(2,1)S(1)} %copy-done, bf16[2,1024,256]{2,1,0:T(8,128)(2,1)S(1)} %copy-done.1), kind=kLoop, calls=%fused_computation.9 | loop fusion | bytes 2097152 | tf_op jit(solution)/shard_map/squeeze | solution.py:172
  57.2 15.8 %collective-permute-done.refs_1_.refs_3_ = bf16[2,1024,256]{2,1,0:T(8,128)(2,1)} collective-permute-done((bf16[2,1024,256]{2,1,0:T(8,128)(2,1)}, bf16[2,1024,256]{2,1,0:T(8,128)(2,1)}, u32[]{:S(2)}, u32[]{:S(2)}) %collective-permute-start) | collective-permute-done | bytes 1048608 | tf_op jit(solution)/shard_map/ppermute | solution.py:19
  73.0 7.7 %shard_map.38 = bf16[2,1024,256]{2,1,0:T(8,128)(2,1)} custom-call(s32[1]{0:T(128)} %bitcast.flag_ref, bf16[1024,256]{1,0:T(8,128)(2,1)} %get-tuple-element.29.refs_0_, bf16[2,1024,256]{2,1,0:T(8,128)(2,1)} %collective-permute-done.refs_1_.refs_3_, bf16[256,1024]{1,0:T(8,128)(2,1)} %bitcast.22, bf16[2,1024,256]{2,1,0:T(8,128)(2,1)} %collective-permute-done.refs_1_.refs_3_, ...), custom_call_target="tpu_custom_call" | custom-call | flops 1610612736 | bytes 3145728 | tf_op jit(solution)/shard_map/pallas_call | solution.py:99
  80.8 0.0 all-to-all-done.1
  80.8 0.3 reshape.58
  81.1 0.8 %constant_dynamic-update-slice_fusion = bf16[2,1024,256]{2,1,0:T(8,128)(2,1)} fusion(bf16[2,1024,256]{2,1,0:T(8,128)(2,1)} %shard_map.38, bf16[1,1024,256]{2,1,0:T(8,128)(2,1)S(1)} %reshape.58), kind=kLoop, calls=%fused_computation.18 | loop fusion | bytes 1048576 | tf_op jit(solution)/shard_map/scatter | solution.py:173
  (4 shorter events, 0.0 us)
Async XLA Ops:
  2.8 38.7 %all-to-all-start = ((bf16[8,3,128,256]{3,2,1,0:T(8,128)(2,1)}), bf16[8,3,128,256]{3,2,1,0:T(8,128)(2,1)S(1)}, u32[]{:S(2)}, u32[]{:S(2)}) async-start(bf16[8,3,128,256]{3,2,1,0:T(8,128)(2,1)} %get-tuple-element.20), calls=%async_computation | async-start | bytes 3145728 | tf_op jit(solution)/shard_map/all_to_all | solution.py:165
  8.4 64.6 %collective-permute-start = (bf16[2,1024,256]{2,1,0:T(8,128)(2,1)}, bf16[2,1024,256]{2,1,0:T(8,128)(2,1)}, u32[]{:S(2)}, u32[]{:S(2)}) collective-permute-start(bf16[2,1024,256]{2,1,0:T(8,128)(2,1)} %get-tuple-element.21), channel_id=1, source_target_pairs={{0,2},{2,4},{4,6},{6,8},{8,10},{10,12},{12,14},{1,3},{3,5},{5,7},{... | collective-permute-start | bytes 3145736 | tf_op jit(solution)/shard_map/ppermute | solution.py:19
  46.1 9.1 %slice-start = ((bf16[2,1024,256]{2,1,0:T(8,128)(2,1)}), bf16[1,1024,256]{2,1,0:T(8,128)(2,1)S(1)}, s32[]{:S(2)}) async-start(bf16[2,1024,256]{2,1,0:T(8,128)(2,1)} %kp_ref.1), calls=%async_computation.2 | async-start | bytes 1048576 | tf_op jit(solution)/shard_map/slice | solution.py:172
  47.3 8.9 %copy-start = (bf16[2,1024,256]{2,1,0:T(8,128)(2,1)S(1)}, bf16[2,1024,256]{2,1,0:T(8,128)(2,1)}, u32[]{:S(2)}) copy-start(bf16[2,1024,256]{2,1,0:T(8,128)(2,1)} %vp_ref.1) | copy-start | bytes 3145732
  47.3 8.9 %copy-start.1 = (bf16[2,1024,256]{2,1,0:T(8,128)(2,1)S(1)}, bf16[2,1024,256]{2,1,0:T(8,128)(2,1)}, u32[]{:S(2)}) copy-start(bf16[2,1024,256]{2,1,0:T(8,128)(2,1)} %q_ref.1) | copy-start | bytes 3145732
  47.3 33.5 %all-to-all-start.1 = ((bf16[8,128,2,128]{3,2,1,0:T(2,128)(2,1)}), bf16[8,128,2,128]{3,2,1,0:T(2,128)(2,1)S(1)}, u32[]{:S(2)}, u32[]{:S(2)}) async-start(bf16[8,128,2,128]{3,2,1,0:T(2,128)(2,1)} %copy.22), calls=%async_computation.1 | async-start | bytes 1048576 | tf_op jit(solution)/shard_map/all_to_all | solution.py:169
